TPU v7x, 32 devices: a whole 2x2x4 slice. The times are simulated.
32 devices in a mesh: dp: 4 (over z), seq: 8 (over y, x, core).
Axes of the slice: x: 2, y: 2, z: 4, core: 2. Of those that a mesh axis runs over, the one named last changes fastest.
Arguments:
- tokens: bfloat16 [4, 1024, 2048], P('dp', 'seq'), may hold values from -6 to 6
- query_weight: bfloat16 [2048, 256], replicated, may hold values from -0.125 to 0.125
- key_weight: bfloat16 [2048, 256], replicated, may hold values from -0.125 to 0.125
- value_weight: bfloat16 [2048, 2048], replicated, may hold values from -0.125 to 0.125
- cotangent: bfloat16 [4, 1024, 2048], P('dp', 'seq'), may hold values from -6 to 6
- doc_ids: int32 [4, 1024], P('dp', 'seq'), may hold values from 0 to 3, never falling along the last dimension, each value on 1 to 512 neighbouring positions
Outputs:
- mixed: bfloat16 [4, 1024, 2048], P('dp', 'seq')
- grad_tokens: bfloat16 [4, 1024, 2048], P('dp', 'seq')
- grad_weights: float32 [2048, 2560], P(('dp', 'seq'))
Inputs may be any that keep to these rules, and one draw needn't show every extreme that they name: `doc_ids`: document numbers never fall along a pack and begin at 0; each document has at most 512 positions and one has exactly that many.
All inputs are finite; a program needn't handle non-finite values.
Results may differ from a plain program's by a relative error of at most 0.0049.
Values sent between devices are 32-bit elements; how exact they have to be, the bound alone decides.
No kernel may reach another device: no remote copies, remote signals or barrier semaphores. Data moves between devices by JAX's collectives and lax.ppermute only.
A program may use at most 256 MiB of HBM per device.

v0:
```python
import jax
import jax.numpy as jnp
import numpy as np
from jax import lax
from jax.sharding import PartitionSpec as P

HEADS = 16
FEAT = 16
HEAD_DIM = 128


highest = lax.Precision.HIGHEST


def pack_heads(state, norm, extra):
    heads, feats, lanes = state.shape
    rows = -(-(feats + 3) // 8) * 8
    norm_rows = jnp.pad(norm, ((0, 0), (0, 2 * lanes - feats))).reshape(heads, 2, lanes)
    extra_rows = jnp.broadcast_to(extra, (heads, 1, lanes)).astype(state.dtype)
    filler = jnp.zeros((heads, rows - feats - 3, lanes), state.dtype)
    return jnp.concatenate([state, norm_rows, extra_rows, filler], axis=1)


def unpack_heads(packed, feats):
    heads, _, lanes = packed.shape
    state = packed[:, :feats, :]
    norm = packed[:, feats : feats + 2, :].reshape(heads, 2 * lanes)[:, :feats]
    return state, norm


def shifted(value, steps):
    count = lax.axis_size("seq")
    if steps > 0:
        pairs = [(source, source + steps) for source in range(count - steps)]
    else:
        pairs = [(source, source + steps) for source in range(-steps, count)]
    return lax.ppermute(value, "seq", pairs)


def segmented_scan(packed, flag_row, direction, reach):
    carry = shifted(packed, direction)
    covered = 1
    while covered < reach:
        earlier = shifted(carry, direction * covered)
        carry = jnp.where(carry[0, flag_row, 0] > 0, carry, carry + earlier)
        covered *= 2
    return carry


def taylor_table(feat_width):
    row_index, col_index = np.triu_indices(feat_width)
    taylor_map = np.zeros((feat_width * feat_width, len(row_index)), np.float32)
    taylor_map[row_index * feat_width + col_index, np.arange(len(row_index))] = np.where(
        row_index == col_index, 1.0 / np.sqrt(2.0), 1.0
    )
    return jnp.asarray(taylor_map)


def expand_features(vectors, taylor_map):
    lead_shape = vectors.shape[:-1]
    feat_width = vectors.shape[-1]
    outer_prod = (vectors[..., :, None] * vectors[..., None, :]).reshape(
        lead_shape + (feat_width * feat_width,)
    )
    square = jnp.einsum(
        "thp,pc->thc", outer_prod, taylor_map.astype(vectors.dtype), precision=highest
    )
    return jnp.concatenate([jnp.ones(lead_shape + (1,), vectors.dtype), vectors, square], axis=-1)


def block_forward(query_raw, key_raw, value_all, doc_local, prev_id, state_in, norm_in, taylor_map):
    length = query_raw.shape[0]
    queries = (0.5 * query_raw).reshape(length, HEADS, FEAT)
    key_feats = (0.5 * key_raw).reshape(length, HEADS, FEAT)
    values = value_all.reshape(length, HEADS, HEAD_DIM)
    scores = jnp.einsum("thf,shf->hts", queries, key_feats, precision=highest)
    kernel = 1.0 + scores + 0.5 * scores * scores
    positions = jnp.arange(length)
    allowed = (positions[:, None] >= positions[None, :]) & (
        doc_local[:, None] == doc_local[None, :]
    )
    kernel = jnp.where(allowed[None], kernel, 0.0)
    numerator = jnp.einsum("hts,shd->thd", kernel, values, precision=highest)
    denominator = jnp.sum(kernel, axis=2).T
    carried = (doc_local == prev_id).astype(kernel.dtype)[:, None]
    phi_query = expand_features(queries, taylor_map)
    numerator = numerator + carried[:, :, None] * jnp.einsum(
        "thf,hfd->thd", phi_query, state_in, precision=highest
    )
    denominator = denominator + carried * jnp.einsum(
        "thf,hf->th", phi_query, norm_in, precision=highest
    )
    return (numerator / denominator[:, :, None]).reshape(length, HEADS * HEAD_DIM)


def block_summary(key_raw, value_all, doc_local, taylor_map):
    length = key_raw.shape[0]
    key_feats = (0.5 * key_raw).reshape(length, HEADS, FEAT)
    values = value_all.reshape(length, HEADS, HEAD_DIM)
    phi_key = expand_features(key_feats, taylor_map)
    tail_mask = (doc_local == doc_local[-1]).astype(phi_key.dtype)[:, None, None]
    weighted = phi_key * tail_mask
    state_sum = jnp.einsum("thf,thd->hfd", weighted, values, precision=highest)
    norm_sum = jnp.sum(weighted, axis=0)
    return (state_sum, norm_sum)


def on_device(tokens, query_weight, key_weight, value_weight, cotangent, doc_ids):
    inputs = tokens[0]
    doc_local = doc_ids[0]
    cotan_local = cotangent[0]
    taylor_map = taylor_table(FEAT)
    width_qk = HEADS * FEAT
    weights = jnp.concatenate([query_weight, key_weight, value_weight], axis=1)
    projected = jnp.dot(inputs, weights, preferred_element_type=jnp.float32)

    def summary(proj_in):
        return block_summary(
            proj_in[:, width_qk : 2 * width_qk], proj_in[:, 2 * width_qk :], doc_local, taylor_map
        )

    (state_loc, norm_loc), summary_pull = jax.vjp(summary, projected)
    feats = state_loc.shape[1]
    count, length = (lax.axis_size("seq"), doc_local.shape[0])
    longest = count * length // 2
    reach = min(count - 1, -(-(longest - 1) // length))
    prev_id = shifted(doc_local[-1:] + 1, 1)[0] - 1
    boundary = (doc_local[-1] != prev_id).astype(jnp.float32)
    forward_sum = segmented_scan(pack_heads(state_loc, norm_loc, boundary), feats + 2, 1, reach)
    state_in, norm_in = unpack_heads(forward_sum, feats)
    tokens_pack = lax.all_gather(inputs.astype(jnp.float32), "seq", axis=0, tiled=True)

    def attend(proj_in, state_sum, norm_sum):
        return block_forward(
            proj_in[:, :width_qk],
            proj_in[:, width_qk : 2 * width_qk],
            proj_in[:, 2 * width_qk :],
            doc_local,
            prev_id,
            state_sum,
            norm_sum,
            taylor_map,
        )

    output, attend_pull = jax.vjp(attend, projected, state_in, norm_in)
    grad_direct, grad_state_in, grad_norm_in = attend_pull(cotan_local.astype(jnp.float32))
    backward_sum = segmented_scan(
        pack_heads(grad_state_in, grad_norm_in, boundary), feats + 2, -1, reach
    )
    grad_state_loc, grad_norm_loc = unpack_heads(backward_sum, feats)
    (grad_carried,) = summary_pull((grad_state_loc, grad_norm_loc))
    grad_projected = (grad_direct + grad_carried).astype(jnp.bfloat16)
    grad_input = jnp.dot(grad_projected, weights.T, preferred_element_type=jnp.float32).astype(
        jnp.bfloat16
    )
    grad_cols = lax.all_to_all(
        grad_projected.astype(jnp.float32), "seq", split_axis=1, concat_axis=0, tiled=True
    )
    pack_part = lax.dot_general(
        tokens_pack,
        grad_cols,
        (((0,), (0,)), ((), ())),
        precision=highest,
        preferred_element_type=jnp.float32,
    )
    row_part = lax.psum_scatter(pack_part, "dp", scatter_dimension=0, tiled=True)
    grad_proj = lax.all_to_all(row_part, "seq", split_axis=0, concat_axis=1, tiled=True)
    return (output.astype(jnp.bfloat16)[None], grad_input[None], grad_proj)


def solution(mesh):
    return jax.shard_map(
        on_device,
        mesh=mesh,
        in_specs=(P("dp", "seq", None), P(), P(), P(), P("dp", "seq", None), P("dp", "seq")),
        out_specs=(P("dp", "seq", None), P("dp", "seq", None), P(("dp", "seq"), None)),
        check_vma=False,
    )
```

profile of v0, /device:TPU:0, one launch (start us, length us, event | category | flops | bytes accessed | tf_op | source)
XLA Modules:
  0.0 351.0 jit_solution(3954575501892244738)
XLA Ops:
  9.1 3.3 collective-permute-start
  12.4 2.1 bitcast_convert_fusion
  17.3 8.8 %constant_dynamic-update-slice_fusion = bf16[2048,2560]{1,0:T(8,128)(2,1)} fusion(bf16[2048,2560]{1,0:T(8,128)(2,1)} %constant_dynamic-update-slice_fusion.1, bf16[2048,2048]{1,0:T(8,128)(2,1)} %param.10), kind=kLoop, calls=%fused_computation.80 | loop fusion | bytes 16777216 | tf_op jit(solution)/shard_map/concatenate | solution.py:114
  26.0 5.8 %convolution_bitcast_fusion = f32[128,2560]{0,1:T(8,128)S(1)} fusion(bf16[2048,2560]{1,0:T(8,128)(2,1)} %constant_dynamic-update-slice_fusion, bf16[1,128,2048]{2,1,0:T(8,128)(2,1)S(1)} %copy-done.10), kind=kOutput, calls=%fused_computation | convolution fusion | flops 1342177280 | bytes 12320768 | tf_op jit(solution)/shard_map/dot_general | solution.py:115
  36.2 3.5 fusion.53
  40.5 1.6 maximum_maximum_fusion
  42.1 5.0 %collective-permute-start.1 = (f32[16,160,128]{2,1,0:T(8,128)S(1)}, f32[16,160,128]{2,1,0:T(8,128)}, u32[]{:S(2)}, u32[]{:S(2)}) collective-permute-start(f32[16,160,128]{2,1,0:T(8,128)S(1)} %maximum_maximum_fusion), channel_id=1, source_target_pairs={{0,1},{1,2},{2,3},{3,4},{4,5},{5,6},{6,7},{8,9},{9,10},{10,11},{11... | collective-permute-start | bytes 3932168 | tf_op jit(solution)/shard_map/ppermute | solution.py:37
  47.1 2.9 collective-permute-done.1
  50.0 34.6 %collective-permute-start.2 = (f32[16,160,128]{2,1,0:T(8,128)}, f32[16,160,128]{2,1,0:T(8,128)}, u32[]{:S(2)}, u32[]{:S(2)}) collective-permute-start(f32[16,160,128]{2,1,0:T(8,128)} %collective-permute-done.1), channel_id=1, source_target_pairs={{0,1},{1,2},{2,3},{3,4},{4,5},{5,6},{6,7},{8,9},{9,10},{10,11},{11... | collective-permute-start | bytes 3932168 | tf_op jit(solution)/shard_map/ppermute | solution.py:37
  87.6 1.9 add_select_fusion.3
  89.5 17.9 %collective-permute-start.3 = (f32[16,160,128]{2,1,0:T(8,128)S(1)}, f32[16,160,128]{2,1,0:T(8,128)S(1)}, u32[]{:S(2)}, u32[]{:S(2)}) collective-permute-start(f32[16,160,128]{2,1,0:T(8,128)S(1)} %add_select_fusion.3), channel_id=1, source_target_pairs={{0,2},{1,3},{2,4},{3,5},{4,6},{5,7},{8,10},{9,11},{10,12},{11,13},... | collective-permute-start | bytes 3932168 | tf_op jit(solution)/shard_map/ppermute | solution.py:37
  107.5 1.8 fusion.35
  113.4 22.0 %collective-permute-done.3 = f32[16,160,128]{2,1,0:T(8,128)S(1)} collective-permute-done((f32[16,160,128]{2,1,0:T(8,128)S(1)}, f32[16,160,128]{2,1,0:T(8,128)S(1)}, u32[]{:S(2)}, u32[]{:S(2)}) %collective-permute-start.3) | collective-permute-done | bytes 1310752 | tf_op jit(solution)/shard_map/ppermute | solution.py:37
  137.3 3.6 %multiply_reduce_fusion.4 = (f32[128,16]{0,1:T(8,128)S(1)}, bf16[128,16,128]{0,2,1:T(8,128)(2,1)S(1)}) fusion(f32[128,16,128]{0,2,1:T(8,128)S(1)} %bitcast.152, f32[128,16]{0,1:T(8,128)S(1)} %get-tuple-element.16, f32[128,16]{0,1:T(8,128)S(1)} %get-tuple-element.17, f32[16,128,128]{2,1,0:T(8,128)S(1)} %fusion.36, f32[128,16,136]{0,2,1:T(8,128)S(1)} %fusion.57, ...), kind=kOutput, calls=%fused_computation.51 | convolution fusion | flops 483756032 | bytes 5203044 | tf_op jit(solution)/shard_map/jvp(thf,hfd->thd)/dot_general | solution.py:87
  141.0 2.3 fusion.54
  143.3 16.0 %fusion.21 = f32[16,153,128]{2,1,0:T(8,128)S(1)} fusion(f32[128]{0:T(128)S(1)} %get-tuple-element.24, f32[128,16,136]{0,2,1:T(8,128)} %copy-done.3, f32[128,16,16]{0,2,1:T(8,128)S(1)} %bitcast.145, f32[153]{0:T(256)S(1)} %pad.40.clone, f32[128,16,128]{0,2,1:T(8,128)} %bitcast.151, f32[128,16]{0,1:T(8,128)S(1)} %get-tuple-element.17), kind=kOutput, calls=%fused_computation.45 | convolution fusion | flops 482447360 | bytes 3556452 | tf_op jit(solution)/shard_map/transpose(jvp(thf,hfd->thd))/dot_general | solution.py:87
  161.1 3.6 %collective-permute-done.4 = f32[16,160,128]{2,1,0:T(8,128)S(1)} collective-permute-done((f32[16,160,128]{2,1,0:T(8,128)S(1)}, f32[16,160,128]{2,1,0:T(8,128)S(1)}, u32[]{:S(2)}, u32[]{:S(2)}) %collective-permute-start.4) | collective-permute-done | bytes 1310752 | tf_op jit(solution)/shard_map/ppermute | solution.py:37
  167.6 1.9 fusion.20
  170.7 13.3 %collective-permute-done.5 = f32[16,160,128]{2,1,0:T(8,128)S(1)} collective-permute-done((f32[16,160,128]{2,1,0:T(8,128)S(1)}, f32[16,160,128]{2,1,0:T(8,128)S(1)}, u32[]{:S(2)}, u32[]{:S(2)}) %collective-permute-start.5) | collective-permute-done | bytes 1310752 | tf_op jit(solution)/shard_map/ppermute | solution.py:37
  185.5 1.7 convolution_multiply_fusion.1
  187.2 1.9 fusion.16
  191.0 2.3 fusion.25
  194.6 32.9 %collective-permute-done.6 = f32[16,160,128]{2,1,0:T(8,128)S(1)} collective-permute-done((f32[16,160,128]{2,1,0:T(8,128)S(1)}, f32[16,160,128]{2,1,0:T(8,128)S(1)}, u32[]{:S(2)}, u32[]{:S(2)}) %collective-permute-start.6) | collective-permute-done | bytes 1310752 | tf_op jit(solution)/shard_map/ppermute | solution.py:37
  229.1 1.9 fusion.14
  231.9 3.8 %fusion.10 = f32[16,128,128]{2,1,0:T(8,128)S(1)} fusion(f32[16,160,128]{2,1,0:T(8,128)S(1)} %add_select_fusion, f32[128,16,136]{0,2,1:T(8,128)S(1)} %fusion.56, f32[128,16,16]{0,2,1:T(8,128)S(1)} %bitcast.136, f32[153]{0:T(256)S(1)} %pad.40.clone, f32[128]{0:T(128)S(1)} %get-tuple-element.25), kind=kOutput, calls=%fused_computation.32 | convolution fusion | flops 482236416 | bytes 3605604 | tf_op jit(solution)/shard_map/transpose(jvp(thf,thd->hfd))/dot_general | solution.py:103
  236.0 24.1 %all_to_all.42 = f32[128,8,320]{0,2,1:T(8,128)S(1)} all-to-all(f32[128,8,320]{0,2,1:T(8,128)S(1)} %convert.2), channel_id=1, replica_groups=mesh['dp'=4,'seq'=8] {'seq'}, dimensions={1} | all-to-all | bytes 2621440 | tf_op jit(solution)/shard_map/all_to_all | solution.py:156
  260.1 12.3 %convolution_bitcast_fusion.1 = f32[2048,320]{0,1:T(8,128)} fusion(f32[1024,2048]{1,0:T(8,128)} %all-gather.2.cloned.1.call-done, f32[128,8,320]{0,2,1:T(8,128)S(1)} %all_to_all.42), kind=kOutput, calls=%fused_computation.1 | convolution fusion | flops 8053063680 | bytes 12320768 | tf_op jit(solution)/shard_map/dot_general | solution.py:159
  273.4 50.3 %reduce-scatter.2.cloned.1.call-done = f32[512,320]{0,1:T(8,128)} async-done(((f32[2048,320]{0,1:T(8,128)}), f32[512,320]{0,1:T(8,128)}) %reduce-scatter.2.cloned.1.call-update) | async-done | bytes 655376 | tf_op jit(solution)/shard_map/reduce_scatter | solution.py:166
  323.8 2.2 copy.57
  326.0 3.7 %all-to-all-start.1 = ((f32[8,64,320]{2,1,0:T(8,128)}), f32[8,64,320]{2,1,0:T(8,128)S(1)}, u32[]{:S(2)}, u32[]{:S(2)}) async-start(f32[8,64,320]{2,1,0:T(8,128)} %bitcast.46), calls=%async_computation.2 | async-start | bytes 1572864 | tf_op jit(solution)/shard_map/all_to_all | solution.py:167
  329.7 8.3 %fusion = bf16[1,128,2048]{2,1,0:T(8,128)(2,1)} fusion(bf16[128,2560]{0,1:T(8,128)(2,1)S(1)} %add_convert_fusion, bf16[2048,2560]{1,0:T(8,128)(2,1)} %constant_dynamic-update-slice_fusion), kind=kOutput, calls=%fused_computation.3 | convolution fusion | flops 1342439424 | bytes 11665408 | tf_op jit(solution)/shard_map/dot_general | solution.py:153
  338.0 4.3 %all-to-all-done.1 = f32[8,64,320]{2,1,0:T(8,128)S(1)} async-done(((f32[8,64,320]{2,1,0:T(8,128)}), f32[8,64,320]{2,1,0:T(8,128)S(1)}, u32[]{:S(2)}, u32[]{:S(2)}) %all-to-all-start.1) | async-done | bytes 655392 | tf_op jit(solution)/shard_map/all_to_all | solution.py:167
  (87 shorter events, 29.9 us)
Async XLA Ops:
  7.2 252.9 %all-gather.2.cloned.1.call-start = ((), (), s32[]{:S(2)}) async-start(), calls=%async_computation.3 | async-start | bytes 9437184 | tf_op jit(solution)/shard_map/all_gather | solution.py:131
  9.1 5.5 %copy-start.8 = (bf16[2048,256]{1,0:T(8,128)(2,1)S(1)}, bf16[2048,256]{1,0:T(8,128)(2,1)}, u32[]{:S(2)}) copy-start(bf16[2048,256]{1,0:T(8,128)(2,1)} %param.8) | copy-start | bytes 3145732
  9.1 25.1 %collective-permute-start = (s32[1]{0:T(128)}, s32[1]{0:T(128)}, u32[]{:S(2)}, u32[]{:S(2)}) collective-permute-start(s32[1]{0:T(128)} %bitcast.6), channel_id=1, source_target_pairs={{0,1},{1,2},{2,3},{3,4},{4,5},{5,6},{6,7},{8,9},{9,10},{10,11},{11... | collective-permute-start | bytes 20 | tf_op jit(solution)/shard_map/ppermute | solution.py:37
  14.5 1.6 copy-start.9
  14.6 309.2 %reduce-scatter.2.cloned.1.call-start = ((), (), s32[]{:S(2)}) async-start(), calls=%async_computation.4 | async-start | bytes 3276800 | tf_op jit(solution)/shard_map/reduce_scatter | solution.py:166
  17.3 8.8 %copy-start.10 = (bf16[1,128,2048]{2,1,0:T(8,128)(2,1)S(1)}, bf16[1,128,2048]{2,1,0:T(8,128)(2,1)}, u32[]{:S(2)}) copy-start(bf16[1,128,2048]{2,1,0:T(8,128)(2,1)} %param.7) | copy-start | bytes 1572868
  32.0 0.9 copy-start
  32.9 2.0 copy-start.12
  40.5 44.1 %copy-start.11 = (bf16[1,128,2048]{2,1,0:T(8,128)(2,1)S(1)}, bf16[1,128,2048]{2,1,0:T(8,128)(2,1)}, u32[]{:S(2)}) copy-start(bf16[1,128,2048]{2,1,0:T(8,128)(2,1)} %param.11) | copy-start | bytes 1572868
  42.1 7.9 %collective-permute-start.1 = (f32[16,160,128]{2,1,0:T(8,128)S(1)}, f32[16,160,128]{2,1,0:T(8,128)}, u32[]{:S(2)}, u32[]{:S(2)}) collective-permute-start(f32[16,160,128]{2,1,0:T(8,128)S(1)} %maximum_maximum_fusion), channel_id=1, source_target_pairs={{0,1},{1,2},{2,3},{3,4},{4,5},{5,6},{6,7},{8,9},{9,10},{10,11},{11... | collective-permute-start | bytes 3932168 | tf_op jit(solution)/shard_map/ppermute | solution.py:37
  50.0 37.6 %collective-permute-start.2 = (f32[16,160,128]{2,1,0:T(8,128)}, f32[16,160,128]{2,1,0:T(8,128)}, u32[]{:S(2)}, u32[]{:S(2)}) collective-permute-start(f32[16,160,128]{2,1,0:T(8,128)} %collective-permute-done.1), channel_id=1, source_target_pairs={{0,1},{1,2},{2,3},{3,4},{4,5},{5,6},{6,7},{8,9},{9,10},{10,11},{11... | collective-permute-start | bytes 3932168 | tf_op jit(solution)/shard_map/ppermute | solution.py:37
  89.5 46.0 %collective-permute-start.3 = (f32[16,160,128]{2,1,0:T(8,128)S(1)}, f32[16,160,128]{2,1,0:T(8,128)S(1)}, u32[]{:S(2)}, u32[]{:S(2)}) collective-permute-start(f32[16,160,128]{2,1,0:T(8,128)S(1)} %add_select_fusion.3), channel_id=1, source_target_pairs={{0,2},{1,3},{2,4},{3,5},{4,6},{5,7},{8,10},{9,11},{10,12},{11,13},... | collective-permute-start | bytes 3932168 | tf_op jit(solution)/shard_map/ppermute | solution.py:37
  109.3 1.5 copy-start.4
  112.2 28.8 %copy-start.3 = (f32[128,16,136]{0,2,1:T(8,128)}, f32[128,16,136]{0,2,1:T(8,128)S(1)}, u32[]{:S(2)}) copy-start(f32[128,16,136]{0,2,1:T(8,128)S(1)} %fusion.57) | copy-start | bytes 3342340
  135.6 5.3 %copy-start.1 = (f32[16,160,128]{2,1,0:T(8,128)}, f32[16,160,128]{2,1,0:T(8,128)S(1)}, u32[]{:S(2)}) copy-start(f32[16,160,128]{2,1,0:T(8,128)S(1)} %add_select_fusion.2) | copy-start | bytes 3932164
  135.6 1.7 copy-start.6
  159.3 6.7 %copy-start.2 = (f32[16,160,128]{2,1,0:T(8,128)S(1)}, f32[16,160,128]{2,1,0:T(8,128)}, u32[]{:S(2)}) copy-start(f32[16,160,128]{2,1,0:T(8,128)} %copy-done.1) | copy-start | bytes 3932164
  159.3 6.7 %copy-start.7 = (f32[1,128,2048]{1,2,0:T(8,128)S(1)}, f32[1,128,2048]{1,2,0:T(8,128)}, u32[]{:S(2)}) copy-start(f32[1,128,2048]{1,2,0:T(8,128)} %copy.46) | copy-start | bytes 3145732
  159.6 5.1 %collective-permute-start.4 = (f32[16,160,128]{2,1,0:T(8,128)S(1)}, f32[16,160,128]{2,1,0:T(8,128)S(1)}, u32[]{:S(2)}, u32[]{:S(2)}) collective-permute-start(f32[16,160,128]{2,1,0:T(8,128)S(1)} %maximum_maximum_fusion.1), channel_id=1, source_target_pairs={{1,0},{2,1},{3,2},{4,3},{5,4},{6,5},{7,6},{9,8},{10,9},{11,10},{12... | collective-permute-start | bytes 3932168 | tf_op jit(solution)/shard_map/ppermute | solution.py:37
  164.7 19.3 %collective-permute-start.5 = (f32[16,160,128]{2,1,0:T(8,128)S(1)}, f32[16,160,128]{2,1,0:T(8,128)S(1)}, u32[]{:S(2)}, u32[]{:S(2)}) collective-permute-start(f32[16,160,128]{2,1,0:T(8,128)S(1)} %collective-permute-done.4), channel_id=1, source_target_pairs={{1,0},{2,1},{3,2},{4,3},{5,4},{6,5},{7,6},{9,8},{10,9},{11,10},{12... | collective-permute-start | bytes 3932168 | tf_op jit(solution)/shard_map/ppermute | solution.py:37
  166.0 1.6 copy-start.5
  184.2 43.3 %collective-permute-start.6 = (f32[16,160,128]{2,1,0:T(8,128)S(1)}, f32[16,160,128]{2,1,0:T(8,128)S(1)}, u32[]{:S(2)}, u32[]{:S(2)}) collective-permute-start(f32[16,160,128]{2,1,0:T(8,128)S(1)} %add_select_fusion.1), channel_id=1, source_target_pairs={{2,0},{3,1},{4,2},{5,3},{6,4},{7,5},{10,8},{11,9},{12,10},{13,11},... | collective-permute-start | bytes 3932168 | tf_op jit(solution)/shard_map/ppermute | solution.py:37
  326.0 16.3 %all-to-all-start.1 = ((f32[8,64,320]{2,1,0:T(8,128)}), f32[8,64,320]{2,1,0:T(8,128)S(1)}, u32[]{:S(2)}, u32[]{:S(2)}) async-start(f32[8,64,320]{2,1,0:T(8,128)} %bitcast.46), calls=%async_computation.2 | async-start | bytes 1572864 | tf_op jit(solution)/shard_map/all_to_all | solution.py:167
Sparse Core Ops, SparseCore 0:
  14.7 67.0 all-gather.1
  272.5 51.2 reduce-scatter.1
where the time goes:
time: 358 us; the launch traced here: 351 us
  waiting for transfers between devices  129 us (36%)
  matrix products  76.4 us (21%)
  starting transfers between devices  68.5 us (19%)
  blocking collectives  24.1 us (7%)
  local copies, waits for them, and re-layouts  22.7 us (6%)
  between operations  19.5 us (5%)
  other arithmetic  10.5 us (3%)
    ppermute x7, waiting for transfers between devices, shifted(): return lax.ppermute(value, 'seq', pairs)  74.7 us
    ppermute x7, starting transfers between devices, shifted(): return lax.ppermute(value, 'seq', pairs)  64.7 us
    reduce_scatter x1, waiting for transfers between devices, on_device(): lax.psum_scatter(pack_part, 'dp', scatter_dimension=0, tiled=True)  50.3 us
    all_to_all x1, blocking collectives, on_device(): lax.all_to_all(grad_projected.astype(jnp.float32), 'seq', split_axis=1, c...  24.1 us
    dot_general x3, matrix products, block_forward(): jnp.einsum('thf,hfd->thd', phi_query, state_in, precision=highest)  21.2 us
    dot_general x1, matrix products, on_device(): lax.dot_general(tokens_pack, grad_cols, (((0,), (0,)), ((), ())), precisi...  12.3 us
    concatenate x1, local copies, waits for them, and re-layouts, on_device(): weights = jnp.concatenate([query_weight, key_weight, value_weight], axis=1)  8.78 us
    dot_general x3, matrix products, block_summary(): state_sum = jnp.einsum('thf,thd->hfd', weighted, values, precision=highest)  8.73 us
  transfers between devices with their start and end apart: 10, of which 7 were waited for; matrix products, arithmetic and copies ran while one was open for 26% of the time, Pallas kernels for 0%

commit v1 on v0

--- a/solution.py
+++ b/solution.py
@@ -111,8 +111,10 @@
     cotan_local = cotangent[0]
     taylor_map = taylor_table(FEAT)
     width_qk = HEADS * FEAT
-    weights = jnp.concatenate([query_weight, key_weight, value_weight], axis=1)
-    projected = jnp.dot(inputs, weights, preferred_element_type=jnp.float32)
+    parts = (query_weight, key_weight, value_weight)
+    projected = jnp.concatenate(
+        [jnp.dot(inputs, part, preferred_element_type=jnp.float32) for part in parts], axis=1
+    )
 
     def summary(proj_in):
         return block_summary(
@@ -150,9 +152,16 @@
     grad_state_loc, grad_norm_loc = unpack_heads(backward_sum, feats)
     (grad_carried,) = summary_pull((grad_state_loc, grad_norm_loc))
     grad_projected = (grad_direct + grad_carried).astype(jnp.bfloat16)
-    grad_input = jnp.dot(grad_projected, weights.T, preferred_element_type=jnp.float32).astype(
-        jnp.bfloat16
-    )
+    edges = np.cumsum([0] + [part.shape[1] for part in parts])
+    grad_input = sum(
+        lax.dot_general(
+            grad_projected[:, start:stop],
+            part,
+            (((1,), (1,)), ((), ())),
+            preferred_element_type=jnp.float32,
+        )
+        for part, start, stop in zip(parts, edges[:-1], edges[1:])
+    ).astype(jnp.bfloat16)
     grad_cols = lax.all_to_all(
         grad_projected.astype(jnp.float32), "seq", split_axis=1, concat_axis=0, tiled=True
     )
@@ -160,7 +169,7 @@
         tokens_pack,
         grad_cols,
         (((0,), (0,)), ((), ())),
-        precision=highest,
+        precision=lax.Precision.HIGH,
         preferred_element_type=jnp.float32,
     )
     row_part = lax.psum_scatter(pack_part, "dp", scatter_dimension=0, tiled=True)

time: 358 us -> 351 us (0.980); the launches traced: 351 us -> 350 us
  local copies, waits for them, and re-layouts: 22.7 us -> 27 us
  starting transfers between devices: 68.5 us -> 64.3 us
    dot_general x0 -> x1, local copies, waits for them, and re-layouts: none -> 12.4 us  [on_device(): jnp.dot(inputs, part, preferred_element_type=jnp.float32)]
    concatenate x1 -> x0, local copies, waits for them, and re-layouts: 8.78 us -> none  [on_device(): weights = jnp.concatenate([query_weight, key_weight, value_weight], axis=1)]
    ppermute x7, starting transfers between devices: 64.7 us -> 60.5 us  [shifted(): return lax.ppermute(value, 'seq', pairs)]
    dot_general x1, matrix products: 12.3 us -> 8.64 us  [on_device(): lax.dot_general(tokens_pack, grad_cols, (((0,), (0,)), ((), ())), precisi...]
    dot_general x2 -> x6, matrix products: 14.1 us -> 16.8 us  [the longest x3 8.71 us: on_device(): jnp.dot(inputs, part, preferred_element_type=jnp.float32)]
  transfers between devices with their start and end apart: 10 -> 10, of which waited for: 7 -> 7; matrix products, arithmetic and copies ran while one was open for 26% -> 29% of each run, Pallas kernels for 0% -> 0%
where the time goes in v1:
time: 351 us; the launch traced here: 350 us
  waiting for transfers between devices  126 us (36%)
  matrix products  77.3 us (22%)
  starting transfers between devices  64.3 us (18%)
  local copies, waits for them, and re-layouts  27 us (8%)
  blocking collectives  24.1 us (7%)
  between operations  19.4 us (6%)
  other arithmetic  11.7 us (3%)
    ppermute x7, waiting for transfers between devices, shifted(): return lax.ppermute(value, 'seq', pairs)  73.1 us
    ppermute x7, starting transfers between devices, shifted(): return lax.ppermute(value, 'seq', pairs)  60.5 us
    reduce_scatter x1, waiting for transfers between devices, on_device(): lax.psum_scatter(pack_part, 'dp', scatter_dimension=0, tiled=True)  49.3 us
    all_to_all x1, blocking collectives, on_device(): lax.all_to_all(grad_projected.astype(jnp.float32), 'seq', split_axis=1, c...  24.1 us
    dot_general x3, matrix products, block_forward(): jnp.einsum('thf,hfd->thd', phi_query, state_in, precision=highest)  22.8 us
    dot_general x1, local copies, waits for them, and re-layouts, on_device(): jnp.dot(inputs, part, preferred_element_type=jnp.float32)  12.4 us
    dot_general x3, matrix products, on_device(): jnp.dot(inputs, part, preferred_element_type=jnp.float32)  8.71 us
    dot_general x3, matrix products, block_summary(): state_sum = jnp.einsum('thf,thd->hfd', weighted, values, precision=highest)  8.7 us
  transfers between devices with their start and end apart: 10, of which 7 were waited for; matrix products, arithmetic and copies ran while one was open for 29% of the time, Pallas kernels for 0%

profile of v1, /device:TPU:0, one launch (start us, length us, event | category | flops | bytes accessed | tf_op | source)
XLA Modules:
  0.0 349.9 jit_solution(14237014579539655600)
XLA Ops:
  9.2 3.4 collective-permute-start
  12.6 2.1 bitcast_convert_fusion
  16.8 12.4 %copy.82 = bf16[2048,2048]{1,0:T(8,128)(2,1)} copy(bf16[2048,2048]{0,1:T(8,128)(2,1)} %bitcast.131) | data formatting | bytes 16777216 | tf_op jit(solution)/shard_map/dot_general | solution.py:116
  29.2 6.4 %fusion.35 = f32[128,16,128]{2,0,1:T(8,128)S(1)} fusion(bf16[16,128,2048]{2,1,0:T(8,128)(2,1)} %bitcast.132, bf16[1,128,2048]{2,1,0:T(8,128)(2,1)S(1)} %copy-done.1), kind=kOutput, calls=%fused_computation.62 | convolution fusion | flops 1073741824 | bytes 9961472 | tf_op jit(solution)/shard_map/dot_general | solution.py:116
  39.0 2.7 fusion.63
  44.0 5.8 %collective-permute-start.1 = (f32[16,160,128]{2,1,0:T(8,128)S(1)}, f32[16,160,128]{2,1,0:T(8,128)}, u32[]{:S(2)}, u32[]{:S(2)}) collective-permute-start(f32[16,160,128]{2,1,0:T(8,128)S(1)} %maximum_maximum_fusion), channel_id=1, source_target_pairs={{0,1},{1,2},{2,3},{3,4},{4,5},{5,6},{6,7},{8,9},{9,10},{10,11},{11... | collective-permute-start | bytes 3932168 | tf_op jit(solution)/shard_map/ppermute | solution.py:37
  51.6 33.1 %collective-permute-start.2 = (f32[16,160,128]{2,1,0:T(8,128)}, f32[16,160,128]{2,1,0:T(8,128)}, u32[]{:S(2)}, u32[]{:S(2)}) collective-permute-start(f32[16,160,128]{2,1,0:T(8,128)} %collective-permute-done.1), channel_id=1, source_target_pairs={{0,1},{1,2},{2,3},{3,4},{4,5},{5,6},{6,7},{8,9},{9,10},{10,11},{11... | collective-permute-start | bytes 3932168 | tf_op jit(solution)/shard_map/ppermute | solution.py:37
  84.7 2.2 copy.55
  86.9 2.0 convolution_multiply_fusion.3
  91.7 1.9 add_select_fusion.3
  93.6 14.0 %collective-permute-start.3 = (f32[16,160,128]{2,1,0:T(8,128)S(1)}, f32[16,160,128]{2,1,0:T(8,128)S(1)}, u32[]{:S(2)}, u32[]{:S(2)}) collective-permute-start(f32[16,160,128]{2,1,0:T(8,128)S(1)} %add_select_fusion.3), channel_id=1, source_target_pairs={{0,2},{1,3},{2,4},{3,5},{4,6},{5,7},{8,10},{9,11},{10,12},{11,13},... | collective-permute-start | bytes 3932168 | tf_op jit(solution)/shard_map/ppermute | solution.py:37
  107.7 1.8 fusion.42
  109.8 2.0 fusion.43
  114.3 21.2 %collective-permute-done.3 = f32[16,160,128]{2,1,0:T(8,128)S(1)} collective-permute-done((f32[16,160,128]{2,1,0:T(8,128)S(1)}, f32[16,160,128]{2,1,0:T(8,128)S(1)}, u32[]{:S(2)}, u32[]{:S(2)}) %collective-permute-start.3) | collective-permute-done | bytes 1310752 | tf_op jit(solution)/shard_map/ppermute | solution.py:37
  137.4 5.1 %multiply_reduce_fusion.4 = (f32[128,16]{0,1:T(8,128)S(1)}, bf16[128,16,128]{0,2,1:T(8,128)(2,1)}) fusion(f32[128,16,128]{0,2,1:T(8,128)S(1)} %bitcast.158, f32[128,16]{0,1:T(8,128)S(1)} %get-tuple-element.16, f32[128,16]{0,1:T(8,128)S(1)} %get-tuple-element.17, f32[16,128,128]{2,1,0:T(8,128)S(1)} %fusion.43, f32[128,16,136]{0,2,1:T(8,128)S(1)} %fusion.67, ...), kind=kOutput, calls=%fused_computation.54 | convolution fusion | flops 483756032 | bytes 5203044 | tf_op jit(solution)/shard_map/jvp(thf,hfd->thd)/dot_general | solution.py:87
  142.6 2.3 fusion.64
  144.9 16.2 %fusion.23 = f32[16,153,128]{2,1,0:T(8,128)S(1)} fusion(f32[128]{0:T(128)} %copy-done.24, f32[128,16,136]{0,2,1:T(8,128)} %copy-done.10, f32[128,16,16]{0,2,1:T(8,128)S(1)} %bitcast.150, f32[153]{0:T(256)S(1)} %pad.40.clone, f32[128,16,128]{0,2,1:T(8,128)} %bitcast.157, f32[128,16]{0,1:T(8,128)} %copy-done.22), kind=kOutput, calls=%fused_computation.48 | convolution fusion | flops 482447360 | bytes 3556452 | tf_op jit(solution)/shard_map/transpose(jvp(thf,hfd->thd))/dot_general | solution.py:87
  162.9 3.6 %collective-permute-done.4 = f32[16,160,128]{2,1,0:T(8,128)S(1)} collective-permute-done((f32[16,160,128]{2,1,0:T(8,128)S(1)}, f32[16,160,128]{2,1,0:T(8,128)S(1)}, u32[]{:S(2)}, u32[]{:S(2)}) %collective-permute-start.4) | collective-permute-done | bytes 1310752 | tf_op jit(solution)/shard_map/ppermute | solution.py:37
  172.1 13.7 %collective-permute-done.5 = f32[16,160,128]{2,1,0:T(8,128)S(1)} collective-permute-done((f32[16,160,128]{2,1,0:T(8,128)S(1)}, f32[16,160,128]{2,1,0:T(8,128)S(1)}, u32[]{:S(2)}, u32[]{:S(2)}) %collective-permute-start.5) | collective-permute-done | bytes 1310752 | tf_op jit(solution)/shard_map/ppermute | solution.py:37
  189.1 1.9 fusion.18
  193.0 2.3 fusion.27
  196.5 32.8 %collective-permute-done.6 = f32[16,160,128]{2,1,0:T(8,128)S(1)} collective-permute-done((f32[16,160,128]{2,1,0:T(8,128)S(1)}, f32[16,160,128]{2,1,0:T(8,128)S(1)}, u32[]{:S(2)}, u32[]{:S(2)}) %collective-permute-start.6) | collective-permute-done | bytes 1310752 | tf_op jit(solution)/shard_map/ppermute | solution.py:37
  229.6 2.3 fusion.5
  231.9 1.9 fusion.16
  234.7 3.8 %fusion.12 = f32[16,128,128]{2,1,0:T(8,128)S(1)} fusion(f32[16,160,128]{2,1,0:T(8,128)S(1)} %add_select_fusion, f32[128,16,136]{0,2,1:T(8,128)S(1)} %fusion.66, f32[128,16,16]{0,2,1:T(8,128)S(1)} %bitcast.141, f32[153]{0:T(256)S(1)} %pad.40.clone, f32[128]{0:T(128)S(1)} %get-tuple-element.23), kind=kOutput, calls=%fused_computation.33 | convolution fusion | flops 482236416 | bytes 3605604 | tf_op jit(solution)/shard_map/transpose(jvp(thf,thd->hfd))/dot_general | solution.py:103
  238.7 24.1 %all_to_all.42 = f32[128,8,320]{0,2,1:T(8,128)S(1)} all-to-all(f32[128,8,320]{0,2,1:T(8,128)S(1)} %convert.2), channel_id=1, replica_groups=mesh['dp'=4,'seq'=8] {'seq'}, dimensions={1} | all-to-all | bytes 2621440 | tf_op jit(solution)/shard_map/all_to_all | solution.py:165
  262.8 8.6 %convolution_bitcast_fusion = f32[2048,320]{0,1:T(8,128)} fusion(f32[1024,2048]{1,0:T(8,128)} %all-gather.2.cloned.1.call-done, f32[128,8,320]{0,2,1:T(8,128)S(1)} %all_to_all.42), kind=kOutput, calls=%fused_computation | convolution fusion | flops 4026531840 | bytes 12320768 | tf_op jit(solution)/shard_map/dot_general | solution.py:168
  273.5 49.3 %reduce-scatter.2.cloned.1.call-done = f32[512,320]{0,1:T(8,128)} async-done(((f32[2048,320]{0,1:T(8,128)}), f32[512,320]{0,1:T(8,128)}) %reduce-scatter.2.cloned.1.call-update) | async-done | bytes 655376 | tf_op jit(solution)/shard_map/reduce_scatter | solution.py:175
  322.9 2.2 copy.64
  325.1 3.7 %all-to-all-start.1 = ((f32[8,64,320]{2,1,0:T(8,128)}), f32[8,64,320]{2,1,0:T(8,128)S(1)}, u32[]{:S(2)}, u32[]{:S(2)}) async-start(f32[8,64,320]{2,1,0:T(8,128)} %bitcast.155), calls=%async_computation.2 | async-start | bytes 1572864 | tf_op jit(solution)/shard_map/all_to_all | solution.py:176
  328.8 6.3 %fusion.33 = f32[128,2048]{1,0:T(8,128)S(1)} fusion(bf16[2048,2048]{1,0:T(8,128)(2,1)} %param.10, bf16[128,2560]{0,1:T(8,128)(2,1)S(1)} %add_convert_fusion), kind=kOutput, calls=%fused_computation.60 | convolution fusion | flops 1073741824 | bytes 9961472 | tf_op jit(solution)/shard_map/dot_general | solution.py:157
  337.6 3.8 %all-to-all-done.1 = f32[8,64,320]{2,1,0:T(8,128)S(1)} async-done(((f32[8,64,320]{2,1,0:T(8,128)}), f32[8,64,320]{2,1,0:T(8,128)S(1)}, u32[]{:S(2)}, u32[]{:S(2)}) %all-to-all-start.1) | async-done | bytes 655392 | tf_op jit(solution)/shard_map/all_to_all | solution.py:176
  (119 shorter events, 35.5 us)
Async XLA Ops:
  7.2 79.7 %copy-start = (bf16[2048,256]{1,0:T(8,128)(2,1)S(1)}, bf16[2048,256]{1,0:T(8,128)(2,1)}, u32[]{:S(2)}) copy-start(bf16[2048,256]{1,0:T(8,128)(2,1)} %param.8) | copy-start | bytes 3145732
  7.2 255.6 %all-gather.2.cloned.1.call-start = ((), (), s32[]{:S(2)}) async-start(), calls=%async_computation.3 | async-start | bytes 9437184 | tf_op jit(solution)/shard_map/all_gather | solution.py:133
  9.2 5.7 %copy-start.1 = (bf16[1,128,2048]{2,1,0:T(8,128)(2,1)S(1)}, bf16[1,128,2048]{2,1,0:T(8,128)(2,1)}, u32[]{:S(2)}) copy-start(bf16[1,128,2048]{2,1,0:T(8,128)(2,1)} %param.7) | copy-start | bytes 1572868
  9.2 5.7 %copy-start.3 = (bf16[2048,256]{1,0:T(8,128)(2,1)S(1)}, bf16[2048,256]{1,0:T(8,128)(2,1)}, u32[]{:S(2)}) copy-start(bf16[2048,256]{1,0:T(8,128)(2,1)} %param.9) | copy-start | bytes 3145732
  9.2 27.9 %collective-permute-start = (s32[1]{0:T(128)}, s32[1]{0:T(128)}, u32[]{:S(2)}, u32[]{:S(2)}) collective-permute-start(s32[1]{0:T(128)} %bitcast.7), channel_id=1, source_target_pairs={{0,1},{1,2},{2,3},{3,4},{4,5},{5,6},{6,7},{8,9},{9,10},{10,11},{11... | collective-permute-start | bytes 20 | tf_op jit(solution)/shard_map/ppermute | solution.py:37
  14.8 308.0 %reduce-scatter.2.cloned.1.call-start = ((), (), s32[]{:S(2)}) async-start(), calls=%async_computation.4 | async-start | bytes 3276800 | tf_op jit(solution)/shard_map/reduce_scatter | solution.py:175
  29.2 6.5 %copy-start.2 = (f32[128,16,16,16]{0,3,2,1:T(8,128)S(1)}, f32[128,16,16,16]{0,3,2,1:T(8,128)}, u32[]{:S(2)}) copy-start(f32[128,16,16,16]{0,3,2,1:T(8,128)} %broadcast_multiply_fusion.1) | copy-start | bytes 6291460
  29.2 6.5 %copy-start.5 = (f32[256,136,1]{0,1,2:T(8,128)S(1)}, f32[256,136,1]{0,1,2:T(8,128)}, u32[]{:S(2)}) copy-start(f32[256,136,1]{0,1,2:T(8,128)} %constant.45) | copy-start | bytes 417796
  35.7 6.7 %copy-start.16 = (f32[160]{0:T(256)}, f32[160]{0:T(256)S(1)}, u32[]{:S(2)}) copy-start(f32[160]{0:T(256)S(1)} %pad.39.clone) | copy-start | bytes 1924
  38.3 98.8 %copy-start.24 = (f32[128]{0:T(128)}, f32[128]{0:T(128)S(1)}, u32[]{:S(2)}) copy-start(f32[128]{0:T(128)S(1)} %get-tuple-element.22) | copy-start | bytes 1540
  44.0 7.5 %collective-permute-start.1 = (f32[16,160,128]{2,1,0:T(8,128)S(1)}, f32[16,160,128]{2,1,0:T(8,128)}, u32[]{:S(2)}, u32[]{:S(2)}) collective-permute-start(f32[16,160,128]{2,1,0:T(8,128)S(1)} %maximum_maximum_fusion), channel_id=1, source_target_pairs={{0,1},{1,2},{2,3},{3,4},{4,5},{5,6},{6,7},{8,9},{9,10},{10,11},{11... | collective-permute-start | bytes 3932168 | tf_op jit(solution)/shard_map/ppermute | solution.py:37
  51.6 40.2 %collective-permute-start.2 = (f32[16,160,128]{2,1,0:T(8,128)}, f32[16,160,128]{2,1,0:T(8,128)}, u32[]{:S(2)}, u32[]{:S(2)}) collective-permute-start(f32[16,160,128]{2,1,0:T(8,128)} %collective-permute-done.1), channel_id=1, source_target_pairs={{0,1},{1,2},{2,3},{3,4},{4,5},{5,6},{6,7},{8,9},{9,10},{10,11},{11... | collective-permute-start | bytes 3932168 | tf_op jit(solution)/shard_map/ppermute | solution.py:37
  93.6 42.0 %collective-permute-start.3 = (f32[16,160,128]{2,1,0:T(8,128)S(1)}, f32[16,160,128]{2,1,0:T(8,128)S(1)}, u32[]{:S(2)}, u32[]{:S(2)}) collective-permute-start(f32[16,160,128]{2,1,0:T(8,128)S(1)} %add_select_fusion.3), channel_id=1, source_target_pairs={{0,2},{1,3},{2,4},{3,5},{4,6},{5,7},{8,10},{9,11},{10,12},{11,13},... | collective-permute-start | bytes 3932168 | tf_op jit(solution)/shard_map/ppermute | solution.py:37
  109.6 2.2 copy-start.11
  109.8 2.0 copy-start.6
  113.1 29.5 %copy-start.10 = (f32[128,16,136]{0,2,1:T(8,128)}, f32[128,16,136]{0,2,1:T(8,128)S(1)}, u32[]{:S(2)}) copy-start(f32[128,16,136]{0,2,1:T(8,128)S(1)} %fusion.67) | copy-start | bytes 3342340
  135.7 6.8 %copy-start.8 = (f32[16,160,128]{2,1,0:T(8,128)}, f32[16,160,128]{2,1,0:T(8,128)S(1)}, u32[]{:S(2)}) copy-start(f32[16,160,128]{2,1,0:T(8,128)S(1)} %add_select_fusion.2) | copy-start | bytes 3932164
  137.1 5.5 %copy-start.22 = (f32[128,16]{0,1:T(8,128)}, f32[128,16]{0,1:T(8,128)S(1)}, u32[]{:S(2)}) copy-start(f32[128,16]{0,1:T(8,128)S(1)} %get-tuple-element.17) | copy-start | bytes 24580
  137.4 5.1 %copy-start.25 = (f32[128]{0:T(128)S(1)}, f32[128]{0:T(128)}, u32[]{:S(2)}) copy-start(f32[128]{0:T(128)} %copy-done.24) | copy-start | bytes 1540
  142.6 2.3 copy-start.20
  144.9 16.2 %copy-start.17 = (f32[160]{0:T(256)S(1)}, f32[160]{0:T(256)}, u32[]{:S(2)}) copy-start(f32[160]{0:T(256)} %copy-done.16) | copy-start | bytes 1924
  144.9 16.2 %copy-start.19 = (f32[160]{0:T(256)S(1)}, f32[160]{0:T(256)}, u32[]{:S(2)}) copy-start(f32[160]{0:T(256)} %copy-done.18) | copy-start | bytes 1924
  161.1 6.7 %copy-start.9 = (f32[16,160,128]{2,1,0:T(8,128)S(1)}, f32[16,160,128]{2,1,0:T(8,128)}, u32[]{:S(2)}) copy-start(f32[16,160,128]{2,1,0:T(8,128)} %copy-done.8) | copy-start | bytes 3932164
  161.1 6.7 %copy-start.14 = (f32[1,128,2048]{1,2,0:T(8,128)S(1)}, f32[1,128,2048]{1,2,0:T(8,128)}, u32[]{:S(2)}) copy-start(f32[1,128,2048]{1,2,0:T(8,128)} %copy.55) | copy-start | bytes 3145732
  161.1 6.7 %copy-start.21 = (f32[16,128]{1,0:T(8,128)S(1)}, f32[16,128]{1,0:T(8,128)}, u32[]{:S(2)}) copy-start(f32[16,128]{1,0:T(8,128)} %copy-done.20) | copy-start | bytes 24580
  161.2 6.7 %copy-start.23 = (f32[128,16]{0,1:T(8,128)S(1)}, f32[128,16]{0,1:T(8,128)}, u32[]{:S(2)}) copy-start(f32[128,16]{0,1:T(8,128)} %copy-done.22) | copy-start | bytes 24580
  161.2 6.7 %copy-start.26 = (f32[128]{0:T(128)S(1)}, f32[128]{0:T(128)}, u32[]{:S(2)}) copy-start(f32[128]{0:T(128)} %copy-done.24) | copy-start | bytes 1540
  161.5 5.1 %collective-permute-start.4 = (f32[16,160,128]{2,1,0:T(8,128)S(1)}, f32[16,160,128]{2,1,0:T(8,128)S(1)}, u32[]{:S(2)}, u32[]{:S(2)}) collective-permute-start(f32[16,160,128]{2,1,0:T(8,128)S(1)} %maximum_maximum_fusion.1), channel_id=1, source_target_pairs={{1,0},{2,1},{3,2},{4,3},{5,4},{6,5},{7,6},{9,8},{10,9},{11,10},{12... | collective-permute-start | bytes 3932168 | tf_op jit(solution)/shard_map/ppermute | solution.py:37
  166.5 19.3 %collective-permute-start.5 = (f32[16,160,128]{2,1,0:T(8,128)S(1)}, f32[16,160,128]{2,1,0:T(8,128)S(1)}, u32[]{:S(2)}, u32[]{:S(2)}) collective-permute-start(f32[16,160,128]{2,1,0:T(8,128)S(1)} %collective-permute-done.4), channel_id=1, source_target_pairs={{1,0},{2,1},{3,2},{4,3},{5,4},{6,5},{7,6},{9,8},{10,9},{11,10},{12... | collective-permute-start | bytes 3932168 | tf_op jit(solution)/shard_map/ppermute | solution.py:37
  185.9 3.2 copy-start.7
  186.0 43.4 %collective-permute-start.6 = (f32[16,160,128]{2,1,0:T(8,128)S(1)}, f32[16,160,128]{2,1,0:T(8,128)S(1)}, u32[]{:S(2)}, u32[]{:S(2)}) collective-permute-start(f32[16,160,128]{2,1,0:T(8,128)S(1)} %add_select_fusion.1), channel_id=1, source_target_pairs={{2,0},{3,1},{4,2},{5,3},{6,4},{7,5},{10,8},{11,9},{12,10},{13,11},... | collective-permute-start | bytes 3932168 | tf_op jit(solution)/shard_map/ppermute | solution.py:37
  325.1 16.3 %all-to-all-start.1 = ((f32[8,64,320]{2,1,0:T(8,128)}), f32[8,64,320]{2,1,0:T(8,128)S(1)}, u32[]{:S(2)}, u32[]{:S(2)}) async-start(f32[8,64,320]{2,1,0:T(8,128)} %bitcast.155), calls=%async_computation.2 | async-start | bytes 1572864 | tf_op jit(solution)/shard_map/all_to_all | solution.py:176
  (6 other events, 9.0 us)
Sparse Core Ops, SparseCore 0:
  14.9 65.8 all-gather.1
  271.6 51.1 reduce-scatter.1

commit v2 on v1

--- a/solution.py
+++ b/solution.py
@@ -112,8 +112,10 @@
     taylor_map = taylor_table(FEAT)
     width_qk = HEADS * FEAT
     parts = (query_weight, key_weight, value_weight)
-    projected = jnp.concatenate(
-        [jnp.dot(inputs, part, preferred_element_type=jnp.float32) for part in parts], axis=1
+    projected = lax.optimization_barrier(
+        jnp.concatenate(
+            [jnp.dot(inputs, part, preferred_element_type=jnp.float32) for part in parts], axis=1
+        )
     )
 
     def summary(proj_in):

time: 351 us -> 336 us (0.957)
  local copies, waits for them, and re-layouts: 27 us -> 16 us
    dot_general x1 -> x0, local copies, waits for them, and re-layouts: 12.4 us -> none  [on_device(): jnp.dot(inputs, part, preferred_element_type=jnp.float32)]
  transfers between devices with their start and end apart: 10 -> 10, of which waited for: 7 -> 7; matrix products, arithmetic and copies ran while one was open for 29% -> 25% of each run, Pallas kernels for 0% -> 0%
where the time goes in v2:
time: 336 us
  waiting for transfers between devices  125 us (37%)
  matrix products  74.8 us (22%)
  starting transfers between devices  64.8 us (19%)
  blocking collectives  24.9 us (7%)
  between operations  19.4 us (6%)
  local copies, waits for them, and re-layouts  16 us (5%)
  other arithmetic  11.2 us (3%)
    ppermute x7, waiting for transfers between devices, shifted(): return lax.ppermute(value, 'seq', pairs)  71.9 us
    ppermute x7, starting transfers between devices, shifted(): return lax.ppermute(value, 'seq', pairs)  61 us
    reduce_scatter x1, waiting for transfers between devices, on_device(): lax.psum_scatter(pack_part, 'dp', scatter_dimension=0, tiled=True)  49.3 us
    all_to_all x1, blocking collectives, on_device(): lax.all_to_all(grad_projected.astype(jnp.float32), 'seq', split_axis=1, c...  24.9 us
    dot_general x3, matrix products, block_forward(): jnp.einsum('thf,hfd->thd', phi_query, state_in, precision=highest)  22.9 us
    dot_general x3, matrix products, block_summary(): state_sum = jnp.einsum('thf,thd->hfd', weighted, values, precision=highest)  9.6 us
    dot_general x1, matrix products, on_device(): lax.dot_general(tokens_pack, grad_cols, (((0,), (0,)), ((), ())), precisi...  8.62 us
    dot_general x3, matrix products, on_device(): lax.dot_general(grad_projected[:, start:stop], part, (((1,), (1,)), ((),...  8.07 us
  transfers between devices with their start and end apart: 10, of which 7 were waited for; matrix products, arithmetic and copies ran while one was open for 25% of the time, Pallas kernels for 0%

profile of v2, /device:TPU:0, one launch (start us, length us, event | category | flops | bytes accessed | tf_op | source)
XLA Modules:
  0.0 336.1 jit_solution(5422942582997927672)
XLA Ops:
  9.2 3.4 %collective-permute-start = (s32[1]{0:T(128)}, s32[1]{0:T(128)}, u32[]{:S(2)}, u32[]{:S(2)}) collective-permute-start(s32[1]{0:T(128)} %bitcast.4), channel_id=1, source_target_pairs={{0,1},{1,2},{2,3},{3,4},{4,5},{5,6},{6,7},{8,9},{9,10},{10,11},{11... | collective-permute-start | bytes 20 | tf_op jit(solution)/shard_map/ppermute | solution.py:37
  12.6 2.2 bitcast_convert_fusion
  14.9 4.7 %fusion.47 = f32[128,2048]{1,0:T(8,128)S(1)} fusion(bf16[2048,2048]{1,0:T(8,128)(2,1)} %param.10, bf16[1,128,2048]{2,1,0:T(8,128)(2,1)S(1)} %copy-done.1), kind=kOutput, calls=%fused_computation.73 | convolution fusion | flops 1073741824 | bytes 9961472 | tf_op jit(solution)/shard_map/dot_general | solution.py:117
  25.4 3.6 %fusion.27 = f32[16,153,128]{2,1,0:T(8,128)} fusion(f32[128,16,136]{0,2,1:T(8,128)S(1)} %fusion.78, f32[128,16,16]{0,2,1:T(8,128)} %bitcast.148, f32[153]{0:T(256)S(1)} %pad.40.clone, f32[128]{0:T(128)S(1)} %get-tuple-element.25, f32[128,2560]{1,0:T(8,128)S(1)} %pad_maximum_fusion), kind=kOutput, calls=%fused_computation.51 | convolution fusion | flops 482236416 | bytes 3548672 | tf_op jit(solution)/shard_map/jvp(thf,thd->hfd)/dot_general | solution.py:103
  31.4 5.3 %collective-permute-start.1 = (f32[16,160,128]{2,1,0:T(8,128)S(1)}, f32[16,160,128]{2,1,0:T(8,128)}, u32[]{:S(2)}, u32[]{:S(2)}) collective-permute-start(f32[16,160,128]{2,1,0:T(8,128)S(1)} %maximum_maximum_fusion), channel_id=1, source_target_pairs={{0,1},{1,2},{2,3},{3,4},{4,5},{5,6},{6,7},{8,9},{9,10},{10,11},{11... | collective-permute-start | bytes 3932168 | tf_op jit(solution)/shard_map/ppermute | solution.py:37
  36.7 1.7 collective-permute-done.1
  38.5 27.2 %collective-permute-start.2 = (f32[16,160,128]{2,1,0:T(8,128)}, f32[16,160,128]{2,1,0:T(8,128)}, u32[]{:S(2)}, u32[]{:S(2)}) collective-permute-start(f32[16,160,128]{2,1,0:T(8,128)} %collective-permute-done.1), channel_id=1, source_target_pairs={{0,1},{1,2},{2,3},{3,4},{4,5},{5,6},{6,7},{8,9},{9,10},{10,11},{11... | collective-permute-start | bytes 3932168 | tf_op jit(solution)/shard_map/ppermute | solution.py:37
  65.6 2.2 copy.59
  71.4 1.9 add_select_fusion.3
  73.3 21.0 %collective-permute-start.3 = (f32[16,160,128]{2,1,0:T(8,128)S(1)}, f32[16,160,128]{2,1,0:T(8,128)S(1)}, u32[]{:S(2)}, u32[]{:S(2)}) collective-permute-start(f32[16,160,128]{2,1,0:T(8,128)S(1)} %add_select_fusion.3), channel_id=1, source_target_pairs={{0,2},{1,3},{2,4},{3,5},{4,6},{5,7},{8,10},{9,11},{10,12},{11,13},... | collective-permute-start | bytes 3932168 | tf_op jit(solution)/shard_map/ppermute | solution.py:37
  94.4 1.8 fusion.56
  96.5 2.0 fusion.23
  101.1 20.3 %collective-permute-done.3 = f32[16,160,128]{2,1,0:T(8,128)S(1)} collective-permute-done((f32[16,160,128]{2,1,0:T(8,128)S(1)}, f32[16,160,128]{2,1,0:T(8,128)S(1)}, u32[]{:S(2)}, u32[]{:S(2)}) %collective-permute-start.3) | collective-permute-done | bytes 1310752 | tf_op jit(solution)/shard_map/ppermute | solution.py:37
  123.2 5.1 %multiply_reduce_fusion.4 = (f32[128,16]{0,1:T(8,128)S(1)}, bf16[128,16,128]{0,2,1:T(8,128)(2,1)}) fusion(f32[128,16,128]{0,2,1:T(8,128)S(1)} %bitcast.169, f32[128,16]{0,1:T(8,128)S(1)} %get-tuple-element.16, f32[128,16]{0,1:T(8,128)S(1)} %get-tuple-element.17, f32[16,128,128]{2,1,0:T(8,128)S(1)} %fusion.23, f32[128,16,136]{0,2,1:T(8,128)S(1)} %fusion.79, ...), kind=kOutput, calls=%fused_computation.60 | convolution fusion | flops 483756032 | bytes 5203044 | tf_op jit(solution)/shard_map/jvp(thf,hfd->thd)/dot_general | solution.py:87
  128.4 2.3 fusion.76
  130.7 16.2 %fusion.29 = f32[16,153,128]{2,1,0:T(8,128)S(1)} fusion(f32[128]{0:T(128)} %copy-done.29, f32[128,16,136]{0,2,1:T(8,128)} %copy-done.15, f32[128,16,16]{0,2,1:T(8,128)} %bitcast.157, f32[153]{0:T(256)S(1)} %pad.40.clone, f32[128,16,128]{0,2,1:T(8,128)} %bitcast.168, f32[128,16]{0,1:T(8,128)} %copy-done.27), kind=kOutput, calls=%fused_computation.54 | convolution fusion | flops 482447360 | bytes 3556452 | tf_op jit(solution)/shard_map/transpose(jvp(thf,hfd->thd))/dot_general | solution.py:87
  148.7 3.6 %collective-permute-done.4 = f32[16,160,128]{2,1,0:T(8,128)S(1)} collective-permute-done((f32[16,160,128]{2,1,0:T(8,128)S(1)}, f32[16,160,128]{2,1,0:T(8,128)S(1)}, u32[]{:S(2)}, u32[]{:S(2)}) %collective-permute-start.4) | collective-permute-done | bytes 1310752 | tf_op jit(solution)/shard_map/ppermute | solution.py:37
  157.8 13.8 %collective-permute-done.5 = f32[16,160,128]{2,1,0:T(8,128)S(1)} collective-permute-done((f32[16,160,128]{2,1,0:T(8,128)S(1)}, f32[16,160,128]{2,1,0:T(8,128)S(1)}, u32[]{:S(2)}, u32[]{:S(2)}) %collective-permute-start.5) | collective-permute-done | bytes 1310752 | tf_op jit(solution)/shard_map/ppermute | solution.py:37
  173.2 1.7 convolution_multiply_fusion.1
  175.0 1.9 fusion.18
  178.8 2.3 fusion.33
  182.3 32.4 %collective-permute-done.6 = f32[16,160,128]{2,1,0:T(8,128)S(1)} collective-permute-done((f32[16,160,128]{2,1,0:T(8,128)S(1)}, f32[16,160,128]{2,1,0:T(8,128)S(1)}, u32[]{:S(2)}, u32[]{:S(2)}) %collective-permute-start.6) | collective-permute-done | bytes 1310752 | tf_op jit(solution)/shard_map/ppermute | solution.py:37
  215.0 2.3 fusion.5
  217.3 1.9 fusion.16
  220.1 3.8 %fusion.12 = f32[16,128,128]{2,1,0:T(8,128)S(1)} fusion(f32[16,160,128]{2,1,0:T(8,128)S(1)} %add_select_fusion, f32[128,16,136]{0,2,1:T(8,128)S(1)} %fusion.78, f32[128,16,16]{0,2,1:T(8,128)S(1)} %bitcast.153, f32[153]{0:T(256)S(1)} %pad.40.clone, f32[128]{0:T(128)S(1)} %get-tuple-element.25), kind=kOutput, calls=%fused_computation.34 | convolution fusion | flops 482236416 | bytes 3605604 | tf_op jit(solution)/shard_map/transpose(jvp(thf,thd->hfd))/dot_general | solution.py:103
  224.2 24.9 %all_to_all.42 = f32[128,8,320]{0,2,1:T(8,128)S(1)} all-to-all(f32[128,8,320]{0,2,1:T(8,128)S(1)} %convert.2), channel_id=1, replica_groups=mesh['dp'=4,'seq'=8] {'seq'}, dimensions={1} | all-to-all | bytes 2621440 | tf_op jit(solution)/shard_map/all_to_all | solution.py:167
  249.0 8.6 %convolution_bitcast_fusion = f32[2048,320]{0,1:T(8,128)} fusion(f32[1024,2048]{1,0:T(8,128)} %all-gather.2.cloned.1.call-done, f32[128,8,320]{0,2,1:T(8,128)S(1)} %all_to_all.42), kind=kOutput, calls=%fused_computation | convolution fusion | flops 4026531840 | bytes 12320768 | tf_op jit(solution)/shard_map/dot_general | solution.py:170
  259.7 49.3 %reduce-scatter.2.cloned.1.call-done = f32[512,320]{0,1:T(8,128)} async-done(((f32[2048,320]{0,1:T(8,128)}), f32[512,320]{0,1:T(8,128)}) %reduce-scatter.2.cloned.1.call-update) | async-done | bytes 655376 | tf_op jit(solution)/shard_map/reduce_scatter | solution.py:177
  309.0 2.3 copy.70
  311.3 3.7 %all-to-all-start.1 = ((f32[8,64,320]{2,1,0:T(8,128)}), f32[8,64,320]{2,1,0:T(8,128)S(1)}, u32[]{:S(2)}, u32[]{:S(2)}) async-start(f32[8,64,320]{2,1,0:T(8,128)} %bitcast.44), calls=%async_computation.2 | async-start | bytes 1572864 | tf_op jit(solution)/shard_map/all_to_all | solution.py:178
  315.0 6.3 %fusion.45 = f32[128,2048]{1,0:T(8,128)S(1)} fusion(bf16[2048,2048]{1,0:T(8,128)(2,1)} %param.10, bf16[128,2560]{0,1:T(8,128)(2,1)S(1)} %add_convert_fusion), kind=kOutput, calls=%fused_computation.70 | convolution fusion | flops 1073741824 | bytes 9961472 | tf_op jit(solution)/shard_map/dot_general | solution.py:159
  323.8 3.8 %all-to-all-done.1 = f32[8,64,320]{2,1,0:T(8,128)S(1)} async-done(((f32[8,64,320]{2,1,0:T(8,128)}), f32[8,64,320]{2,1,0:T(8,128)S(1)}, u32[]{:S(2)}, u32[]{:S(2)}) %all-to-all-start.1) | async-done | bytes 655392 | tf_op jit(solution)/shard_map/all_to_all | solution.py:178
  (130 shorter events, 33.2 us)
Async XLA Ops:
  7.2 12.8 %copy-start = (bf16[2048,256]{1,0:T(8,128)(2,1)S(1)}, bf16[2048,256]{1,0:T(8,128)(2,1)}, u32[]{:S(2)}) copy-start(bf16[2048,256]{1,0:T(8,128)(2,1)} %param.8) | copy-start | bytes 3145732
  7.2 241.8 %all-gather.2.cloned.1.call-start = ((), (), s32[]{:S(2)}) async-start(), calls=%async_computation.3 | async-start | bytes 9437184 | tf_op jit(solution)/shard_map/all_gather | solution.py:135
  9.2 5.7 %copy-start.1 = (bf16[1,128,2048]{2,1,0:T(8,128)(2,1)S(1)}, bf16[1,128,2048]{2,1,0:T(8,128)(2,1)}, u32[]{:S(2)}) copy-start(bf16[1,128,2048]{2,1,0:T(8,128)(2,1)} %param.7) | copy-start | bytes 1572868
  9.2 14.3 %collective-permute-start = (s32[1]{0:T(128)}, s32[1]{0:T(128)}, u32[]{:S(2)}, u32[]{:S(2)}) collective-permute-start(s32[1]{0:T(128)} %bitcast.4), channel_id=1, source_target_pairs={{0,1},{1,2},{2,3},{3,4},{4,5},{5,6},{6,7},{8,9},{9,10},{10,11},{11... | collective-permute-start | bytes 20 | tf_op jit(solution)/shard_map/ppermute | solution.py:37
  14.8 4.8 %copy-start.8 = (bf16[2048,256]{1,0:T(8,128)(2,1)S(1)}, bf16[2048,256]{1,0:T(8,128)(2,1)}, u32[]{:S(2)}) copy-start(bf16[2048,256]{1,0:T(8,128)(2,1)} %param.9) | copy-start | bytes 3145732
  14.9 294.2 %reduce-scatter.2.cloned.1.call-start = ((), (), s32[]{:S(2)}) async-start(), calls=%async_computation.4 | async-start | bytes 3276800 | tf_op jit(solution)/shard_map/reduce_scatter | solution.py:177
  21.8 8.0 %copy-start.21 = (f32[160]{0:T(256)}, f32[160]{0:T(256)S(1)}, u32[]{:S(2)}) copy-start(f32[160]{0:T(256)S(1)} %pad.39.clone) | copy-start | bytes 1924
  24.7 98.1 %copy-start.29 = (f32[128]{0:T(128)}, f32[128]{0:T(128)S(1)}, u32[]{:S(2)}) copy-start(f32[128]{0:T(128)S(1)} %get-tuple-element.24) | copy-start | bytes 1540
  25.4 3.6 %copy-start.3 = (f32[128,256]{0,1:T(8,128)S(1)}, f32[128,256]{0,1:T(8,128)}, u32[]{:S(2)}) copy-start(f32[128,256]{0,1:T(8,128)} %copy-done.2) | copy-start | bytes 393220
  31.4 7.1 %collective-permute-start.1 = (f32[16,160,128]{2,1,0:T(8,128)S(1)}, f32[16,160,128]{2,1,0:T(8,128)}, u32[]{:S(2)}, u32[]{:S(2)}) collective-permute-start(f32[16,160,128]{2,1,0:T(8,128)S(1)} %maximum_maximum_fusion), channel_id=1, source_target_pairs={{0,1},{1,2},{2,3},{3,4},{4,5},{5,6},{6,7},{8,9},{9,10},{10,11},{11... | collective-permute-start | bytes 3932168 | tf_op jit(solution)/shard_map/ppermute | solution.py:37
  38.5 32.9 %collective-permute-start.2 = (f32[16,160,128]{2,1,0:T(8,128)}, f32[16,160,128]{2,1,0:T(8,128)}, u32[]{:S(2)}, u32[]{:S(2)}) collective-permute-start(f32[16,160,128]{2,1,0:T(8,128)} %collective-permute-done.1), channel_id=1, source_target_pairs={{0,1},{1,2},{2,3},{3,4},{4,5},{5,6},{6,7},{8,9},{9,10},{10,11},{11... | collective-permute-start | bytes 3932168 | tf_op jit(solution)/shard_map/ppermute | solution.py:37
  71.4 23.0 %copy-start.4 = (f32[128,256]{0,1:T(8,128)S(1)}, f32[128,256]{0,1:T(8,128)}, u32[]{:S(2)}) copy-start(f32[128,256]{0,1:T(8,128)} %copy-done.2) | copy-start | bytes 393220
  71.4 23.0 %copy-start.6 = (f32[128,256]{0,1:T(8,128)S(1)}, f32[128,256]{0,1:T(8,128)}, u32[]{:S(2)}) copy-start(f32[128,256]{0,1:T(8,128)} %copy.52) | copy-start | bytes 393220
  73.3 48.1 %collective-permute-start.3 = (f32[16,160,128]{2,1,0:T(8,128)S(1)}, f32[16,160,128]{2,1,0:T(8,128)S(1)}, u32[]{:S(2)}, u32[]{:S(2)}) collective-permute-start(f32[16,160,128]{2,1,0:T(8,128)S(1)} %add_select_fusion.3), channel_id=1, source_target_pairs={{0,2},{1,3},{2,4},{3,5},{4,6},{5,7},{8,10},{9,11},{10,12},{11,13},... | collective-permute-start | bytes 3932168 | tf_op jit(solution)/shard_map/ppermute | solution.py:37
  96.3 2.2 copy-start.16
  99.8 28.5 %copy-start.15 = (f32[128,16,136]{0,2,1:T(8,128)}, f32[128,16,136]{0,2,1:T(8,128)S(1)}, u32[]{:S(2)}) copy-start(f32[128,16,136]{0,2,1:T(8,128)S(1)} %fusion.79) | copy-start | bytes 3342340
  121.5 6.8 %copy-start.13 = (f32[16,160,128]{2,1,0:T(8,128)}, f32[16,160,128]{2,1,0:T(8,128)S(1)}, u32[]{:S(2)}) copy-start(f32[16,160,128]{2,1,0:T(8,128)S(1)} %add_select_fusion.2) | copy-start | bytes 3932164
  122.9 5.4 %copy-start.27 = (f32[128,16]{0,1:T(8,128)}, f32[128,16]{0,1:T(8,128)S(1)}, u32[]{:S(2)}) copy-start(f32[128,16]{0,1:T(8,128)S(1)} %get-tuple-element.17) | copy-start | bytes 24580
  123.2 5.1 %copy-start.30 = (f32[128]{0:T(128)S(1)}, f32[128]{0:T(128)}, u32[]{:S(2)}) copy-start(f32[128]{0:T(128)} %copy-done.29) | copy-start | bytes 1540
  128.3 2.3 copy-start.25
  130.7 16.2 %copy-start.22 = (f32[160]{0:T(256)S(1)}, f32[160]{0:T(256)}, u32[]{:S(2)}) copy-start(f32[160]{0:T(256)} %copy-done.21) | copy-start | bytes 1924
  130.7 16.2 %copy-start.24 = (f32[160]{0:T(256)S(1)}, f32[160]{0:T(256)}, u32[]{:S(2)}) copy-start(f32[160]{0:T(256)} %copy-done.23) | copy-start | bytes 1924
  146.9 6.7 %copy-start.14 = (f32[16,160,128]{2,1,0:T(8,128)S(1)}, f32[16,160,128]{2,1,0:T(8,128)}, u32[]{:S(2)}) copy-start(f32[16,160,128]{2,1,0:T(8,128)} %copy-done.13) | copy-start | bytes 3932164
  146.9 6.7 %copy-start.19 = (f32[1,128,2048]{1,2,0:T(8,128)S(1)}, f32[1,128,2048]{1,2,0:T(8,128)}, u32[]{:S(2)}) copy-start(f32[1,128,2048]{1,2,0:T(8,128)} %copy.59) | copy-start | bytes 3145732
  147.0 6.7 %copy-start.26 = (f32[16,128]{1,0:T(8,128)S(1)}, f32[16,128]{1,0:T(8,128)}, u32[]{:S(2)}) copy-start(f32[16,128]{1,0:T(8,128)} %copy-done.25) | copy-start | bytes 24580
  147.0 6.7 %copy-start.28 = (f32[128,16]{0,1:T(8,128)S(1)}, f32[128,16]{0,1:T(8,128)}, u32[]{:S(2)}) copy-start(f32[128,16]{0,1:T(8,128)} %copy-done.27) | copy-start | bytes 24580
  147.0 6.7 %copy-start.31 = (f32[128]{0:T(128)S(1)}, f32[128]{0:T(128)}, u32[]{:S(2)}) copy-start(f32[128]{0:T(128)} %copy-done.29) | copy-start | bytes 1540
  147.3 5.1 %collective-permute-start.4 = (f32[16,160,128]{2,1,0:T(8,128)S(1)}, f32[16,160,128]{2,1,0:T(8,128)S(1)}, u32[]{:S(2)}, u32[]{:S(2)}) collective-permute-start(f32[16,160,128]{2,1,0:T(8,128)S(1)} %maximum_maximum_fusion.1), channel_id=1, source_target_pairs={{1,0},{2,1},{3,2},{4,3},{5,4},{6,5},{7,6},{9,8},{10,9},{11,10},{12... | collective-permute-start | bytes 3932168 | tf_op jit(solution)/shard_map/ppermute | solution.py:37
  152.3 19.3 %collective-permute-start.5 = (f32[16,160,128]{2,1,0:T(8,128)S(1)}, f32[16,160,128]{2,1,0:T(8,128)S(1)}, u32[]{:S(2)}, u32[]{:S(2)}) collective-permute-start(f32[16,160,128]{2,1,0:T(8,128)S(1)} %collective-permute-done.4), channel_id=1, source_target_pairs={{1,0},{2,1},{3,2},{4,3},{5,4},{6,5},{7,6},{9,8},{10,9},{11,10},{12... | collective-permute-start | bytes 3932168 | tf_op jit(solution)/shard_map/ppermute | solution.py:37
  171.8 3.2 copy-start.12
  171.8 43.0 %collective-permute-start.6 = (f32[16,160,128]{2,1,0:T(8,128)S(1)}, f32[16,160,128]{2,1,0:T(8,128)S(1)}, u32[]{:S(2)}, u32[]{:S(2)}) collective-permute-start(f32[16,160,128]{2,1,0:T(8,128)S(1)} %add_select_fusion.1), channel_id=1, source_target_pairs={{2,0},{3,1},{4,2},{5,3},{6,4},{7,5},{10,8},{11,9},{12,10},{13,11},... | collective-permute-start | bytes 3932168 | tf_op jit(solution)/shard_map/ppermute | solution.py:37
  311.3 16.3 %all-to-all-start.1 = ((f32[8,64,320]{2,1,0:T(8,128)}), f32[8,64,320]{2,1,0:T(8,128)S(1)}, u32[]{:S(2)}, u32[]{:S(2)}) async-start(f32[8,64,320]{2,1,0:T(8,128)} %bitcast.44), calls=%async_computation.2 | async-start | bytes 1572864 | tf_op jit(solution)/shard_map/all_to_all | solution.py:178
  (11 other events, 15.2 us)
Sparse Core Ops, SparseCore 0:
  15.0 64.6 all-gather.1
  257.8 51.2 reduce-scatter.1

commit v3 on v2

--- a/solution.py
+++ b/solution.py
@@ -37,14 +37,14 @@
     return lax.ppermute(value, "seq", pairs)
 
 
-def segmented_scan(packed, flag_row, direction, reach):
-    carry = shifted(packed, direction)
-    covered = 1
-    while covered < reach:
-        earlier = shifted(carry, direction * covered)
-        carry = jnp.where(carry[0, flag_row, 0] > 0, carry, carry + earlier)
-        covered *= 2
-    return carry
+def direct_scan(packed, flag_row, direction, reach):
+    total, keep = None, None
+    for distance in range(1, reach + 1):
+        piece = shifted(packed, direction * distance)
+        total = piece if total is None else total + keep * piece
+        stays = 1.0 - piece[0, flag_row, 0]
+        keep = stays if keep is None else keep * stays
+    return total
 
 
 def taylor_table(feat_width):
@@ -130,7 +130,7 @@
     reach = min(count - 1, -(-(longest - 1) // length))
     prev_id = shifted(doc_local[-1:] + 1, 1)[0] - 1
     boundary = (doc_local[-1] != prev_id).astype(jnp.float32)
-    forward_sum = segmented_scan(pack_heads(state_loc, norm_loc, boundary), feats + 2, 1, reach)
+    forward_sum = direct_scan(pack_heads(state_loc, norm_loc, boundary), feats + 2, 1, reach)
     state_in, norm_in = unpack_heads(forward_sum, feats)
     tokens_pack = lax.all_gather(inputs.astype(jnp.float32), "seq", axis=0, tiled=True)
 
@@ -148,7 +148,7 @@
 
     output, attend_pull = jax.vjp(attend, projected, state_in, norm_in)
     grad_direct, grad_state_in, grad_norm_in = attend_pull(cotan_local.astype(jnp.float32))
-    backward_sum = segmented_scan(
+    backward_sum = direct_scan(
         pack_heads(grad_state_in, grad_norm_in, boundary), feats + 2, -1, reach
     )
     grad_state_loc, grad_norm_loc = unpack_heads(backward_sum, feats)

time: 336 us -> 373 us (1.11); the launches traced: 336 us -> 367 us
  waiting for transfers between devices: 125 us -> 188 us
  starting transfers between devices: 64.8 us -> 25.3 us
  blocking collectives: 24.9 us -> 35.1 us
  matrix products: 74.8 us -> 66 us
  other arithmetic: 11.2 us -> 15.8 us
    ppermute x7 -> x9, waiting for transfers between devices: 71.9 us -> 134 us  [shifted(): return lax.ppermute(value, 'seq', pairs)]
    ppermute x7 -> x9, starting transfers between devices: 61 us -> 21.4 us  [shifted(): return lax.ppermute(value, 'seq', pairs)]
    dot_general x3, matrix products: 22.9 us -> 10.7 us  [block_forward(): jnp.einsum('thf,hfd->thd', phi_query, state_in, precision=highest)]
    all_to_all x1, blocking collectives: 24.9 us -> 35.1 us  [on_device(): lax.all_to_all(grad_projected.astype(jnp.float32), 'seq', split_axis=1, c...]
    add x0 -> x2, other arithmetic: none -> 5.99 us  [direct_scan(): total = piece if total is None else total + keep * piece]
  transfers between devices with their start and end apart: 10 -> 12, of which waited for: 7 -> 6; matrix products, arithmetic and copies ran while one was open for 25% -> 21% of each run, Pallas kernels for 0% -> 0%
where the time goes in v3:
time: 373 us; the launch traced here: 367 us
  waiting for transfers between devices  188 us (50%)
  matrix products  66 us (18%)
  blocking collectives  35.1 us (9%)
  starting transfers between devices  25.3 us (7%)
  between operations  21 us (6%)
  local copies, waits for them, and re-layouts  16 us (4%)
  other arithmetic  15.8 us (4%)
    ppermute x9, waiting for transfers between devices, shifted(): return lax.ppermute(value, 'seq', pairs)  134 us
    reduce_scatter x1, waiting for transfers between devices, on_device(): lax.psum_scatter(pack_part, 'dp', scatter_dimension=0, tiled=True)  49.8 us
    all_to_all x1, blocking collectives, on_device(): lax.all_to_all(grad_projected.astype(jnp.float32), 'seq', split_axis=1, c...  35.1 us
    ppermute x9, starting transfers between devices, shifted(): return lax.ppermute(value, 'seq', pairs)  21.4 us
    dot_general x3, matrix products, block_forward(): jnp.einsum('thf,hfd->thd', phi_query, state_in, precision=highest)  10.7 us
    dot_general x1, matrix products, on_device(): lax.dot_general(tokens_pack, grad_cols, (((0,), (0,)), ((), ())), precisi...  8.54 us
    dot_general x3, matrix products, block_summary(): state_sum = jnp.einsum('thf,thd->hfd', weighted, values, precision=highest)  8.32 us
    dot_general x3, matrix products, on_device(): lax.dot_general(grad_projected[:, start:stop], part, (((1,), (1,)), ((),...  8.07 us
  transfers between devices with their start and end apart: 12, of which 6 were waited for; matrix products, arithmetic and copies ran while one was open for 21% of the time, Pallas kernels for 0%

profile of v3, /device:TPU:0, one launch (start us, length us, event | category | flops | bytes accessed | tf_op | source)
XLA Modules:
  0.0 367.3 jit_solution(18008983168016770214)
XLA Ops:
  7.2 2.2 bitcast_convert_fusion
  10.8 3.3 collective-permute-start
  16.0 4.7 %fusion.47 = f32[128,2048]{1,0:T(8,128)S(1)} fusion(bf16[2048,2048]{1,0:T(8,128)(2,1)} %param.10, bf16[1,128,2048]{2,1,0:T(8,128)(2,1)S(1)} %copy-done.1), kind=kOutput, calls=%fused_computation.71 | convolution fusion | flops 1073741824 | bytes 9961472 | tf_op jit(solution)/shard_map/dot_general | solution.py:117
  27.7 2.5 fusion.27
  31.5 5.7 %collective-permute-start.4 = (f32[16,160,128]{2,1,0:T(8,128)}, f32[16,160,128]{2,1,0:T(8,128)}, u32[]{:S(2)}, u32[]{:S(2)}) collective-permute-start(f32[16,160,128]{2,1,0:T(8,128)} %maximum_maximum_fusion), channel_id=1, source_target_pairs={{0,4},{1,5},{2,6},{3,7},{8,12},{9,13},{10,14},{11,15},{16,20},{17,... | collective-permute-start | bytes 3932168 | tf_op jit(solution)/shard_map/ppermute | solution.py:37
  37.2 2.7 collective-permute-start.3
  40.0 2.1 collective-permute-start.1
  42.1 2.4 collective-permute-start.2
  46.7 2.9 fusion.23
  49.6 2.3 fusion.79
  53.2 65.3 %collective-permute-done.2 = f32[16,160,128]{2,1,0:T(8,128)S(1)} collective-permute-done((f32[16,160,128]{2,1,0:T(8,128)}, f32[16,160,128]{2,1,0:T(8,128)S(1)}, u32[]{:S(2)}, u32[]{:S(2)}) %collective-permute-start.2) | collective-permute-done | bytes 1310752 | tf_op jit(solution)/shard_map/ppermute | solution.py:37
  121.9 21.6 %collective-permute-done.4 = f32[16,160,128]{2,1,0:T(8,128)} collective-permute-done((f32[16,160,128]{2,1,0:T(8,128)}, f32[16,160,128]{2,1,0:T(8,128)}, u32[]{:S(2)}, u32[]{:S(2)}) %collective-permute-start.4) | collective-permute-done | bytes 1310752 | tf_op jit(solution)/shard_map/ppermute | solution.py:37
  143.5 3.0 multiply_add_fusion.2
  148.3 5.1 %multiply_reduce_fusion.4 = (f32[128,16]{0,1:T(8,128)S(1)}, bf16[128,16,128]{0,2,1:T(8,128)(2,1)}) fusion(f32[128,16,128]{0,2,1:T(8,128)S(1)} %bitcast.171, f32[128,16]{0,1:T(8,128)S(1)} %get-tuple-element.16, f32[128,16]{0,1:T(8,128)S(1)} %get-tuple-element.17, f32[16,128,128]{2,1,0:T(8,128)S(1)} %copy-done.27, f32[128,16,136]{0,2,1:T(8,128)S(1)} %copy-done.23, ...), kind=kOutput, calls=%fused_computation.58 | convolution fusion | flops 483756032 | bytes 5203044 | tf_op jit(solution)/shard_map/jvp(thf,hfd->thd)/dot_general | solution.py:87
  153.4 2.3 fusion.76
  155.9 4.0 %fusion.29 = f32[16,153,128]{2,1,0:T(8,128)S(1)} fusion(f32[128]{0:T(128)} %copy-done.42, f32[128,16,136]{0,2,1:T(8,128)} %fusion.79, f32[128,16,16]{0,2,1:T(8,128)} %bitcast.159, f32[153]{0:T(256)S(1)} %pad.40.clone, f32[128,16,128]{0,2,1:T(8,128)} %bitcast.170, f32[128,16]{0,1:T(8,128)} %copy-done.40), kind=kOutput, calls=%fused_computation.52 | convolution fusion | flops 482447360 | bytes 3556452 | tf_op jit(solution)/shard_map/transpose(jvp(thf,hfd->thd))/dot_general | solution.py:87
  169.7 2.4 convolution_multiply_fusion.1
  172.1 1.9 fusion.18
  176.5 3.3 fusion.33
  179.9 5.9 %collective-permute-done.5 = f32[16,160,128]{2,1,0:T(8,128)S(1)} collective-permute-done((f32[16,160,128]{2,1,0:T(8,128)}, f32[16,160,128]{2,1,0:T(8,128)S(1)}, u32[]{:S(2)}, u32[]{:S(2)}) %collective-permute-start.5) | collective-permute-done | bytes 1310752 | tf_op jit(solution)/shard_map/ppermute | solution.py:37
  186.9 41.7 %collective-permute-done.6 = f32[16,160,128]{2,1,0:T(8,128)S(1)} collective-permute-done((f32[16,160,128]{2,1,0:T(8,128)}, f32[16,160,128]{2,1,0:T(8,128)S(1)}, u32[]{:S(2)}, u32[]{:S(2)}) %collective-permute-start.6) | collective-permute-done | bytes 1310752 | tf_op jit(solution)/shard_map/ppermute | solution.py:37
  232.1 3.0 multiply_add_fusion.1
  235.1 2.3 fusion.5
  237.5 2.3 fusion.16
  240.8 3.6 fusion.12
  244.7 35.1 %all_to_all.42 = f32[128,8,320]{0,2,1:T(8,128)S(1)} all-to-all(f32[128,8,320]{0,2,1:T(8,128)S(1)} %convert.2), channel_id=1, replica_groups=mesh['dp'=4,'seq'=8] {'seq'}, dimensions={1} | all-to-all | bytes 2621440 | tf_op jit(solution)/shard_map/all_to_all | solution.py:167
  279.8 8.5 %convolution_bitcast_fusion = f32[2048,320]{0,1:T(8,128)} fusion(f32[1024,2048]{1,0:T(8,128)} %all-gather.2.cloned.1.call-done, f32[128,8,320]{0,2,1:T(8,128)S(1)} %all_to_all.42), kind=kOutput, calls=%fused_computation | convolution fusion | flops 4026531840 | bytes 12320768 | tf_op jit(solution)/shard_map/dot_general | solution.py:170
  290.4 49.8 %reduce-scatter.2.cloned.1.call-done = f32[512,320]{0,1:T(8,128)} async-done(((f32[2048,320]{0,1:T(8,128)}), f32[512,320]{0,1:T(8,128)}) %reduce-scatter.2.cloned.1.call-update) | async-done | bytes 655376 | tf_op jit(solution)/shard_map/reduce_scatter | solution.py:177
  340.1 2.3 copy.70
  342.4 3.8 %all-to-all-start.1 = ((f32[8,64,320]{2,1,0:T(8,128)}), f32[8,64,320]{2,1,0:T(8,128)S(1)}, u32[]{:S(2)}, u32[]{:S(2)}) async-start(f32[8,64,320]{2,1,0:T(8,128)} %bitcast.46), calls=%async_computation.2 | async-start | bytes 1572864 | tf_op jit(solution)/shard_map/all_to_all | solution.py:178
  346.2 6.3 %fusion.45 = f32[128,2048]{1,0:T(8,128)S(1)} fusion(bf16[2048,2048]{1,0:T(8,128)(2,1)} %param.10, bf16[128,2560]{0,1:T(8,128)(2,1)S(1)} %add_convert_fusion), kind=kOutput, calls=%fused_computation.68 | convolution fusion | flops 1073741824 | bytes 9961472 | tf_op jit(solution)/shard_map/dot_general | solution.py:159
  355.1 3.7 %all-to-all-done.1 = f32[8,64,320]{2,1,0:T(8,128)S(1)} async-done(((f32[8,64,320]{2,1,0:T(8,128)}), f32[8,64,320]{2,1,0:T(8,128)S(1)}, u32[]{:S(2)}, u32[]{:S(2)}) %all-to-all-start.1) | async-done | bytes 655392 | tf_op jit(solution)/shard_map/all_to_all | solution.py:178
  (160 shorter events, 38.2 us)
Async XLA Ops:
  7.2 8.5 %copy-start = (bf16[2048,256]{1,0:T(8,128)(2,1)S(1)}, bf16[2048,256]{1,0:T(8,128)(2,1)}, u32[]{:S(2)}) copy-start(bf16[2048,256]{1,0:T(8,128)(2,1)} %param.8) | copy-start | bytes 3145732
  7.2 6.9 %copy-start.30 = (bf16[1,128,2048]{2,1,0:T(8,128)(2,1)S(1)}, bf16[1,128,2048]{2,1,0:T(8,128)(2,1)}, u32[]{:S(2)}) copy-start(bf16[1,128,2048]{2,1,0:T(8,128)(2,1)} %param.11) | copy-start | bytes 1572868
  7.2 272.6 %all-gather.2.cloned.1.call-start = ((), (), s32[]{:S(2)}) async-start(), calls=%async_computation.3 | async-start | bytes 9437184 | tf_op jit(solution)/shard_map/all_gather | solution.py:135
  9.5 5.8 %copy-start.1 = (bf16[1,128,2048]{2,1,0:T(8,128)(2,1)S(1)}, bf16[1,128,2048]{2,1,0:T(8,128)(2,1)}, u32[]{:S(2)}) copy-start(bf16[1,128,2048]{2,1,0:T(8,128)(2,1)} %param.7) | copy-start | bytes 1572868
  9.5 5.8 %copy-start.9 = (bf16[2048,256]{1,0:T(8,128)(2,1)S(1)}, bf16[2048,256]{1,0:T(8,128)(2,1)}, u32[]{:S(2)}) copy-start(bf16[2048,256]{1,0:T(8,128)(2,1)} %param.9) | copy-start | bytes 3145732
  9.5 330.6 %reduce-scatter.2.cloned.1.call-start = ((), (), s32[]{:S(2)}) async-start(), calls=%async_computation.4 | async-start | bytes 3276800 | tf_op jit(solution)/shard_map/reduce_scatter | solution.py:177
  10.8 13.2 %collective-permute-start = (s32[1]{0:T(128)}, s32[1]{0:T(128)}, u32[]{:S(2)}, u32[]{:S(2)}) collective-permute-start(s32[1]{0:T(128)} %bitcast.4), channel_id=1, source_target_pairs={{0,1},{1,2},{2,3},{3,4},{4,5},{5,6},{6,7},{8,9},{9,10},{10,11},{11... | collective-permute-start | bytes 20 | tf_op jit(solution)/shard_map/ppermute | solution.py:37
  21.8 8.3 %copy-start.34 = (f32[160]{0:T(256)}, f32[160]{0:T(256)S(1)}, u32[]{:S(2)}) copy-start(f32[160]{0:T(256)S(1)} %pad.39.clone) | copy-start | bytes 1924
  26.0 121.9 %copy-start.42 = (f32[128]{0:T(128)}, f32[128]{0:T(128)S(1)}, u32[]{:S(2)}) copy-start(f32[128]{0:T(128)S(1)} %get-tuple-element.24) | copy-start | bytes 1540
  30.2 14.4 %copy-start.3 = (f32[128,256]{0,1:T(8,128)S(1)}, f32[128,256]{0,1:T(8,128)}, u32[]{:S(2)}) copy-start(f32[128,256]{0,1:T(8,128)} %copy-done.2) | copy-start | bytes 393220
  30.2 14.4 %copy-start.6 = (f32[128,256]{0,1:T(8,128)S(1)}, f32[128,256]{0,1:T(8,128)}, u32[]{:S(2)}) copy-start(f32[128,256]{0,1:T(8,128)} %copy.52) | copy-start | bytes 393220
  31.5 112.0 %collective-permute-start.4 = (f32[16,160,128]{2,1,0:T(8,128)}, f32[16,160,128]{2,1,0:T(8,128)}, u32[]{:S(2)}, u32[]{:S(2)}) collective-permute-start(f32[16,160,128]{2,1,0:T(8,128)} %maximum_maximum_fusion), channel_id=1, source_target_pairs={{0,4},{1,5},{2,6},{3,7},{8,12},{9,13},{10,14},{11,15},{16,20},{17,... | collective-permute-start | bytes 3932168 | tf_op jit(solution)/shard_map/ppermute | solution.py:37
  37.2 82.4 %collective-permute-start.3 = (f32[16,160,128]{2,1,0:T(8,128)}, f32[16,160,128]{2,1,0:T(8,128)S(1)}, u32[]{:S(2)}, u32[]{:S(2)}) collective-permute-start(f32[16,160,128]{2,1,0:T(8,128)} %maximum_maximum_fusion), channel_id=1, source_target_pairs={{0,3},{1,4},{2,5},{3,6},{4,7},{8,11},{9,12},{10,13},{11,14},{12,15... | collective-permute-start | bytes 3932168 | tf_op jit(solution)/shard_map/ppermute | solution.py:37
  40.0 12.0 %collective-permute-start.1 = (f32[16,160,128]{2,1,0:T(8,128)}, f32[16,160,128]{2,1,0:T(8,128)S(1)}, u32[]{:S(2)}, u32[]{:S(2)}) collective-permute-start(f32[16,160,128]{2,1,0:T(8,128)} %maximum_maximum_fusion), channel_id=1, source_target_pairs={{0,1},{1,2},{2,3},{3,4},{4,5},{5,6},{6,7},{8,9},{9,10},{10,11},{11... | collective-permute-start | bytes 3932168 | tf_op jit(solution)/shard_map/ppermute | solution.py:37
  42.1 76.3 %collective-permute-start.2 = (f32[16,160,128]{2,1,0:T(8,128)}, f32[16,160,128]{2,1,0:T(8,128)S(1)}, u32[]{:S(2)}, u32[]{:S(2)}) collective-permute-start(f32[16,160,128]{2,1,0:T(8,128)} %maximum_maximum_fusion), channel_id=1, source_target_pairs={{0,2},{1,3},{2,4},{3,5},{4,6},{5,7},{8,10},{9,11},{10,12},{11,13},... | collective-permute-start | bytes 3932168 | tf_op jit(solution)/shard_map/ppermute | solution.py:37
  52.0 69.3 %copy-start.21 = (f32[16,160,128]{2,1,0:T(8,128)}, f32[16,160,128]{2,1,0:T(8,128)S(1)}, u32[]{:S(2)}) copy-start(f32[16,160,128]{2,1,0:T(8,128)S(1)} %collective-permute-done.1) | copy-start | bytes 3932164
  121.9 24.7 %copy-start.7 = (f32[128,256]{0,1:T(8,128)S(1)}, f32[128,256]{0,1:T(8,128)}, u32[]{:S(2)}) copy-start(f32[128,256]{0,1:T(8,128)} %copy.52) | copy-start | bytes 393220
  121.9 24.7 %copy-start.23 = (f32[128,16,136]{0,2,1:T(8,128)S(1)}, f32[128,16,136]{0,2,1:T(8,128)}, u32[]{:S(2)}) copy-start(f32[128,16,136]{0,2,1:T(8,128)} %fusion.79) | copy-start | bytes 3342340
  146.6 6.8 %copy-start.15 = (f32[16,160,128]{2,1,0:T(8,128)}, f32[16,160,128]{2,1,0:T(8,128)S(1)}, u32[]{:S(2)}) copy-start(f32[16,160,128]{2,1,0:T(8,128)S(1)} %multiply_add_fusion.2) | copy-start | bytes 3932164
  147.9 5.4 %copy-start.40 = (f32[128,16]{0,1:T(8,128)}, f32[128,16]{0,1:T(8,128)S(1)}, u32[]{:S(2)}) copy-start(f32[128,16]{0,1:T(8,128)S(1)} %get-tuple-element.17) | copy-start | bytes 24580
  148.3 5.1 %copy-start.43 = (f32[128]{0:T(128)S(1)}, f32[128]{0:T(128)}, u32[]{:S(2)}) copy-start(f32[128]{0:T(128)} %copy-done.42) | copy-start | bytes 1540
  160.0 6.6 %copy-start.16 = (f32[16,160,128]{2,1,0:T(8,128)S(1)}, f32[16,160,128]{2,1,0:T(8,128)}, u32[]{:S(2)}) copy-start(f32[16,160,128]{2,1,0:T(8,128)} %copy-done.15) | copy-start | bytes 3932164
  160.0 6.6 %copy-start.29 = (f32[1,128,2048]{1,2,0:T(8,128)S(1)}, f32[1,128,2048]{1,2,0:T(8,128)}, u32[]{:S(2)}) copy-start(f32[1,128,2048]{1,2,0:T(8,128)} %copy.59) | copy-start | bytes 3145732
  160.0 6.6 %copy-start.39 = (f32[16,128]{1,0:T(8,128)S(1)}, f32[16,128]{1,0:T(8,128)}, u32[]{:S(2)}) copy-start(f32[16,128]{1,0:T(8,128)} %copy-done.38) | copy-start | bytes 24580
  160.0 6.6 %copy-start.41 = (f32[128,16]{0,1:T(8,128)S(1)}, f32[128,16]{0,1:T(8,128)}, u32[]{:S(2)}) copy-start(f32[128,16]{0,1:T(8,128)} %copy-done.40) | copy-start | bytes 24580
  160.0 6.6 %copy-start.44 = (f32[128]{0:T(128)S(1)}, f32[128]{0:T(128)}, u32[]{:S(2)}) copy-start(f32[128]{0:T(128)} %copy-done.42) | copy-start | bytes 1540
  161.3 70.8 %collective-permute-start.8 = (f32[16,160,128]{2,1,0:T(8,128)}, f32[16,160,128]{2,1,0:T(8,128)}, u32[]{:S(2)}, u32[]{:S(2)}) collective-permute-start(f32[16,160,128]{2,1,0:T(8,128)} %maximum_maximum_fusion.1), channel_id=1, source_target_pairs={{4,0},{5,1},{6,2},{7,3},{12,8},{13,9},{14,10},{15,11},{20,16},{21,... | collective-permute-start | bytes 3932168 | tf_op jit(solution)/shard_map/ppermute | solution.py:37
  162.6 67.3 %collective-permute-start.7 = (f32[16,160,128]{2,1,0:T(8,128)}, f32[16,160,128]{2,1,0:T(8,128)S(1)}, u32[]{:S(2)}, u32[]{:S(2)}) collective-permute-start(f32[16,160,128]{2,1,0:T(8,128)} %maximum_maximum_fusion.1), channel_id=1, source_target_pairs={{3,0},{4,1},{5,2},{6,3},{7,4},{11,8},{12,9},{13,10},{14,11},{15,12... | collective-permute-start | bytes 3932168 | tf_op jit(solution)/shard_map/ppermute | solution.py:37
  163.9 21.9 %collective-permute-start.5 = (f32[16,160,128]{2,1,0:T(8,128)}, f32[16,160,128]{2,1,0:T(8,128)S(1)}, u32[]{:S(2)}, u32[]{:S(2)}) collective-permute-start(f32[16,160,128]{2,1,0:T(8,128)} %maximum_maximum_fusion.1), channel_id=1, source_target_pairs={{1,0},{2,1},{3,2},{4,3},{5,4},{6,5},{7,6},{9,8},{10,9},{11,10},{12... | collective-permute-start | bytes 3932168 | tf_op jit(solution)/shard_map/ppermute | solution.py:37
  165.2 63.4 %collective-permute-start.6 = (f32[16,160,128]{2,1,0:T(8,128)}, f32[16,160,128]{2,1,0:T(8,128)S(1)}, u32[]{:S(2)}, u32[]{:S(2)}) collective-permute-start(f32[16,160,128]{2,1,0:T(8,128)} %maximum_maximum_fusion.1), channel_id=1, source_target_pairs={{2,0},{3,1},{4,2},{5,3},{6,4},{7,5},{10,8},{11,9},{12,10},{13,11},... | collective-permute-start | bytes 3932168 | tf_op jit(solution)/shard_map/ppermute | solution.py:37
  185.8 45.7 %copy-start.18 = (f32[16,160,128]{2,1,0:T(8,128)}, f32[16,160,128]{2,1,0:T(8,128)S(1)}, u32[]{:S(2)}) copy-start(f32[16,160,128]{2,1,0:T(8,128)S(1)} %collective-permute-done.5) | copy-start | bytes 3932164
  342.4 16.4 %all-to-all-start.1 = ((f32[8,64,320]{2,1,0:T(8,128)}), f32[8,64,320]{2,1,0:T(8,128)S(1)}, u32[]{:S(2)}, u32[]{:S(2)}) async-start(f32[8,64,320]{2,1,0:T(8,128)} %bitcast.46), calls=%async_computation.2 | async-start | bytes 1572864 | tf_op jit(solution)/shard_map/all_to_all | solution.py:178
  (26 other events, 62.6 us)
Sparse Core Ops, SparseCore 0:
  9.9 131.7 all-gather.1
  288.5 51.6 reduce-scatter.1

commit v4 on v2

--- a/solution.py
+++ b/solution.py
@@ -45,6 +45,41 @@
         carry = jnp.where(carry[0, flag_row, 0] > 0, carry, carry + earlier)
         covered *= 2
     return carry
+
+
+def chip_scan(packed, flag_row, direction, reach):
+    count = lax.axis_size("seq")
+    if count % 2:
+        return segmented_scan(packed, flag_row, direction, reach)
+    chips = count // 2
+    lead, other = (1, 0) if direction > 0 else (0, 1)
+
+    def fold(near, far):
+        return jnp.where(near[0, flag_row, 0] > 0, near, near + far)
+
+    def chip_shift(value, distance):
+        step = direction * distance
+        pairs = [
+            (2 * chip + lead, 2 * (chip + step) + lead)
+            for chip in range(chips)
+            if 0 <= chip + step < chips
+        ]
+        return lax.ppermute(value, "seq", pairs)
+
+    partner = lax.ppermute(
+        packed, "seq", [(2 * chip + other, 2 * chip + lead) for chip in range(chips)]
+    )
+    carry = chip_shift(fold(packed, partner), 1)
+    chip_reach = min(chips - 1, -(-reach // 2))
+    covered = 1
+    while covered < chip_reach:
+        carry = fold(carry, chip_shift(carry, covered))
+        covered *= 2
+    handed = lax.ppermute(
+        carry, "seq", [(2 * chip + lead, 2 * chip + other) for chip in range(chips)]
+    )
+    core = lax.axis_index("seq") % 2
+    return jnp.where(core == lead, fold(partner, carry), handed)
 
 
 def taylor_table(feat_width):
@@ -130,7 +165,7 @@
     reach = min(count - 1, -(-(longest - 1) // length))
     prev_id = shifted(doc_local[-1:] + 1, 1)[0] - 1
     boundary = (doc_local[-1] != prev_id).astype(jnp.float32)
-    forward_sum = segmented_scan(pack_heads(state_loc, norm_loc, boundary), feats + 2, 1, reach)
+    forward_sum = chip_scan(pack_heads(state_loc, norm_loc, boundary), feats + 2, 1, reach)
     state_in, norm_in = unpack_heads(forward_sum, feats)
     tokens_pack = lax.all_gather(inputs.astype(jnp.float32), "seq", axis=0, tiled=True)
 
@@ -148,7 +183,7 @@
 
     output, attend_pull = jax.vjp(attend, projected, state_in, norm_in)
     grad_direct, grad_state_in, grad_norm_in = attend_pull(cotan_local.astype(jnp.float32))
-    backward_sum = segmented_scan(
+    backward_sum = chip_scan(
         pack_heads(grad_state_in, grad_norm_in, boundary), feats + 2, -1, reach
     )
     grad_state_loc, grad_norm_loc = unpack_heads(backward_sum, feats)

time: 336 us -> 326 us (0.970)
  starting transfers between devices: 64.8 us -> 23 us
  waiting for transfers between devices: 125 us -> 147 us
  other arithmetic: 11.2 us -> 18.9 us
    ppermute x0 -> x8, waiting for transfers between devices: none -> 92 us  [the longest x2 50.7 us: chip_scan(): lax.ppermute(carry, 'seq', [(2 * chip + lead, 2 * chip + other) for chip...]
    ppermute x7 -> x1, waiting for transfers between devices: 71.9 us -> 0.01 us  [shifted(): return lax.ppermute(value, 'seq', pairs)]
    ppermute x7 -> x1, starting transfers between devices: 61 us -> 3.43 us  [shifted(): return lax.ppermute(value, 'seq', pairs)]
    ppermute x0 -> x8, starting transfers between devices: none -> 15.9 us  [the longest x2 6.67 us: chip_scan(): lax.ppermute(packed, 'seq', [(2 * chip + other, 2 * chip + lead) for chip...]
    select_n x4 -> x6, other arithmetic: 2.4 us -> 9.54 us  [the longest x4 7.61 us: fold(): return jnp.where(near[0, flag_row, 0] > 0, near, near + far)]
  transfers between devices with their start and end apart: 10 -> 12, of which waited for: 7 -> 7; matrix products, arithmetic and copies ran while one was open for 25% -> 26% of each run, Pallas kernels for 0% -> 0%
where the time goes in v4:
time: 326 us; the launch traced here: 325 us
  waiting for transfers between devices  147 us (45%)
  matrix products  76 us (23%)
  starting transfers between devices  23 us (7%)
  blocking collectives  22.2 us (7%)
  between operations  19.4 us (6%)
  other arithmetic  18.9 us (6%)
  local copies, waits for them, and re-layouts  18.8 us (6%)
    reduce_scatter x1, waiting for transfers between devices, on_device(): lax.psum_scatter(pack_part, 'dp', scatter_dimension=0, tiled=True)  51 us
    ppermute x2, waiting for transfers between devices, chip_scan(): lax.ppermute(carry, 'seq', [(2 * chip + lead, 2 * chip + other) for chip...  50.7 us
    ppermute x4, waiting for transfers between devices, chip_shift(): return lax.ppermute(value, 'seq', pairs)  31.6 us
    dot_general x3, matrix products, block_forward(): jnp.einsum('thf,hfd->thd', phi_query, state_in, precision=highest)  24.9 us
    all_to_all x1, blocking collectives, on_device(): lax.all_to_all(grad_projected.astype(jnp.float32), 'seq', split_axis=1, c...  22.2 us
    ppermute x2, waiting for transfers between devices, chip_scan(): lax.ppermute(packed, 'seq', [(2 * chip + other, 2 * chip + lead) for chip...  9.75 us
    dot_general x3, matrix products, block_summary(): state_sum = jnp.einsum('thf,thd->hfd', weighted, values, precision=highest)  8.66 us
    dot_general x1, matrix products, on_device(): lax.dot_general(tokens_pack, grad_cols, (((0,), (0,)), ((), ())), precisi...  8.6 us
  transfers between devices with their start and end apart: 12, of which 7 were waited for; matrix products, arithmetic and copies ran while one was open for 26% of the time, Pallas kernels for 0%

profile of v4, /device:TPU:0, one launch (start us, length us, event | category | flops | bytes accessed | tf_op | source)
XLA Modules:
  0.0 325.1 jit_solution(13551869792980051829)
XLA Ops:
  9.2 3.4 %collective-permute-start = (s32[1]{0:T(128)}, s32[1]{0:T(128)}, u32[]{:S(2)}, u32[]{:S(2)}) collective-permute-start(s32[1]{0:T(128)} %bitcast.4), channel_id=1, source_target_pairs={{0,1},{1,2},{2,3},{3,4},{4,5},{5,6},{6,7},{8,9},{9,10},{10,11},{11... | collective-permute-start | bytes 20 | tf_op jit(solution)/shard_map/ppermute | solution.py:37
  12.6 4.8 %fusion.49 = f32[128,2048]{1,0:T(8,128)S(1)} fusion(bf16[2048,2048]{1,0:T(8,128)(2,1)} %param.10, bf16[1,128,2048]{2,1,0:T(8,128)(2,1)} %param.7), kind=kOutput, calls=%fused_computation.77 | convolution fusion | flops 1073741824 | bytes 9961472 | tf_op jit(solution)/shard_map/dot_general | solution.py:152
  23.9 2.6 fusion.29
  27.2 2.6 maximum_maximum_fusion
  29.9 5.4 %collective-permute-start.1 = (f32[16,160,128]{2,1,0:T(8,128)}, f32[16,160,128]{2,1,0:T(8,128)}, u32[]{:S(2)}, u32[]{:S(2)}) collective-permute-start(f32[16,160,128]{2,1,0:T(8,128)} %maximum_maximum_fusion), channel_id=1, source_target_pairs={{0,1},{2,3},{4,5},{6,7},{8,9},{10,11},{12,13},{14,15},{16,17},{18,... | collective-permute-start | bytes 3932168 | tf_op jit(solution)/shard_map/ppermute | solution.py:69
  35.3 1.9 collective-permute-done.1
  37.1 3.2 add_select_fusion.5
  44.9 2.2 copy.59
  50.7 2.2 add_select_fusion.4
  54.7 1.8 fusion.58
  56.8 2.0 fusion.25
  62.0 50.7 %collective-permute-done.4 = f32[16,160,128]{2,1,0:T(8,128)S(1)} collective-permute-done((f32[16,160,128]{2,1,0:T(8,128)S(1)}, f32[16,160,128]{2,1,0:T(8,128)S(1)}, u32[]{:S(2)}, u32[]{:S(2)}) %collective-permute-start.4) | collective-permute-done | bytes 1310752 | tf_op jit(solution)/shard_map/ppermute | solution.py:78
  116.0 5.1 %multiply_reduce_fusion.4 = (f32[128,16]{0,1:T(8,128)S(1)}, bf16[128,16,128]{0,2,1:T(8,128)(2,1)}) fusion(f32[128,16,128]{0,2,1:T(8,128)S(1)} %bitcast.170, f32[128,16]{0,1:T(8,128)S(1)} %get-tuple-element.16, f32[128,16]{0,1:T(8,128)S(1)} %get-tuple-element.17, f32[16,128,128]{2,1,0:T(8,128)S(1)} %fusion.25, f32[128,16,136]{0,2,1:T(8,128)S(1)} %fusion.81, ...), kind=kOutput, calls=%fused_computation.64 | convolution fusion | flops 483756032 | bytes 5203044 | tf_op jit(solution)/shard_map/jvp(thf,hfd->thd)/dot_general | solution.py:122
  121.7 2.3 fusion.78
  124.0 16.4 %fusion.31 = f32[16,153,128]{2,1,0:T(8,128)S(1)} fusion(f32[128]{0:T(128)} %get-tuple-element.24, f32[128,16,136]{0,2,1:T(8,128)} %copy-done.17, f32[128,16,16]{0,2,1:T(8,128)} %bitcast.157, f32[153]{0:T(256)} %copy-done.23, f32[128,16,128]{0,2,1:T(8,128)} %bitcast.168, f32[128,16]{0,1:T(8,128)} %copy-done.30), kind=kOutput, calls=%fused_computation.58 | convolution fusion | flops 482447360 | bytes 3556452 | tf_op jit(solution)/shard_map/transpose(jvp(thf,hfd->thd))/dot_general | solution.py:122
  142.1 7.9 %collective-permute-done.5 = f32[16,160,128]{2,1,0:T(8,128)S(1)} collective-permute-done((f32[16,160,128]{2,1,0:T(8,128)S(1)}, f32[16,160,128]{2,1,0:T(8,128)S(1)}, u32[]{:S(2)}, u32[]{:S(2)}) %collective-permute-start.5) | collective-permute-done | bytes 1310752 | tf_op jit(solution)/shard_map/ppermute | solution.py:69
  152.3 18.8 %collective-permute-done.6 = f32[16,160,128]{2,1,0:T(8,128)} collective-permute-done((f32[16,160,128]{2,1,0:T(8,128)S(1)}, f32[16,160,128]{2,1,0:T(8,128)}, u32[]{:S(2)}, u32[]{:S(2)}) %collective-permute-start.6) | collective-permute-done | bytes 1310752 | tf_op jit(solution)/shard_map/ppermute | solution.py:67
  172.5 3.3 %fusion.4 = f32[128,16,153]{0,2,1:T(8,128)S(1)} fusion(f32[16,160,128]{2,1,0:T(8,128)} %copy-done.16, f32[16,153]{1,0:T(8,128)S(1)} %get-tuple-element.22, f32[16,128]{1,0:T(8,128)S(1)} %copy-done.29, f32[128]{0:T(128)} %get-tuple-element.24, f32[128,16,128]{0,2,1:T(8,128)} %bitcast.169, f32[128,16]{0,1:T(8,128)} %copy-done.30), kind=kOutput, calls=%fused_computation.20 | convolution fusion | flops 482447360 | bytes 3639360 | tf_op jit(solution)/shard_map/transpose(jvp(thf,hfd->thd))/dot_general | solution.py:122
  179.1 12.8 %collective-permute-done.7 = f32[16,160,128]{2,1,0:T(8,128)} collective-permute-done((f32[16,160,128]{2,1,0:T(8,128)}, f32[16,160,128]{2,1,0:T(8,128)}, u32[]{:S(2)}, u32[]{:S(2)}) %collective-permute-start.7) | collective-permute-done | bytes 1310752 | tf_op jit(solution)/shard_map/ppermute | solution.py:67
  191.8 1.9 add_select_fusion.1
  197.0 1.9 fusion.20
  200.8 2.3 fusion.35
  205.0 2.3 fusion.5
  207.3 1.9 fusion.18
  210.2 3.8 %fusion.14 = f32[16,128,128]{2,1,0:T(8,128)S(1)} fusion(f32[16,160,128]{2,1,0:T(8,128)S(1)} %fusion.10, f32[128,16,136]{0,2,1:T(8,128)S(1)} %fusion.80, f32[128,16,16]{0,2,1:T(8,128)S(1)} %bitcast.153, f32[153]{0:T(256)S(1)} %copy-done.25, f32[128]{0:T(128)S(1)} %copy-done.27), kind=kOutput, calls=%fused_computation.38 | convolution fusion | flops 482236416 | bytes 3605604 | tf_op jit(solution)/shard_map/transpose(jvp(thf,thd->hfd))/dot_general | solution.py:138
  214.2 22.2 %all_to_all.42 = f32[128,8,320]{0,2,1:T(8,128)S(1)} all-to-all(f32[128,8,320]{0,2,1:T(8,128)S(1)} %convert.2), channel_id=1, replica_groups=mesh['dp'=4,'seq'=8] {'seq'}, dimensions={1} | all-to-all | bytes 2621440 | tf_op jit(solution)/shard_map/all_to_all | solution.py:202
  236.4 8.6 %convolution_bitcast_fusion = f32[2048,320]{0,1:T(8,128)} fusion(f32[1024,2048]{1,0:T(8,128)} %all-gather.2.cloned.1.call-done, f32[128,8,320]{0,2,1:T(8,128)S(1)} %all_to_all.42), kind=kOutput, calls=%fused_computation | convolution fusion | flops 4026531840 | bytes 12320768 | tf_op jit(solution)/shard_map/dot_general | solution.py:205
  247.0 51.0 %reduce-scatter.2.cloned.1.call-done = f32[512,320]{0,1:T(8,128)} async-done(((f32[2048,320]{0,1:T(8,128)}), f32[512,320]{0,1:T(8,128)}) %reduce-scatter.2.cloned.1.call-update) | async-done | bytes 655376 | tf_op jit(solution)/shard_map/reduce_scatter | solution.py:212
  298.0 2.2 copy.70
  300.3 3.7 %all-to-all-start.1 = ((f32[8,64,320]{2,1,0:T(8,128)}), f32[8,64,320]{2,1,0:T(8,128)S(1)}, u32[]{:S(2)}, u32[]{:S(2)}) async-start(f32[8,64,320]{2,1,0:T(8,128)} %bitcast.44), calls=%async_computation.2 | async-start | bytes 1572864 | tf_op jit(solution)/shard_map/all_to_all | solution.py:213
  303.9 6.3 %fusion.47 = f32[128,2048]{1,0:T(8,128)S(1)} fusion(bf16[2048,2048]{1,0:T(8,128)(2,1)} %param.10, bf16[128,2560]{0,1:T(8,128)(2,1)S(1)} %add_convert_fusion), kind=kOutput, calls=%fused_computation.74 | convolution fusion | flops 1073741824 | bytes 9961472 | tf_op jit(solution)/shard_map/dot_general | solution.py:194
  312.8 3.8 %all-to-all-done.1 = f32[8,64,320]{2,1,0:T(8,128)S(1)} async-done(((f32[8,64,320]{2,1,0:T(8,128)}), f32[8,64,320]{2,1,0:T(8,128)S(1)}, u32[]{:S(2)}, u32[]{:S(2)}) %all-to-all-start.1) | async-done | bytes 655392 | tf_op jit(solution)/shard_map/all_to_all | solution.py:213
  (138 shorter events, 44.5 us)
Async XLA Ops:
  7.2 10.6 %copy-start = (bf16[2048,256]{1,0:T(8,128)(2,1)S(1)}, bf16[2048,256]{1,0:T(8,128)(2,1)}, u32[]{:S(2)}) copy-start(bf16[2048,256]{1,0:T(8,128)(2,1)} %param.8) | copy-start | bytes 3145732
  7.2 229.2 %all-gather.2.cloned.1.call-start = ((), (), s32[]{:S(2)}) async-start(), calls=%async_computation.3 | async-start | bytes 9437184 | tf_op jit(solution)/shard_map/all_gather | solution.py:170
  9.2 8.3 %copy-start.1 = (bf16[1,128,2048]{2,1,0:T(8,128)(2,1)S(1)}, bf16[1,128,2048]{2,1,0:T(8,128)(2,1)}, u32[]{:S(2)}) copy-start(bf16[1,128,2048]{2,1,0:T(8,128)(2,1)} %param.7) | copy-start | bytes 1572868
  9.2 8.3 %copy-start.11 = (bf16[2048,256]{1,0:T(8,128)(2,1)S(1)}, bf16[2048,256]{1,0:T(8,128)(2,1)}, u32[]{:S(2)}) copy-start(bf16[2048,256]{1,0:T(8,128)(2,1)} %param.9) | copy-start | bytes 3145732
  9.2 12.1 %collective-permute-start = (s32[1]{0:T(128)}, s32[1]{0:T(128)}, u32[]{:S(2)}, u32[]{:S(2)}) collective-permute-start(s32[1]{0:T(128)} %bitcast.4), channel_id=1, source_target_pairs={{0,1},{1,2},{2,3},{3,4},{4,5},{5,6},{6,7},{8,9},{9,10},{10,11},{11... | collective-permute-start | bytes 20 | tf_op jit(solution)/shard_map/ppermute | solution.py:37
  19.3 95.0 %copy-start.23 = (f32[153]{0:T(256)}, f32[153]{0:T(256)S(1)}, u32[]{:S(2)}) copy-start(f32[153]{0:T(256)S(1)} %pad.40.clone) | copy-start | bytes 1840
  20.0 3.1 copy-start.4
  23.1 3.4 %copy-start.26 = (f32[128]{0:T(128)}, f32[128]{0:T(128)S(1)}, u32[]{:S(2)}) copy-start(f32[128]{0:T(128)S(1)} %get-tuple-element.25) | copy-start | bytes 1540
  29.9 7.3 %collective-permute-start.1 = (f32[16,160,128]{2,1,0:T(8,128)}, f32[16,160,128]{2,1,0:T(8,128)}, u32[]{:S(2)}, u32[]{:S(2)}) collective-permute-start(f32[16,160,128]{2,1,0:T(8,128)} %maximum_maximum_fusion), channel_id=1, source_target_pairs={{0,1},{2,3},{4,5},{6,7},{8,9},{10,11},{12,13},{14,15},{16,17},{18,... | collective-permute-start | bytes 3932168 | tf_op jit(solution)/shard_map/ppermute | solution.py:69
  35.3 6.8 %copy-start.2 = (bf16[1,128,2048]{2,1,0:T(8,128)(2,1)S(1)}, bf16[1,128,2048]{2,1,0:T(8,128)(2,1)}, u32[]{:S(2)}) copy-start(bf16[1,128,2048]{2,1,0:T(8,128)(2,1)} %param.7) | copy-start | bytes 1572868
  40.3 2.9 collective-permute-start.2
  43.1 254.9 %reduce-scatter.2.cloned.1.call-start = ((), (), s32[]{:S(2)}) async-start(), calls=%async_computation.4 | async-start | bytes 3276800 | tf_op jit(solution)/shard_map/reduce_scatter | solution.py:212
  43.2 7.5 %collective-permute-start.3 = (f32[16,160,128]{2,1,0:T(8,128)}, f32[16,160,128]{2,1,0:T(8,128)}, u32[]{:S(2)}, u32[]{:S(2)}) collective-permute-start(f32[16,160,128]{2,1,0:T(8,128)} %collective-permute-done.2), channel_id=1, source_target_pairs={{1,3},{3,5},{5,7},{9,11},{11,13},{13,15},{17,19},{19,21},{21,23},{... | collective-permute-start | bytes 3932168 | tf_op jit(solution)/shard_map/ppermute | solution.py:67
  50.7 4.0 %copy-start.5 = (f32[128,256]{0,1:T(8,128)S(1)}, f32[128,256]{0,1:T(8,128)}, u32[]{:S(2)}) copy-start(f32[128,256]{0,1:T(8,128)} %copy-done.3) | copy-start | bytes 393220
  50.7 4.0 %copy-start.9 = (f32[128,256]{0,1:T(8,128)S(1)}, f32[128,256]{0,1:T(8,128)}, u32[]{:S(2)}) copy-start(f32[128,256]{0,1:T(8,128)} %copy.52) | copy-start | bytes 393220
  52.9 59.7 %collective-permute-start.4 = (f32[16,160,128]{2,1,0:T(8,128)S(1)}, f32[16,160,128]{2,1,0:T(8,128)S(1)}, u32[]{:S(2)}, u32[]{:S(2)}) collective-permute-start(f32[16,160,128]{2,1,0:T(8,128)S(1)} %add_select_fusion.4), channel_id=1, source_target_pairs={{1,0},{3,2},{5,4},{7,6},{9,8},{11,10},{13,12},{15,14},{17,16},{19,... | collective-permute-start | bytes 3932168 | tf_op jit(solution)/shard_map/ppermute | solution.py:78
  60.1 61.0 %copy-start.17 = (f32[128,16,136]{0,2,1:T(8,128)}, f32[128,16,136]{0,2,1:T(8,128)S(1)}, u32[]{:S(2)}) copy-start(f32[128,16,136]{0,2,1:T(8,128)S(1)} %fusion.81) | copy-start | bytes 3342340
  114.2 6.9 %copy-start.16 = (f32[16,160,128]{2,1,0:T(8,128)}, f32[16,160,128]{2,1,0:T(8,128)S(1)}, u32[]{:S(2)}) copy-start(f32[16,160,128]{2,1,0:T(8,128)S(1)} %fusion.9) | copy-start | bytes 3932164
  115.6 5.5 %copy-start.30 = (f32[128,16]{0,1:T(8,128)}, f32[128,16]{0,1:T(8,128)S(1)}, u32[]{:S(2)}) copy-start(f32[128,16]{0,1:T(8,128)S(1)} %get-tuple-element.17) | copy-start | bytes 24580
  116.0 5.8 %copy-start.24 = (f32[153]{0:T(256)S(1)}, f32[153]{0:T(256)}, u32[]{:S(2)}) copy-start(f32[153]{0:T(256)} %copy-done.23) | copy-start | bytes 1840
  140.7 31.7 %copy-start.29 = (f32[16,128]{1,0:T(8,128)S(1)}, f32[16,128]{1,0:T(8,128)}, u32[]{:S(2)}) copy-start(f32[16,128]{1,0:T(8,128)} %copy-done.28) | copy-start | bytes 24580
  140.8 9.2 %collective-permute-start.5 = (f32[16,160,128]{2,1,0:T(8,128)S(1)}, f32[16,160,128]{2,1,0:T(8,128)S(1)}, u32[]{:S(2)}, u32[]{:S(2)}) collective-permute-start(f32[16,160,128]{2,1,0:T(8,128)S(1)} %maximum_maximum_fusion.1), channel_id=1, source_target_pairs={{1,0},{3,2},{5,4},{7,6},{9,8},{11,10},{13,12},{15,14},{17,16},{19,... | collective-permute-start | bytes 3932168 | tf_op jit(solution)/shard_map/ppermute | solution.py:69
  151.0 20.1 %collective-permute-start.6 = (f32[16,160,128]{2,1,0:T(8,128)S(1)}, f32[16,160,128]{2,1,0:T(8,128)}, u32[]{:S(2)}, u32[]{:S(2)}) collective-permute-start(f32[16,160,128]{2,1,0:T(8,128)S(1)} %add_select_fusion.2), channel_id=1, source_target_pairs={{2,0},{4,2},{6,4},{10,8},{12,10},{14,12},{18,16},{20,18},{22,20},{... | collective-permute-start | bytes 3932168 | tf_op jit(solution)/shard_map/ppermute | solution.py:67
  171.1 20.7 %collective-permute-start.7 = (f32[16,160,128]{2,1,0:T(8,128)}, f32[16,160,128]{2,1,0:T(8,128)}, u32[]{:S(2)}, u32[]{:S(2)}) collective-permute-start(f32[16,160,128]{2,1,0:T(8,128)} %collective-permute-done.6), channel_id=1, source_target_pairs={{2,0},{4,2},{6,4},{10,8},{12,10},{14,12},{18,16},{20,18},{22,20},{... | collective-permute-start | bytes 3932168 | tf_op jit(solution)/shard_map/ppermute | solution.py:67
  172.4 3.3 %copy-start.19 = (f32[16,128,128]{1,2,0:T(8,128)S(1)}, f32[16,128,128]{1,2,0:T(8,128)}, u32[]{:S(2)}) copy-start(f32[16,128,128]{1,2,0:T(8,128)} %copy-done.18) | copy-start | bytes 3145732
  172.5 3.3 %copy-start.21 = (f32[1,128,2048]{1,2,0:T(8,128)S(1)}, f32[1,128,2048]{1,2,0:T(8,128)}, u32[]{:S(2)}) copy-start(f32[1,128,2048]{1,2,0:T(8,128)} %copy.59) | copy-start | bytes 3145732
  172.5 3.3 %copy-start.31 = (f32[128,16]{0,1:T(8,128)S(1)}, f32[128,16]{0,1:T(8,128)}, u32[]{:S(2)}) copy-start(f32[128,16]{0,1:T(8,128)} %copy-done.30) | copy-start | bytes 24580
  191.8 3.4 %copy-start.10 = (f32[128,256]{0,1:T(8,128)S(1)}, f32[128,256]{0,1:T(8,128)}, u32[]{:S(2)}) copy-start(f32[128,256]{0,1:T(8,128)} %copy.52) | copy-start | bytes 393220
  193.7 3.3 %copy-start.15 = (f32[256,136,1]{0,1,2:T(8,128)S(1)}, f32[256,136,1]{0,1,2:T(8,128)}, u32[]{:S(2)}) copy-start(f32[256,136,1]{0,1,2:T(8,128)} %constant.64) | copy-start | bytes 417796
  193.7 10.6 %collective-permute-start.8 = (f32[16,160,128]{2,1,0:T(8,128)S(1)}, f32[16,160,128]{2,1,0:T(8,128)S(1)}, u32[]{:S(2)}, u32[]{:S(2)}) collective-permute-start(f32[16,160,128]{2,1,0:T(8,128)S(1)} %add_select_fusion.1), channel_id=1, source_target_pairs={{0,1},{2,3},{4,5},{6,7},{8,9},{10,11},{12,13},{14,15},{16,17},{18,... | collective-permute-start | bytes 3932168 | tf_op jit(solution)/shard_map/ppermute | solution.py:78
  200.8 2.4 copy-start.8
  300.3 16.3 %all-to-all-start.1 = ((f32[8,64,320]{2,1,0:T(8,128)}), f32[8,64,320]{2,1,0:T(8,128)S(1)}, u32[]{:S(2)}, u32[]{:S(2)}) async-start(f32[8,64,320]{2,1,0:T(8,128)} %bitcast.44), calls=%async_computation.2 | async-start | bytes 1572864 | tf_op jit(solution)/shard_map/all_to_all | solution.py:213
  (14 other events, 17.3 us)
Sparse Core Ops, SparseCore 0:
  43.2 70.1 all-gather.1
  245.1 52.8 reduce-scatter.1

commit v5 on v4

--- a/solution.py
+++ b/solution.py
@@ -167,7 +167,13 @@
     boundary = (doc_local[-1] != prev_id).astype(jnp.float32)
     forward_sum = chip_scan(pack_heads(state_loc, norm_loc, boundary), feats + 2, 1, reach)
     state_in, norm_in = unpack_heads(forward_sum, feats)
-    tokens_pack = lax.all_gather(inputs.astype(jnp.float32), "seq", axis=0, tiled=True)
+    tokens_wide = inputs.astype(jnp.float32)
+    half = tokens_wide.shape[1] // 2
+    tokens_first = lax.all_gather(tokens_wide[:, :half], "seq", axis=0, tiled=True)
+    tokens_rest, state_in, norm_in = lax.optimization_barrier(
+        (tokens_wide[:, half:], state_in, norm_in)
+    )
+    tokens_second = lax.all_gather(tokens_rest, "seq", axis=0, tiled=True)
 
     def attend(proj_in, state_sum, norm_sum):
         return block_forward(
@@ -202,12 +208,18 @@
     grad_cols = lax.all_to_all(
         grad_projected.astype(jnp.float32), "seq", split_axis=1, concat_axis=0, tiled=True
     )
-    pack_part = lax.dot_general(
-        tokens_pack,
-        grad_cols,
-        (((0,), (0,)), ((), ())),
-        precision=lax.Precision.HIGH,
-        preferred_element_type=jnp.float32,
+    pack_part = jnp.concatenate(
+        [
+            lax.dot_general(
+                tokens_half,
+                grad_cols,
+                (((0,), (0,)), ((), ())),
+                precision=lax.Precision.HIGH,
+                preferred_element_type=jnp.float32,
+            )
+            for tokens_half in (tokens_first, tokens_second)
+        ],
+        axis=0,
     )
     row_part = lax.psum_scatter(pack_part, "dp", scatter_dimension=0, tiled=True)
     grad_proj = lax.all_to_all(row_part, "seq", split_axis=0, concat_axis=1, tiled=True)

time: 326 us -> 333 us (1.021); the launches traced: 325 us -> 327 us
  blocking collectives: 22.2 us -> 0 us
  waiting for transfers between devices: 147 us -> 163 us
  between operations: 19.4 us -> 32.2 us
  matrix products: 76 us -> 64.7 us
  starting transfers between devices: 23 us -> 26.5 us
    all_to_all x1 -> x0, blocking collectives: 22.2 us -> none  [on_device(): lax.all_to_all(grad_projected.astype(jnp.float32), 'seq', split_axis=1, c...]
    ppermute x2, waiting for transfers between devices: 50.7 us -> 29.4 us  [chip_scan(): lax.ppermute(carry, 'seq', [(2 * chip + lead, 2 * chip + other) for chip...]
    all_to_all x0 -> x1, waiting for transfers between devices: none -> 18.1 us  [on_device(): lax.all_to_all(grad_projected.astype(jnp.float32), 'seq', split_axis=1, c...]
    ppermute x4, waiting for transfers between devices: 31.6 us -> 48.9 us  [chip_shift(): return lax.ppermute(value, 'seq', pairs)]
    dot_general x3, matrix products: 24.9 us -> 10.2 us  [block_forward(): jnp.einsum('thf,hfd->thd', phi_query, state_in, precision=highest)]
    all_to_all x0 -> x1, starting transfers between devices: none -> 4.19 us  [on_device(): lax.all_to_all(grad_projected.astype(jnp.float32), 'seq', split_axis=1, c...]
    dot_general x1 -> x2, matrix products: 8.6 us -> 10.2 us  [on_device(): lax.dot_general(tokens_half, grad_cols, (((0,), (0,)), ((), ())), precisi...]
  transfers between devices with their start and end apart: 12 -> 14, of which waited for: 7 -> 8; matrix products, arithmetic and copies ran while one was open for 26% -> 25% of each run, Pallas kernels for 0% -> 0%
where the time goes in v5:
time: 333 us; the launch traced here: 327 us
  waiting for transfers between devices  163 us (49%)
  matrix products  64.7 us (19%)
  between operations  32.2 us (10%)
  starting transfers between devices  26.5 us (8%)
  local copies, waits for them, and re-layouts  20.9 us (6%)
  other arithmetic  19.5 us (6%)
    reduce_scatter x1, waiting for transfers between devices, on_device(): lax.psum_scatter(pack_part, 'dp', scatter_dimension=0, tiled=True)  49.6 us
    ppermute x4, waiting for transfers between devices, chip_shift(): return lax.ppermute(value, 'seq', pairs)  48.9 us
    ppermute x2, waiting for transfers between devices, chip_scan(): lax.ppermute(carry, 'seq', [(2 * chip + lead, 2 * chip + other) for chip...  29.4 us
    all_to_all x1, waiting for transfers between devices, on_device(): lax.all_to_all(grad_projected.astype(jnp.float32), 'seq', split_axis=1, c...  18.1 us
    ppermute x2, waiting for transfers between devices, chip_scan(): lax.ppermute(packed, 'seq', [(2 * chip + other, 2 * chip + lead) for chip...  13 us
    dot_general x2, matrix products, on_device(): lax.dot_general(tokens_half, grad_cols, (((0,), (0,)), ((), ())), precisi...  10.2 us
    dot_general x3, matrix products, block_forward(): jnp.einsum('thf,hfd->thd', phi_query, state_in, precision=highest)  10.2 us
    dot_general x3, matrix products, on_device(): lax.dot_general(grad_projected[:, start:stop], part, (((1,), (1,)), ((),...  8.07 us
  transfers between devices with their start and end apart: 14, of which 8 were waited for; matrix products, arithmetic and copies ran while one was open for 25% of the time, Pallas kernels for 0%

profile of v5, /device:TPU:0, one launch (start us, length us, event | category | flops | bytes accessed | tf_op | source)
XLA Modules:
  0.0 326.6 jit_solution(16623716394405789824)
XLA Ops:
  9.2 3.4 %collective-permute-start = (s32[1]{0:T(128)}, s32[1]{0:T(128)}, u32[]{:S(2)}, u32[]{:S(2)}) collective-permute-start(s32[1]{0:T(128)} %bitcast.4), channel_id=1, source_target_pairs={{0,1},{1,2},{2,3},{3,4},{4,5},{5,6},{6,7},{8,9},{9,10},{10,11},{11... | collective-permute-start | bytes 20 | tf_op jit(solution)/shard_map/ppermute | solution.py:37
  12.6 4.8 %fusion.50 = f32[128,2048]{1,0:T(8,128)S(1)} fusion(bf16[2048,2048]{1,0:T(8,128)(2,1)} %param.10, bf16[1,128,2048]{2,1,0:T(8,128)(2,1)} %param.7), kind=kOutput, calls=%fused_computation.80 | convolution fusion | flops 1073741824 | bytes 9961472 | tf_op jit(solution)/shard_map/dot_general | solution.py:152
  27.3 5.4 %collective-permute-start.1 = (f32[16,160,128]{2,1,0:T(8,128)}, f32[16,160,128]{2,1,0:T(8,128)}, u32[]{:S(2)}, u32[]{:S(2)}) collective-permute-start(f32[16,160,128]{2,1,0:T(8,128)} %maximum_maximum_fusion), channel_id=1, source_target_pairs={{0,1},{2,3},{4,5},{6,7},{8,9},{10,11},{12,13},{14,15},{16,17},{18,... | collective-permute-start | bytes 3932168 | tf_op jit(solution)/shard_map/ppermute | solution.py:69
  32.6 1.9 collective-permute-done.1
  41.2 2.5 add_select_fusion.4
  46.4 2.2 copy.59
  48.7 2.8 fusion.59
  55.6 29.4 %collective-permute-done.4 = f32[16,160,128]{2,1,0:T(8,128)} collective-permute-done((f32[16,160,128]{2,1,0:T(8,128)}, f32[16,160,128]{2,1,0:T(8,128)}, u32[]{:S(2)}, u32[]{:S(2)}) %collective-permute-start.4) | collective-permute-done | bytes 1310752 | tf_op jit(solution)/shard_map/ppermute | solution.py:78
  85.0 2.3 fusion.8
  89.1 2.1 fusion.68
  91.2 3.6 %convolution_multiply_fusion = f32[16,128,128]{2,1,0:T(8,128)S(1)} fusion(f32[16,153,128]{2,1,0:T(8,128)S(1)} %bitcast.181, f32[128]{0:T(128)S(1)} %get-tuple-element.30, f32[128,16,136]{0,2,1:T(8,128)S(1)} %fusion.80, f32[128,16,16]{0,2,1:T(8,128)S(1)} %bitcast.174, f32[153]{0:T(256)S(1)} %pad.42.clone), kind=kOutput, calls=%fused_computation.27 | convolution fusion | flops 482185216 | bytes 3548260 | tf_op jit(solution)/shard_map/jvp(thf,hfd->thd)/dot_general | solution.py:122
  94.9 2.9 multiply_reduce_fusion.4
  97.8 2.3 fusion.77
  114.2 3.6 %fusion.32 = f32[16,153,128]{2,1,0:T(8,128)S(1)} fusion(f32[128]{0:T(128)} %copy-done.37, f32[128,16,136]{0,2,1:T(8,128)S(1)} %fusion.80, f32[128,16,16]{0,2,1:T(8,128)S(1)} %bitcast.176, f32[153]{0:T(256)} %copy-done.25, f32[128,16,128]{0,2,1:T(8,128)} %bitcast.186, f32[128,16]{0,1:T(8,128)} %copy-done.41), kind=kOutput, calls=%fused_computation.61 | convolution fusion | flops 482447360 | bytes 3556452 | tf_op jit(solution)/shard_map/transpose(jvp(thf,hfd->thd))/dot_general | solution.py:122
  119.6 11.1 %collective-permute-done.5 = f32[16,160,128]{2,1,0:T(8,128)S(1)} collective-permute-done((f32[16,160,128]{2,1,0:T(8,128)S(1)}, f32[16,160,128]{2,1,0:T(8,128)S(1)}, u32[]{:S(2)}, u32[]{:S(2)}) %collective-permute-start.5) | collective-permute-done | bytes 1310752 | tf_op jit(solution)/shard_map/ppermute | solution.py:69
  133.5 23.5 %collective-permute-done.6 = f32[16,160,128]{2,1,0:T(8,128)} collective-permute-done((f32[16,160,128]{2,1,0:T(8,128)}, f32[16,160,128]{2,1,0:T(8,128)}, u32[]{:S(2)}, u32[]{:S(2)}) %collective-permute-start.6) | collective-permute-done | bytes 1310752 | tf_op jit(solution)/shard_map/ppermute | solution.py:67
  158.4 3.0 fusion.4
  164.9 25.3 %collective-permute-done.7 = f32[16,160,128]{2,1,0:T(8,128)} collective-permute-done((f32[16,160,128]{2,1,0:T(8,128)}, f32[16,160,128]{2,1,0:T(8,128)}, u32[]{:S(2)}, u32[]{:S(2)}) %collective-permute-start.7) | collective-permute-done | bytes 1310752 | tf_op jit(solution)/shard_map/ppermute | solution.py:67
  195.3 1.9 fusion.22
  199.2 2.3 fusion.36
  203.3 2.3 fusion.5
  205.6 1.9 fusion.20
  208.6 3.8 %fusion.16 = f32[16,128,128]{2,1,0:T(8,128)S(1)} fusion(f32[16,160,128]{2,1,0:T(8,128)S(1)} %fusion.9, f32[128,16,136]{0,2,1:T(8,128)S(1)} %fusion.79, f32[128,16,16]{0,2,1:T(8,128)S(1)} %bitcast.168, f32[153]{0:T(256)S(1)} %copy-done.26, f32[128]{0:T(128)S(1)} %copy-done.36), kind=kOutput, calls=%fused_computation.42 | convolution fusion | flops 482236416 | bytes 3605604 | tf_op jit(solution)/shard_map/transpose(jvp(thf,thd->hfd))/dot_general | solution.py:138
  213.6 4.2 %all-to-all-start = ((f32[128,8,320]{0,2,1:T(8,128)}), f32[128,8,320]{0,2,1:T(8,128)S(1)}, u32[]{:S(2)}, u32[]{:S(2)}) async-start(f32[128,8,320]{0,2,1:T(8,128)} %convert.2), calls=%async_computation | async-start | bytes 2621440 | tf_op jit(solution)/shard_map/all_to_all | solution.py:208
  217.9 18.1 %all-to-all-done = f32[128,8,320]{0,2,1:T(8,128)S(1)} async-done(((f32[128,8,320]{0,2,1:T(8,128)}), f32[128,8,320]{0,2,1:T(8,128)S(1)}, u32[]{:S(2)}, u32[]{:S(2)}) %all-to-all-start) | async-done | bytes 1310752 | tf_op jit(solution)/shard_map/all_to_all | solution.py:208
  236.0 5.7 %convolution_bitcast_fusion = f32[1024,320]{0,1:T(8,128)} fusion(f32[1024,1024]{1,0:T(8,128)} %all-gather.3.cloned.1.call-done, f32[128,8,320]{0,2,1:T(8,128)S(1)} %all-to-all-done), kind=kOutput, calls=%fused_computation.17 | convolution fusion | flops 2013265920 | bytes 6815744 | tf_op jit(solution)/shard_map/dot_general | solution.py:213
  241.7 4.6 %fusion.10 = f32[1024,320]{0,1:T(8,128)S(1)} fusion(f32[1024,1024]{1,0:T(8,128)} %all-gather.5.cloned.1.call-done, f32[128,8,320]{0,2,1:T(8,128)S(1)} %all-to-all-done), kind=kOutput, calls=%fused_computation.30 | convolution fusion | flops 2013265920 | bytes 6815744 | tf_op jit(solution)/shard_map/dot_general | solution.py:213
  250.0 49.6 %reduce-scatter.2.cloned.1.call-done = f32[512,320]{0,1:T(8,128)} async-done(((f32[2048,320]{0,1:T(8,128)}), f32[512,320]{0,1:T(8,128)}) %reduce-scatter.2.cloned.1.call-update) | async-done | bytes 655376 | tf_op jit(solution)/shard_map/reduce_scatter | solution.py:224
  299.6 2.3 copy.70
  301.9 3.7 %all-to-all-start.1 = ((f32[8,64,320]{2,1,0:T(8,128)}), f32[8,64,320]{2,1,0:T(8,128)S(1)}, u32[]{:S(2)}, u32[]{:S(2)}) async-start(f32[8,64,320]{2,1,0:T(8,128)} %bitcast.184), calls=%async_computation.2 | async-start | bytes 1572864 | tf_op jit(solution)/shard_map/all_to_all | solution.py:225
  305.6 6.3 %fusion.48 = f32[128,2048]{1,0:T(8,128)S(1)} fusion(bf16[2048,2048]{1,0:T(8,128)(2,1)} %param.10, bf16[128,2560]{0,1:T(8,128)(2,1)S(1)} %add_convert_fusion), kind=kOutput, calls=%fused_computation.77 | convolution fusion | flops 1073741824 | bytes 9961472 | tf_op jit(solution)/shard_map/dot_general | solution.py:200
  314.4 3.8 %all-to-all-done.1 = f32[8,64,320]{2,1,0:T(8,128)S(1)} async-done(((f32[8,64,320]{2,1,0:T(8,128)}), f32[8,64,320]{2,1,0:T(8,128)S(1)}, u32[]{:S(2)}, u32[]{:S(2)}) %all-to-all-start.1) | async-done | bytes 655392 | tf_op jit(solution)/shard_map/all_to_all | solution.py:225
  (168 shorter events, 51.9 us)
Async XLA Ops:
  7.2 10.7 %copy-start = (bf16[2048,256]{1,0:T(8,128)(2,1)S(1)}, bf16[2048,256]{1,0:T(8,128)(2,1)}, u32[]{:S(2)}) copy-start(bf16[2048,256]{1,0:T(8,128)(2,1)} %param.8) | copy-start | bytes 3145732
  7.2 210.7 %all-gather.3.cloned.1.call-start = ((), (), s32[]{:S(2)}) async-start(), calls=%async_computation.3 | async-start | bytes 4718592 | tf_op jit(solution)/shard_map/all_gather | solution.py:172
  9.2 8.3 %copy-start.1 = (bf16[1,128,2048]{2,1,0:T(8,128)(2,1)S(1)}, bf16[1,128,2048]{2,1,0:T(8,128)(2,1)}, u32[]{:S(2)}) copy-start(bf16[1,128,2048]{2,1,0:T(8,128)(2,1)} %param.7) | copy-start | bytes 1572868
  9.2 8.3 %copy-start.15 = (bf16[2048,256]{1,0:T(8,128)(2,1)S(1)}, bf16[2048,256]{1,0:T(8,128)(2,1)}, u32[]{:S(2)}) copy-start(bf16[2048,256]{1,0:T(8,128)(2,1)} %param.9) | copy-start | bytes 3145732
  9.2 12.4 %collective-permute-start = (s32[1]{0:T(128)}, s32[1]{0:T(128)}, u32[]{:S(2)}, u32[]{:S(2)}) collective-permute-start(s32[1]{0:T(128)} %bitcast.4), channel_id=1, source_target_pairs={{0,1},{1,2},{2,3},{3,4},{4,5},{5,6},{6,7},{8,9},{9,10},{10,11},{11... | collective-permute-start | bytes 20 | tf_op jit(solution)/shard_map/ppermute | solution.py:37
  19.7 78.1 %copy-start.25 = (f32[153]{0:T(256)}, f32[153]{0:T(256)S(1)}, u32[]{:S(2)}) copy-start(f32[153]{0:T(256)S(1)} %pad.42.clone) | copy-start | bytes 1840
  20.1 14.4 %copy-start.27 = (f32[160]{0:T(256)}, f32[160]{0:T(256)S(1)}, u32[]{:S(2)}) copy-start(f32[160]{0:T(256)S(1)} %pad.41.clone) | copy-start | bytes 1924
  22.8 75.0 %copy-start.37 = (f32[128]{0:T(128)}, f32[128]{0:T(128)S(1)}, u32[]{:S(2)}) copy-start(f32[128]{0:T(128)S(1)} %get-tuple-element.30) | copy-start | bytes 1540
  26.0 8.6 %copy-start.29 = (f32[160]{0:T(256)}, f32[160]{0:T(256)S(1)}, u32[]{:S(2)}) copy-start(f32[160]{0:T(256)S(1)} %pad.40.clone) | copy-start | bytes 1924
  27.3 7.3 %collective-permute-start.1 = (f32[16,160,128]{2,1,0:T(8,128)}, f32[16,160,128]{2,1,0:T(8,128)}, u32[]{:S(2)}, u32[]{:S(2)}) collective-permute-start(f32[16,160,128]{2,1,0:T(8,128)} %maximum_maximum_fusion), channel_id=1, source_target_pairs={{0,1},{2,3},{4,5},{6,7},{8,9},{10,11},{12,13},{14,15},{16,17},{18,... | collective-permute-start | bytes 3932168 | tf_op jit(solution)/shard_map/ppermute | solution.py:69
  32.6 6.2 %copy-start.2 = (bf16[1,128,2048]{2,1,0:T(8,128)(2,1)S(1)}, bf16[1,128,2048]{2,1,0:T(8,128)(2,1)}, u32[]{:S(2)}) copy-start(bf16[1,128,2048]{2,1,0:T(8,128)(2,1)} %param.7) | copy-start | bytes 1572868
  36.2 0.8 collective-permute-start.2
  37.0 4.2 %collective-permute-start.3 = (f32[16,160,128]{2,1,0:T(8,128)S(1)}, f32[16,160,128]{2,1,0:T(8,128)}, u32[]{:S(2)}, u32[]{:S(2)}) collective-permute-start(f32[16,160,128]{2,1,0:T(8,128)S(1)} %collective-permute-done.2), channel_id=1, source_target_pairs={{1,3},{3,5},{5,7},{9,11},{11,13},{13,15},{17,19},{19,21},{21,23},{... | collective-permute-start | bytes 3932168 | tf_op jit(solution)/shard_map/ppermute | solution.py:67
  40.0 201.7 %all-gather.5.cloned.1.call-start = ((), (), s32[]{:S(2)}) async-start(), calls=%async_computation.4 | async-start | bytes 4718592 | tf_op jit(solution)/shard_map/all_gather | solution.py:176
  43.7 5.0 %copy-start.5 = (f32[128,256]{0,1:T(8,128)S(1)}, f32[128,256]{0,1:T(8,128)}, u32[]{:S(2)}) copy-start(f32[128,256]{0,1:T(8,128)} %copy-done.3) | copy-start | bytes 393220
  43.7 41.3 %collective-permute-start.4 = (f32[16,160,128]{2,1,0:T(8,128)}, f32[16,160,128]{2,1,0:T(8,128)}, u32[]{:S(2)}, u32[]{:S(2)}) collective-permute-start(f32[16,160,128]{2,1,0:T(8,128)} %add_select_fusion.4), channel_id=1, source_target_pairs={{1,0},{3,2},{5,4},{7,6},{9,8},{11,10},{13,12},{15,14},{17,16},{19,... | collective-permute-start | bytes 3932168 | tf_op jit(solution)/shard_map/ppermute | solution.py:78
  114.1 3.7 %copy-start.28 = (f32[160]{0:T(256)S(1)}, f32[160]{0:T(256)}, u32[]{:S(2)}) copy-start(f32[160]{0:T(256)} %copy-done.27) | copy-start | bytes 1924
  114.2 3.7 %copy-start.30 = (f32[160]{0:T(256)S(1)}, f32[160]{0:T(256)}, u32[]{:S(2)}) copy-start(f32[160]{0:T(256)} %copy-done.29) | copy-start | bytes 1924
  118.1 40.2 %copy-start.24 = (f32[128,16]{0,1:T(8,128)S(1)}, f32[128,16]{0,1:T(8,128)}, u32[]{:S(2)}) copy-start(f32[128,16]{0,1:T(8,128)} %copy-done.23) | copy-start | bytes 24580
  118.1 40.2 %copy-start.21 = (f32[1,128,2048]{1,2,0:T(8,128)S(1)}, f32[1,128,2048]{1,2,0:T(8,128)}, u32[]{:S(2)}) copy-start(f32[1,128,2048]{1,2,0:T(8,128)} %copy.59) | copy-start | bytes 3145732
  118.1 40.2 %copy-start.34 = (f32[2,8,2,128]{3,1,2,0:T(8,128)S(1)}, f32[2,8,2,128]{3,1,2,0:T(8,128)}, u32[]{:S(2)}) copy-start(f32[2,8,2,128]{3,1,2,0:T(8,128)} %copy.123) | copy-start | bytes 49156
  118.1 40.2 %copy-start.38 = (f32[128]{0:T(128)S(1)}, f32[128]{0:T(128)}, u32[]{:S(2)}) copy-start(f32[128]{0:T(128)} %copy-done.37) | copy-start | bytes 1540
  118.1 40.2 %copy-start.40 = (f32[16,128]{1,0:T(8,128)S(1)}, f32[16,128]{1,0:T(8,128)}, u32[]{:S(2)}) copy-start(f32[16,128]{1,0:T(8,128)} %copy-done.39) | copy-start | bytes 24580
  118.1 40.2 %copy-start.42 = (f32[128,16]{0,1:T(8,128)S(1)}, f32[128,16]{0,1:T(8,128)}, u32[]{:S(2)}) copy-start(f32[128,16]{0,1:T(8,128)} %copy-done.41) | copy-start | bytes 24580
  118.2 12.5 %collective-permute-start.5 = (f32[16,160,128]{2,1,0:T(8,128)S(1)}, f32[16,160,128]{2,1,0:T(8,128)S(1)}, u32[]{:S(2)}, u32[]{:S(2)}) collective-permute-start(f32[16,160,128]{2,1,0:T(8,128)S(1)} %maximum_maximum_fusion.1), channel_id=1, source_target_pairs={{1,0},{3,2},{5,4},{7,6},{9,8},{11,10},{13,12},{15,14},{17,16},{19,... | collective-permute-start | bytes 3932168 | tf_op jit(solution)/shard_map/ppermute | solution.py:69
  132.1 24.9 %collective-permute-start.6 = (f32[16,160,128]{2,1,0:T(8,128)}, f32[16,160,128]{2,1,0:T(8,128)}, u32[]{:S(2)}, u32[]{:S(2)}) collective-permute-start(f32[16,160,128]{2,1,0:T(8,128)} %add_select_fusion.2), channel_id=1, source_target_pairs={{2,0},{4,2},{6,4},{10,8},{12,10},{14,12},{18,16},{20,18},{22,20},{... | collective-permute-start | bytes 3932168 | tf_op jit(solution)/shard_map/ppermute | solution.py:67
  157.0 33.2 %collective-permute-start.7 = (f32[16,160,128]{2,1,0:T(8,128)}, f32[16,160,128]{2,1,0:T(8,128)}, u32[]{:S(2)}, u32[]{:S(2)}) collective-permute-start(f32[16,160,128]{2,1,0:T(8,128)} %collective-permute-done.6), channel_id=1, source_target_pairs={{2,0},{4,2},{6,4},{10,8},{12,10},{14,12},{18,16},{20,18},{22,20},{... | collective-permute-start | bytes 3932168 | tf_op jit(solution)/shard_map/ppermute | solution.py:67
  192.0 10.6 %collective-permute-start.8 = (f32[16,160,128]{2,1,0:T(8,128)S(1)}, f32[16,160,128]{2,1,0:T(8,128)S(1)}, u32[]{:S(2)}, u32[]{:S(2)}) collective-permute-start(f32[16,160,128]{2,1,0:T(8,128)S(1)} %add_select_fusion.1), channel_id=1, source_target_pairs={{0,1},{2,3},{4,5},{6,7},{8,9},{10,11},{12,13},{14,15},{16,17},{18,... | collective-permute-start | bytes 3932168 | tf_op jit(solution)/shard_map/ppermute | solution.py:78
  213.6 22.4 %all-to-all-start = ((f32[128,8,320]{0,2,1:T(8,128)}), f32[128,8,320]{0,2,1:T(8,128)S(1)}, u32[]{:S(2)}, u32[]{:S(2)}) async-start(f32[128,8,320]{0,2,1:T(8,128)} %convert.2), calls=%async_computation | async-start | bytes 2621440 | tf_op jit(solution)/shard_map/all_to_all | solution.py:208
  217.8 81.8 %reduce-scatter.2.cloned.1.call-start = ((), (), s32[]{:S(2)}) async-start(), calls=%async_computation.5 | async-start | bytes 3276800 | tf_op jit(solution)/shard_map/reduce_scatter | solution.py:224
  241.7 4.6 %copy-start.12 = (f32[1024,320]{0,1:T(8,128)S(1)}, f32[1024,320]{0,1:T(8,128)}, u32[]{:S(2)}) copy-start(f32[1024,320]{0,1:T(8,128)} %convolution_bitcast_fusion) | copy-start | bytes 3932164
  301.9 16.3 %all-to-all-start.1 = ((f32[8,64,320]{2,1,0:T(8,128)}), f32[8,64,320]{2,1,0:T(8,128)S(1)}, u32[]{:S(2)}, u32[]{:S(2)}) async-start(f32[8,64,320]{2,1,0:T(8,128)} %bitcast.184), calls=%async_computation.2 | async-start | bytes 1572864 | tf_op jit(solution)/shard_map/all_to_all | solution.py:225
  (28 other events, 61.3 us)
Sparse Core Ops, SparseCore 0:
  40.1 59.4 all-gather.2
  133.6 52.3 all-gather.4
  248.1 51.4 reduce-scatter.1

commit v6 on v4

--- a/solution.py
+++ b/solution.py
@@ -209,7 +209,16 @@
         precision=lax.Precision.HIGH,
         preferred_element_type=jnp.float32,
     )
-    row_part = lax.psum_scatter(pack_part, "dp", scatter_dimension=0, tiled=True)
+    planes = lax.axis_size("dp")
+    row_part = jnp.sum(
+        lax.all_to_all(
+            pack_part.reshape((planes, pack_part.shape[0] // planes) + pack_part.shape[1:]),
+            "dp",
+            0,
+            0,
+        ),
+        axis=0,
+    )
     grad_proj = lax.all_to_all(row_part, "seq", split_axis=0, concat_axis=1, tiled=True)
     return (output.astype(jnp.bfloat16)[None], grad_input[None], grad_proj)
 

time: 326 us -> 339 us (1.040)
  waiting for transfers between devices: 147 us -> 154 us
  starting transfers between devices: 23 us -> 29.2 us
    all_to_all x0 -> x1, waiting for transfers between devices: none -> 57.9 us  [on_device(): lax.all_to_all(pack_part.reshape((planes, pack_part.shape[0] // planes) +...]
    reduce_scatter x1 -> x0, waiting for transfers between devices: 51 us -> none  [on_device(): lax.psum_scatter(pack_part, 'dp', scatter_dimension=0, tiled=True)]
    all_to_all x0 -> x1, starting transfers between devices: none -> 6.29 us  [on_device(): lax.all_to_all(pack_part.reshape((planes, pack_part.shape[0] // planes) +...]
  transfers between devices with their start and end apart: 12 -> 12, of which waited for: 7 -> 7; matrix products, arithmetic and copies ran while one was open for 26% -> 25% of each run, Pallas kernels for 0% -> 0%
where the time goes in v6:
time: 339 us; the launch traced here: 338 us
  waiting for transfers between devices  154 us (45%)
  matrix products  74.5 us (22%)
  starting transfers between devices  29.2 us (9%)
  blocking collectives  22.2 us (7%)
  other arithmetic  20.9 us (6%)
  between operations  19.6 us (6%)
  local copies, waits for them, and re-layouts  18.5 us (5%)
    all_to_all x1, waiting for transfers between devices, on_device(): lax.all_to_all(pack_part.reshape((planes, pack_part.shape[0] // planes) +...  57.9 us
    ppermute x2, waiting for transfers between devices, chip_scan(): lax.ppermute(carry, 'seq', [(2 * chip + lead, 2 * chip + other) for chip...  50.8 us
    ppermute x4, waiting for transfers between devices, chip_shift(): return lax.ppermute(value, 'seq', pairs)  31.4 us
    dot_general x3, matrix products, block_forward(): jnp.einsum('thf,hfd->thd', phi_query, state_in, precision=highest)  24.9 us
    all_to_all x1, blocking collectives, on_device(): lax.all_to_all(grad_projected.astype(jnp.float32), 'seq', split_axis=1, c...  22.2 us
    ppermute x2, waiting for transfers between devices, chip_scan(): lax.ppermute(packed, 'seq', [(2 * chip + other, 2 * chip + lead) for chip...  9.75 us
    dot_general x3, matrix products, block_summary(): state_sum = jnp.einsum('thf,thd->hfd', weighted, values, precision=highest)  8.67 us
    dot_general x3, matrix products, on_device(): lax.dot_general(grad_projected[:, start:stop], part, (((1,), (1,)), ((),...  8.07 us
  transfers between devices with their start and end apart: 12, of which 7 were waited for; matrix products, arithmetic and copies ran while one was open for 25% of the time, Pallas kernels for 0%

profile of v6, /device:TPU:0, one launch (start us, length us, event | category | flops | bytes accessed | tf_op | source)
XLA Modules:
  0.0 338.4 jit_solution(13504858964472175484)
XLA Ops:
  9.2 3.3 collective-permute-start
  12.5 4.8 %fusion.50 = f32[128,2048]{1,0:T(8,128)S(1)} fusion(bf16[2048,2048]{1,0:T(8,128)(2,1)} %param.10, bf16[1,128,2048]{2,1,0:T(8,128)(2,1)} %param.7), kind=kOutput, calls=%fused_computation.78 | convolution fusion | flops 1073741824 | bytes 9961472 | tf_op jit(solution)/shard_map/dot_general | solution.py:152
  23.8 2.6 fusion.30
  27.2 2.6 maximum_maximum_fusion
  29.8 5.5 %collective-permute-start.1 = (f32[16,160,128]{2,1,0:T(8,128)}, f32[16,160,128]{2,1,0:T(8,128)}, u32[]{:S(2)}, u32[]{:S(2)}) collective-permute-start(f32[16,160,128]{2,1,0:T(8,128)} %maximum_maximum_fusion), channel_id=1, source_target_pairs={{0,1},{2,3},{4,5},{6,7},{8,9},{10,11},{12,13},{14,15},{16,17},{18,... | collective-permute-start | bytes 3932168 | tf_op jit(solution)/shard_map/ppermute | solution.py:69
  35.3 1.9 collective-permute-done.1
  37.2 3.1 add_select_fusion.5
  44.9 2.2 copy.77
  50.7 2.2 add_select_fusion.4
  56.8 2.0 fusion.26
  62.0 50.8 %collective-permute-done.4 = f32[16,160,128]{2,1,0:T(8,128)S(1)} collective-permute-done((f32[16,160,128]{2,1,0:T(8,128)S(1)}, f32[16,160,128]{2,1,0:T(8,128)S(1)}, u32[]{:S(2)}, u32[]{:S(2)}) %collective-permute-start.4) | collective-permute-done | bytes 1310752 | tf_op jit(solution)/shard_map/ppermute | solution.py:78
  116.0 5.1 %multiply_reduce_fusion.4 = (f32[128,16]{0,1:T(8,128)S(1)}, bf16[128,16,128]{0,2,1:T(8,128)(2,1)}) fusion(f32[128,16,128]{0,2,1:T(8,128)S(1)} %bitcast.176, f32[128,16]{0,1:T(8,128)S(1)} %get-tuple-element.19, f32[128,16]{0,1:T(8,128)S(1)} %get-tuple-element.20, f32[16,128,128]{2,1,0:T(8,128)S(1)} %fusion.26, f32[128,16,136]{0,2,1:T(8,128)S(1)} %fusion.82, ...), kind=kOutput, calls=%fused_computation.65 | convolution fusion | flops 483756032 | bytes 5203044 | tf_op jit(solution)/shard_map/jvp(thf,hfd->thd)/dot_general | solution.py:122
  121.8 2.3 fusion.79
  124.1 16.4 %fusion.32 = f32[16,153,128]{2,1,0:T(8,128)S(1)} fusion(f32[128]{0:T(128)} %get-tuple-element.27, f32[128,16,136]{0,2,1:T(8,128)} %copy-done.17, f32[128,16,16]{0,2,1:T(8,128)} %bitcast.162, f32[153]{0:T(256)} %copy-done.23, f32[128,16,128]{0,2,1:T(8,128)} %bitcast.174, f32[128,16]{0,1:T(8,128)} %copy-done.30), kind=kOutput, calls=%fused_computation.59 | convolution fusion | flops 482447360 | bytes 3556452 | tf_op jit(solution)/shard_map/transpose(jvp(thf,hfd->thd))/dot_general | solution.py:122
  142.1 7.9 %collective-permute-done.5 = f32[16,160,128]{2,1,0:T(8,128)S(1)} collective-permute-done((f32[16,160,128]{2,1,0:T(8,128)S(1)}, f32[16,160,128]{2,1,0:T(8,128)S(1)}, u32[]{:S(2)}, u32[]{:S(2)}) %collective-permute-start.5) | collective-permute-done | bytes 1310752 | tf_op jit(solution)/shard_map/ppermute | solution.py:69
  152.4 18.8 %collective-permute-done.6 = f32[16,160,128]{2,1,0:T(8,128)} collective-permute-done((f32[16,160,128]{2,1,0:T(8,128)S(1)}, f32[16,160,128]{2,1,0:T(8,128)}, u32[]{:S(2)}, u32[]{:S(2)}) %collective-permute-start.6) | collective-permute-done | bytes 1310752 | tf_op jit(solution)/shard_map/ppermute | solution.py:67
  172.6 3.3 fusion.4
  179.3 12.6 %collective-permute-done.7 = f32[16,160,128]{2,1,0:T(8,128)} collective-permute-done((f32[16,160,128]{2,1,0:T(8,128)}, f32[16,160,128]{2,1,0:T(8,128)}, u32[]{:S(2)}, u32[]{:S(2)}) %collective-permute-start.7) | collective-permute-done | bytes 1310752 | tf_op jit(solution)/shard_map/ppermute | solution.py:67
  191.9 1.9 add_select_fusion.1
  197.1 1.9 fusion.21
  200.9 2.3 fusion.36
  205.0 2.3 fusion.5
  207.3 1.9 fusion.19
  210.2 3.8 %fusion.15 = f32[16,128,128]{2,1,0:T(8,128)S(1)} fusion(f32[16,160,128]{2,1,0:T(8,128)S(1)} %fusion.10, f32[128,16,136]{0,2,1:T(8,128)S(1)} %fusion.81, f32[128,16,16]{0,2,1:T(8,128)S(1)} %bitcast.157, f32[153]{0:T(256)S(1)} %copy-done.25, f32[128]{0:T(128)S(1)} %copy-done.27), kind=kOutput, calls=%fused_computation.39 | convolution fusion | flops 482236416 | bytes 3605604 | tf_op jit(solution)/shard_map/transpose(jvp(thf,thd->hfd))/dot_general | solution.py:138
  214.2 22.2 %all_to_all.47 = f32[128,8,320]{0,2,1:T(8,128)S(1)} all-to-all(f32[128,8,320]{0,2,1:T(8,128)S(1)} %convert.2), channel_id=1, replica_groups=mesh['dp'=4,'seq'=8] {'seq'}, dimensions={1} | all-to-all | bytes 2621440 | tf_op jit(solution)/shard_map/all_to_all | solution.py:202
  236.3 7.1 %fusion.11 = f32[320,2048]{1,0:T(8,128)S(1)} fusion(f32[1024,2048]{1,0:T(8,128)} %all-gather.2.cloned.1.call-done, f32[128,8,320]{0,2,1:T(8,128)S(1)} %all_to_all.47), kind=kOutput, calls=%fused_computation.29 | convolution fusion | flops 4026531840 | bytes 12320768 | tf_op jit(solution)/shard_map/dot_general | solution.py:205
  245.3 6.3 %all-to-all-start.1 = ((f32[4,512,320]{1,2,0:T(8,128)}), f32[4,512,320]{1,2,0:T(8,128)}, u32[]{:S(2)}, u32[]{:S(2)}) async-start(f32[4,512,320]{1,2,0:T(8,128)} %bitcast.158), calls=%async_computation.1 | async-start | bytes 5242880 | tf_op jit(solution)/shard_map/all_to_all | solution.py:214
  252.6 57.9 %all-to-all-done.1 = f32[4,512,320]{1,2,0:T(8,128)} async-done(((f32[4,512,320]{1,2,0:T(8,128)}), f32[4,512,320]{1,2,0:T(8,128)}, u32[]{:S(2)}, u32[]{:S(2)}) %all-to-all-start.1) | async-done | bytes 2621472 | tf_op jit(solution)/shard_map/all_to_all | solution.py:214
  310.5 2.1 reduce_sum.83
  313.7 3.5 %all-to-all-start.2 = ((f32[8,64,320]{2,1,0:T(8,128)}), f32[8,64,320]{2,1,0:T(8,128)S(1)}, u32[]{:S(2)}, u32[]{:S(2)}) async-start(f32[8,64,320]{2,1,0:T(8,128)} %bitcast.172), calls=%async_computation.2 | async-start | bytes 1572864 | tf_op jit(solution)/shard_map/all_to_all | solution.py:222
  317.3 6.3 %fusion.48 = f32[128,2048]{1,0:T(8,128)S(1)} fusion(bf16[2048,2048]{1,0:T(8,128)(2,1)} %param.10, bf16[128,2560]{0,1:T(8,128)(2,1)S(1)} %add_convert_fusion), kind=kOutput, calls=%fused_computation.75 | convolution fusion | flops 1073741824 | bytes 9961472 | tf_op jit(solution)/shard_map/dot_general | solution.py:194
  326.1 3.7 %all-to-all-done.2 = f32[8,64,320]{2,1,0:T(8,128)S(1)} async-done(((f32[8,64,320]{2,1,0:T(8,128)}), f32[8,64,320]{2,1,0:T(8,128)S(1)}, u32[]{:S(2)}, u32[]{:S(2)}) %all-to-all-start.2) | async-done | bytes 655392 | tf_op jit(solution)/shard_map/all_to_all | solution.py:222
  (139 shorter events, 48.2 us)
Async XLA Ops:
  7.2 10.5 %copy-start = (bf16[2048,256]{1,0:T(8,128)(2,1)S(1)}, bf16[2048,256]{1,0:T(8,128)(2,1)}, u32[]{:S(2)}) copy-start(bf16[2048,256]{1,0:T(8,128)(2,1)} %param.8) | copy-start | bytes 3145732
  7.2 229.2 %all-gather.2.cloned.1.call-start = ((), (), s32[]{:S(2)}) async-start(), calls=%async_computation.3 | async-start | bytes 9437184 | tf_op jit(solution)/shard_map/all_gather | solution.py:170
  9.2 8.2 %copy-start.1 = (bf16[1,128,2048]{2,1,0:T(8,128)(2,1)S(1)}, bf16[1,128,2048]{2,1,0:T(8,128)(2,1)}, u32[]{:S(2)}) copy-start(bf16[1,128,2048]{2,1,0:T(8,128)(2,1)} %param.7) | copy-start | bytes 1572868
  9.2 8.2 %copy-start.11 = (bf16[2048,256]{1,0:T(8,128)(2,1)S(1)}, bf16[2048,256]{1,0:T(8,128)(2,1)}, u32[]{:S(2)}) copy-start(bf16[2048,256]{1,0:T(8,128)(2,1)} %param.9) | copy-start | bytes 3145732
  9.2 12.0 %collective-permute-start = (s32[1]{0:T(128)}, s32[1]{0:T(128)}, u32[]{:S(2)}, u32[]{:S(2)}) collective-permute-start(s32[1]{0:T(128)} %bitcast.4), channel_id=1, source_target_pairs={{0,1},{1,2},{2,3},{3,4},{4,5},{5,6},{6,7},{8,9},{9,10},{10,11},{11... | collective-permute-start | bytes 20 | tf_op jit(solution)/shard_map/ppermute | solution.py:37
  19.1 95.3 %copy-start.23 = (f32[153]{0:T(256)}, f32[153]{0:T(256)S(1)}, u32[]{:S(2)}) copy-start(f32[153]{0:T(256)S(1)} %pad.40.clone) | copy-start | bytes 1840
  19.9 3.2 copy-start.4
  23.1 3.4 copy-start.26
  29.8 7.4 %collective-permute-start.1 = (f32[16,160,128]{2,1,0:T(8,128)}, f32[16,160,128]{2,1,0:T(8,128)}, u32[]{:S(2)}, u32[]{:S(2)}) collective-permute-start(f32[16,160,128]{2,1,0:T(8,128)} %maximum_maximum_fusion), channel_id=1, source_target_pairs={{0,1},{2,3},{4,5},{6,7},{8,9},{10,11},{12,13},{14,15},{16,17},{18,... | collective-permute-start | bytes 3932168 | tf_op jit(solution)/shard_map/ppermute | solution.py:69
  35.3 6.7 %copy-start.2 = (bf16[1,128,2048]{2,1,0:T(8,128)(2,1)S(1)}, bf16[1,128,2048]{2,1,0:T(8,128)(2,1)}, u32[]{:S(2)}) copy-start(bf16[1,128,2048]{2,1,0:T(8,128)(2,1)} %param.7) | copy-start | bytes 1572868
  40.4 2.8 collective-permute-start.2
  43.2 7.5 %collective-permute-start.3 = (f32[16,160,128]{2,1,0:T(8,128)}, f32[16,160,128]{2,1,0:T(8,128)}, u32[]{:S(2)}, u32[]{:S(2)}) collective-permute-start(f32[16,160,128]{2,1,0:T(8,128)} %collective-permute-done.2), channel_id=1, source_target_pairs={{1,3},{3,5},{5,7},{9,11},{11,13},{13,15},{17,19},{19,21},{21,23},{... | collective-permute-start | bytes 3932168 | tf_op jit(solution)/shard_map/ppermute | solution.py:67
  50.7 4.0 %copy-start.5 = (f32[128,256]{0,1:T(8,128)S(1)}, f32[128,256]{0,1:T(8,128)}, u32[]{:S(2)}) copy-start(f32[128,256]{0,1:T(8,128)} %copy-done.3) | copy-start | bytes 393220
  50.7 4.0 %copy-start.9 = (f32[128,256]{0,1:T(8,128)S(1)}, f32[128,256]{0,1:T(8,128)}, u32[]{:S(2)}) copy-start(f32[128,256]{0,1:T(8,128)} %copy.70) | copy-start | bytes 393220
  52.9 59.8 %collective-permute-start.4 = (f32[16,160,128]{2,1,0:T(8,128)S(1)}, f32[16,160,128]{2,1,0:T(8,128)S(1)}, u32[]{:S(2)}, u32[]{:S(2)}) collective-permute-start(f32[16,160,128]{2,1,0:T(8,128)S(1)} %add_select_fusion.4), channel_id=1, source_target_pairs={{1,0},{3,2},{5,4},{7,6},{9,8},{11,10},{13,12},{15,14},{17,16},{19,... | collective-permute-start | bytes 3932168 | tf_op jit(solution)/shard_map/ppermute | solution.py:78
  60.1 61.1 %copy-start.17 = (f32[128,16,136]{0,2,1:T(8,128)}, f32[128,16,136]{0,2,1:T(8,128)S(1)}, u32[]{:S(2)}) copy-start(f32[128,16,136]{0,2,1:T(8,128)S(1)} %fusion.82) | copy-start | bytes 3342340
  114.3 6.9 %copy-start.16 = (f32[16,160,128]{2,1,0:T(8,128)}, f32[16,160,128]{2,1,0:T(8,128)S(1)}, u32[]{:S(2)}) copy-start(f32[16,160,128]{2,1,0:T(8,128)S(1)} %fusion.9) | copy-start | bytes 3932164
  115.7 5.5 %copy-start.30 = (f32[128,16]{0,1:T(8,128)}, f32[128,16]{0,1:T(8,128)S(1)}, u32[]{:S(2)}) copy-start(f32[128,16]{0,1:T(8,128)S(1)} %get-tuple-element.20) | copy-start | bytes 24580
  116.0 5.7 %copy-start.24 = (f32[153]{0:T(256)S(1)}, f32[153]{0:T(256)}, u32[]{:S(2)}) copy-start(f32[153]{0:T(256)} %copy-done.23) | copy-start | bytes 1840
  140.8 31.7 %copy-start.29 = (f32[16,128]{1,0:T(8,128)S(1)}, f32[16,128]{1,0:T(8,128)}, u32[]{:S(2)}) copy-start(f32[16,128]{1,0:T(8,128)} %copy-done.28) | copy-start | bytes 24580
  140.8 9.2 %collective-permute-start.5 = (f32[16,160,128]{2,1,0:T(8,128)S(1)}, f32[16,160,128]{2,1,0:T(8,128)S(1)}, u32[]{:S(2)}, u32[]{:S(2)}) collective-permute-start(f32[16,160,128]{2,1,0:T(8,128)S(1)} %maximum_maximum_fusion.1), channel_id=1, source_target_pairs={{1,0},{3,2},{5,4},{7,6},{9,8},{11,10},{13,12},{15,14},{17,16},{19,... | collective-permute-start | bytes 3932168 | tf_op jit(solution)/shard_map/ppermute | solution.py:69
  151.1 20.1 %collective-permute-start.6 = (f32[16,160,128]{2,1,0:T(8,128)S(1)}, f32[16,160,128]{2,1,0:T(8,128)}, u32[]{:S(2)}, u32[]{:S(2)}) collective-permute-start(f32[16,160,128]{2,1,0:T(8,128)S(1)} %add_select_fusion.2), channel_id=1, source_target_pairs={{2,0},{4,2},{6,4},{10,8},{12,10},{14,12},{18,16},{20,18},{22,20},{... | collective-permute-start | bytes 3932168 | tf_op jit(solution)/shard_map/ppermute | solution.py:67
  171.2 20.7 %collective-permute-start.7 = (f32[16,160,128]{2,1,0:T(8,128)}, f32[16,160,128]{2,1,0:T(8,128)}, u32[]{:S(2)}, u32[]{:S(2)}) collective-permute-start(f32[16,160,128]{2,1,0:T(8,128)} %collective-permute-done.6), channel_id=1, source_target_pairs={{2,0},{4,2},{6,4},{10,8},{12,10},{14,12},{18,16},{20,18},{22,20},{... | collective-permute-start | bytes 3932168 | tf_op jit(solution)/shard_map/ppermute | solution.py:67
  172.5 3.3 copy-start.19
  172.5 3.3 copy-start.21
  172.5 3.3 copy-start.31
  191.9 3.4 %copy-start.10 = (f32[128,256]{0,1:T(8,128)S(1)}, f32[128,256]{0,1:T(8,128)}, u32[]{:S(2)}) copy-start(f32[128,256]{0,1:T(8,128)} %copy.70) | copy-start | bytes 393220
  193.8 3.3 copy-start.15
  193.8 10.6 %collective-permute-start.8 = (f32[16,160,128]{2,1,0:T(8,128)S(1)}, f32[16,160,128]{2,1,0:T(8,128)S(1)}, u32[]{:S(2)}, u32[]{:S(2)}) collective-permute-start(f32[16,160,128]{2,1,0:T(8,128)S(1)} %add_select_fusion.1), channel_id=1, source_target_pairs={{0,1},{2,3},{4,5},{6,7},{8,9},{10,11},{12,13},{14,15},{16,17},{18,... | collective-permute-start | bytes 3932168 | tf_op jit(solution)/shard_map/ppermute | solution.py:78
  245.3 6.3 %copy-start.22 = (bf16[128,16,128]{0,2,1:T(8,128)(2,1)S(1)}, bf16[128,16,128]{0,2,1:T(8,128)(2,1)}, u32[]{:S(2)}) copy-start(bf16[128,16,128]{0,2,1:T(8,128)(2,1)} %get-tuple-element.24) | copy-start | bytes 1572868
  245.3 65.2 %all-to-all-start.1 = ((f32[4,512,320]{1,2,0:T(8,128)}), f32[4,512,320]{1,2,0:T(8,128)}, u32[]{:S(2)}, u32[]{:S(2)}) async-start(f32[4,512,320]{1,2,0:T(8,128)} %bitcast.158), calls=%async_computation.1 | async-start | bytes 5242880 | tf_op jit(solution)/shard_map/all_to_all | solution.py:214
  313.7 16.1 %all-to-all-start.2 = ((f32[8,64,320]{2,1,0:T(8,128)}), f32[8,64,320]{2,1,0:T(8,128)S(1)}, u32[]{:S(2)}, u32[]{:S(2)}) async-start(f32[8,64,320]{2,1,0:T(8,128)} %bitcast.172), calls=%async_computation.2 | async-start | bytes 1572864 | tf_op jit(solution)/shard_map/all_to_all | solution.py:222
  (14 other events, 18.6 us)
Sparse Core Ops, SparseCore 0:
  43.3 70.1 all-gather.1

commit v7 on v4

--- a/solution.py
+++ b/solution.py
@@ -49,10 +49,12 @@
 
 def chip_scan(packed, flag_row, direction, reach):
     count = lax.axis_size("seq")
-    if count % 2:
+    if count % 2 or packed.shape[0] % 2:
         return segmented_scan(packed, flag_row, direction, reach)
-    chips = count // 2
-    lead, other = (1, 0) if direction > 0 else (0, 1)
+    chips, split = (count // 2, packed.shape[0] // 2)
+    lead = 1 if direction > 0 else 0
+    core = lax.axis_index("seq") % 2
+    swap = [(2 * chip + side, 2 * chip + 1 - side) for chip in range(chips) for side in (0, 1)]
 
     def fold(near, far):
         return jnp.where(near[0, flag_row, 0] > 0, near, near + far)
@@ -60,26 +62,28 @@
     def chip_shift(value, distance):
         step = direction * distance
         pairs = [
-            (2 * chip + lead, 2 * (chip + step) + lead)
+            (2 * chip + side, 2 * (chip + step) + side)
             for chip in range(chips)
             if 0 <= chip + step < chips
+            for side in (0, 1)
         ]
         return lax.ppermute(value, "seq", pairs)
 
-    partner = lax.ppermute(
-        packed, "seq", [(2 * chip + other, 2 * chip + lead) for chip in range(chips)]
-    )
-    carry = chip_shift(fold(packed, partner), 1)
+    low, high = (packed[:split], packed[split:])
+    mine = jnp.where(core == 0, low, high)
+    got = lax.ppermute(jnp.where(core == 0, high, low), "seq", swap)
+    summary = jnp.where(core == lead, fold(mine, got), fold(got, mine))
+    carry = chip_shift(summary, 1)
     chip_reach = min(chips - 1, -(-reach // 2))
     covered = 1
     while covered < chip_reach:
         carry = fold(carry, chip_shift(carry, covered))
         covered *= 2
-    handed = lax.ppermute(
-        carry, "seq", [(2 * chip + lead, 2 * chip + other) for chip in range(chips)]
-    )
-    core = lax.axis_index("seq") % 2
-    return jnp.where(core == lead, fold(partner, carry), handed)
+    back = lax.ppermute(jnp.where(core == lead, carry, fold(mine, carry)), "seq", swap)
+    kept = jnp.where(core == lead, fold(got, carry), carry)
+    return jnp.where(
+        core == 0, jnp.concatenate([kept, back], axis=0), jnp.concatenate([back, kept], axis=0)
+    )
 
 
 def taylor_table(feat_width):

time: 326 us -> 307 us (0.942); the launches traced: 325 us -> 301 us
  waiting for transfers between devices: 147 us -> 126 us
  other arithmetic: 18.9 us -> 13.7 us
    ppermute x4, waiting for transfers between devices: 60.4 us -> 1.46 us  [the longest x2 1.46 us: chip_scan(): got = lax.ppermute(jnp.where(core == 0, high, low), 'seq', swap)]
    ppermute x4, waiting for transfers between devices: 31.6 us -> 70.8 us  [chip_shift(): return lax.ppermute(value, 'seq', pairs)]
    dot_general x3, matrix products: 24.9 us -> 8.77 us  [block_forward(): jnp.einsum('thf,hfd->thd', phi_query, state_in, precision=highest)]
    dot_general x2, matrix products: 3.54 us -> 16.2 us  [block_forward(): jnp.einsum('thf,hf->th', phi_query, norm_in, precision=highest)]
    ppermute x4, starting transfers between devices: 9.84 us -> 3.11 us  [the longest x2 3.04 us: chip_scan(): got = lax.ppermute(jnp.where(core == 0, high, low), 'seq', swap)]
    ppermute x4, starting transfers between devices: 6.04 us -> 12.5 us  [chip_shift(): return lax.ppermute(value, 'seq', pairs)]
    select_n x6 -> x8, other arithmetic: 9.54 us -> 6.8 us  [the longest x2 2.95 us: chip_scan(): kept = jnp.where(core == lead, fold(got, carry), carry)]
  transfers between devices with their start and end apart: 12 -> 12, of which waited for: 7 -> 8; matrix products, arithmetic and copies ran while one was open for 26% -> 30% of each run, Pallas kernels for 0% -> 0%
where the time goes in v7:
time: 307 us; the launch traced here: 301 us
  waiting for transfers between devices  126 us (41%)
  matrix products  75.9 us (25%)
  starting transfers between devices  22.6 us (7%)
  blocking collectives  22.1 us (7%)
  between operations  21.2 us (7%)
  local copies, waits for them, and re-layouts  19.5 us (6%)
  other arithmetic  13.7 us (4%)
    ppermute x4, waiting for transfers between devices, chip_shift(): return lax.ppermute(value, 'seq', pairs)  70.8 us
    reduce_scatter x1, waiting for transfers between devices, on_device(): lax.psum_scatter(pack_part, 'dp', scatter_dimension=0, tiled=True)  49.8 us
    all_to_all x1, blocking collectives, on_device(): lax.all_to_all(grad_projected.astype(jnp.float32), 'seq', split_axis=1, c...  22.1 us
    dot_general x2, matrix products, block_forward(): jnp.einsum('thf,hf->th', phi_query, norm_in, precision=highest)  16.2 us
    ppermute x4, starting transfers between devices, chip_shift(): return lax.ppermute(value, 'seq', pairs)  12.5 us
    dot_general x1, matrix products, on_device(): lax.dot_general(tokens_pack, grad_cols, (((0,), (0,)), ((), ())), precisi...  9.95 us
    dot_general x3, matrix products, block_summary(): state_sum = jnp.einsum('thf,thd->hfd', weighted, values, precision=highest)  8.89 us
    dot_general x3, matrix products, block_forward(): jnp.einsum('thf,hfd->thd', phi_query, state_in, precision=highest)  8.77 us
  transfers between devices with their start and end apart: 12, of which 8 were waited for; matrix products, arithmetic and copies ran while one was open for 30% of the time, Pallas kernels for 0%

profile of v7, /device:TPU:0, one launch (start us, length us, event | category | flops | bytes accessed | tf_op | source)
XLA Modules:
  0.0 300.8 jit_solution(6783263667482197292)
XLA Ops:
  9.2 3.3 %collective-permute-start = (s32[1]{0:T(128)}, s32[1]{0:T(128)}, u32[]{:S(2)}, u32[]{:S(2)}) collective-permute-start(s32[1]{0:T(128)} %bitcast.4), channel_id=1, source_target_pairs={{0,1},{1,2},{2,3},{3,4},{4,5},{5,6},{6,7},{8,9},{9,10},{10,11},{11... | collective-permute-start | bytes 20 | tf_op jit(solution)/shard_map/ppermute | solution.py:37
  12.5 2.1 bitcast_convert_fusion
  14.7 4.7 %fusion.51 = f32[128,2048]{1,0:T(8,128)S(1)} fusion(bf16[2048,2048]{1,0:T(8,128)(2,1)} %param.10, bf16[1,128,2048]{2,1,0:T(8,128)(2,1)S(1)} %copy-done.1), kind=kOutput, calls=%fused_computation.90 | convolution fusion | flops 1073741824 | bytes 9961472 | tf_op jit(solution)/shard_map/dot_general | solution.py:156
  26.4 2.8 fusion.25
  30.5 2.5 collective-permute-start.1
  38.1 4.3 %collective-permute-start.2 = (f32[8,160,128]{2,1,0:T(8,128)S(1)}, f32[8,160,128]{2,1,0:T(8,128)}, u32[]{:S(2)}, u32[]{:S(2)}) collective-permute-start(f32[8,160,128]{2,1,0:T(8,128)S(1)} %fusion.47), channel_id=1, source_target_pairs={{0,2},{1,3},{2,4},{3,5},{4,6},{5,7},{8,10},{9,11},{10,12},{11,13},... | collective-permute-start | bytes 1966088 | tf_op jit(solution)/shard_map/ppermute | solution.py:70
  42.3 25.0 %collective-permute-done.2 = f32[8,160,128]{2,1,0:T(8,128)} collective-permute-done((f32[8,160,128]{2,1,0:T(8,128)S(1)}, f32[8,160,128]{2,1,0:T(8,128)}, u32[]{:S(2)}, u32[]{:S(2)}) %collective-permute-start.2) | collective-permute-done | bytes 655392 | tf_op jit(solution)/shard_map/ppermute | solution.py:70
  67.4 5.6 %collective-permute-start.3 = (f32[8,160,128]{2,1,0:T(8,128)}, f32[8,160,128]{2,1,0:T(8,128)}, u32[]{:S(2)}, u32[]{:S(2)}) collective-permute-start(f32[8,160,128]{2,1,0:T(8,128)} %collective-permute-done.2), channel_id=1, source_target_pairs={{0,2},{1,3},{2,4},{3,5},{4,6},{5,7},{8,10},{9,11},{10,12},{11,13},... | collective-permute-start | bytes 1966088 | tf_op jit(solution)/shard_map/ppermute | solution.py:70
  75.1 17.6 %collective-permute-done.3 = f32[8,160,128]{2,1,0:T(8,128)} collective-permute-done((f32[8,160,128]{2,1,0:T(8,128)}, f32[8,160,128]{2,1,0:T(8,128)}, u32[]{:S(2)}, u32[]{:S(2)}) %collective-permute-start.3) | collective-permute-done | bytes 655392 | tf_op jit(solution)/shard_map/ppermute | solution.py:70
  92.6 2.8 fusion.42
  95.4 2.8 fusion.60
  105.2 3.6 %convolution_multiply_fusion = f32[16,128,128]{2,1,0:T(8,128)S(1)} fusion(f32[16,160,128]{2,1,0:T(8,128)S(1)} %maximum_select_fusion, f32[128]{0:T(128)S(1)} %get-tuple-element.32, f32[128,16,136]{0,2,1:T(8,128)S(1)} %fusion.83, f32[128,16,16]{0,2,1:T(8,128)S(1)} %bitcast.163, f32[153]{0:T(256)S(1)} %pad.48.clone), kind=kOutput, calls=%fused_computation.20 | convolution fusion | flops 482185216 | bytes 3605604 | tf_op jit(solution)/shard_map/jvp(thf,hfd->thd)/dot_general | solution.py:126
  108.8 2.9 multiply_reduce_fusion.4
  111.8 14.9 %fusion.80 = f32[16,1,153]{2,1,0:T(1,128)S(1)} fusion(f32[16,128,1]{1,2,0:T(1,128)S(1)} %bitcast.187, f32[128,16,136]{0,2,1:T(8,128)S(1)} %fusion.83, f32[128,16,16]{0,2,1:T(8,128)S(1)} %bitcast.164, f32[153]{0:T(256)S(1)} %pad.48.clone), kind=kOutput, calls=%fused_computation.133 | convolution fusion | flops 4386816 | bytes 1263780 | tf_op jit(solution)/shard_map/transpose(jvp(thf,hf->th))/dot_general | solution.py:129
  128.1 3.6 %fusion.27 = f32[16,153,128]{2,1,0:T(8,128)S(1)} fusion(f32[128]{0:T(128)} %copy-done.31, f32[128,16,136]{0,2,1:T(8,128)S(1)} %fusion.83, f32[128,16,16]{0,2,1:T(8,128)S(1)} %bitcast.165, f32[153]{0:T(256)} %copy-done.19, f32[128,16,128]{0,2,1:T(8,128)} %bitcast.173, f32[128,16]{0,1:T(8,128)} %copy-done.35), kind=kOutput, calls=%fused_computation.51 | convolution fusion | flops 482447360 | bytes 3556452 | tf_op jit(solution)/shard_map/transpose(jvp(thf,hfd->thd))/dot_general | solution.py:126
  137.1 1.6 fusion.4
  138.7 1.9 fusion.17
  140.6 14.8 %collective-permute-done.6 = f32[8,160,128]{2,1,0:T(8,128)S(1)} collective-permute-done((f32[8,160,128]{2,1,0:T(8,128)S(1)}, f32[8,160,128]{2,1,0:T(8,128)S(1)}, u32[]{:S(2)}, u32[]{:S(2)}) %collective-permute-start.6) | collective-permute-done | bytes 655392 | tf_op jit(solution)/shard_map/ppermute | solution.py:70
  158.3 1.5 fusion.21
  161.0 13.4 %collective-permute-done.7 = f32[8,160,128]{2,1,0:T(8,128)S(1)} collective-permute-done((f32[8,160,128]{2,1,0:T(8,128)S(1)}, f32[8,160,128]{2,1,0:T(8,128)S(1)}, u32[]{:S(2)}, u32[]{:S(2)}) %collective-permute-start.7) | collective-permute-done | bytes 655392 | tf_op jit(solution)/shard_map/ppermute | solution.py:70
  174.6 1.7 convolution_multiply_fusion.1
  177.4 2.3 fusion.31
  180.4 2.3 fusion.5
  182.7 1.9 fusion.15
  185.6 3.8 %fusion.11 = f32[16,128,128]{2,1,0:T(8,128)S(1)} fusion(f32[16,160,128]{2,1,0:T(8,128)S(1)} %maximum_select_fusion.1, f32[128,16,136]{0,2,1:T(8,128)S(1)} %fusion.82, f32[128,16,16]{0,2,1:T(8,128)S(1)} %bitcast.157, f32[153]{0:T(256)S(1)} %copy-done.20, f32[128]{0:T(128)S(1)} %copy-done.26), kind=kOutput, calls=%fused_computation.32 | convolution fusion | flops 482236416 | bytes 3605604 | tf_op jit(solution)/shard_map/transpose(jvp(thf,thd->hfd))/dot_general | solution.py:142
  189.7 22.1 %all_to_all.42 = f32[128,8,320]{0,2,1:T(8,128)} all-to-all(f32[128,8,320]{0,2,1:T(8,128)S(1)} %convert.2), channel_id=1, replica_groups=mesh['dp'=4,'seq'=8] {'seq'}, dimensions={1} | all-to-all | bytes 2621440 | tf_op jit(solution)/shard_map/all_to_all | solution.py:206
  211.8 10.0 %convolution_bitcast_fusion = f32[2048,320]{0,1:T(8,128)} fusion(f32[1024,2048]{1,0:T(8,128)} %all-gather.2.cloned.1.call-done, f32[128,8,320]{0,2,1:T(8,128)} %all_to_all.42), kind=kOutput, calls=%fused_computation | convolution fusion | flops 4026531840 | bytes 12320768 | tf_op jit(solution)/shard_map/dot_general | solution.py:209
  223.8 49.8 %reduce-scatter.2.cloned.1.call-done = f32[512,320]{0,1:T(8,128)} async-done(((f32[2048,320]{0,1:T(8,128)}), f32[512,320]{0,1:T(8,128)}) %reduce-scatter.2.cloned.1.call-update) | async-done | bytes 655376 | tf_op jit(solution)/shard_map/reduce_scatter | solution.py:216
  273.6 2.3 copy.70
  275.8 3.7 %all-to-all-start.1 = ((f32[8,64,320]{2,1,0:T(8,128)}), f32[8,64,320]{2,1,0:T(8,128)S(1)}, u32[]{:S(2)}, u32[]{:S(2)}) async-start(f32[8,64,320]{2,1,0:T(8,128)} %bitcast.171), calls=%async_computation.2 | async-start | bytes 1572864 | tf_op jit(solution)/shard_map/all_to_all | solution.py:217
  279.5 6.3 %fusion.49 = f32[128,2048]{1,0:T(8,128)S(1)} fusion(bf16[2048,2048]{1,0:T(8,128)(2,1)} %param.10, bf16[128,2560]{0,1:T(8,128)(2,1)S(1)} %add_convert_fusion), kind=kOutput, calls=%fused_computation.87 | convolution fusion | flops 1073741824 | bytes 9961472 | tf_op jit(solution)/shard_map/dot_general | solution.py:198
  288.3 3.8 %all-to-all-done.1 = f32[8,64,320]{2,1,0:T(8,128)S(1)} async-done(((f32[8,64,320]{2,1,0:T(8,128)}), f32[8,64,320]{2,1,0:T(8,128)S(1)}, u32[]{:S(2)}, u32[]{:S(2)}) %all-to-all-start.1) | async-done | bytes 655392 | tf_op jit(solution)/shard_map/all_to_all | solution.py:217
  (154 shorter events, 38.1 us)
Async XLA Ops:
  7.2 12.6 %copy-start = (bf16[2048,256]{1,0:T(8,128)(2,1)S(1)}, bf16[2048,256]{1,0:T(8,128)(2,1)}, u32[]{:S(2)}) copy-start(bf16[2048,256]{1,0:T(8,128)(2,1)} %param.8) | copy-start | bytes 3145732
  7.2 204.6 %all-gather.2.cloned.1.call-start = ((), (), s32[]{:S(2)}) async-start(), calls=%async_computation.3 | async-start | bytes 9437184 | tf_op jit(solution)/shard_map/all_gather | solution.py:174
  9.2 5.5 %copy-start.1 = (bf16[1,128,2048]{2,1,0:T(8,128)(2,1)S(1)}, bf16[1,128,2048]{2,1,0:T(8,128)(2,1)}, u32[]{:S(2)}) copy-start(bf16[1,128,2048]{2,1,0:T(8,128)(2,1)} %param.7) | copy-start | bytes 1572868
  9.2 14.3 %collective-permute-start = (s32[1]{0:T(128)}, s32[1]{0:T(128)}, u32[]{:S(2)}, u32[]{:S(2)}) collective-permute-start(s32[1]{0:T(128)} %bitcast.4), channel_id=1, source_target_pairs={{0,1},{1,2},{2,3},{3,4},{4,5},{5,6},{6,7},{8,9},{9,10},{10,11},{11... | collective-permute-start | bytes 20 | tf_op jit(solution)/shard_map/ppermute | solution.py:37
  14.7 4.8 %copy-start.7 = (bf16[2048,256]{1,0:T(8,128)(2,1)S(1)}, bf16[2048,256]{1,0:T(8,128)(2,1)}, u32[]{:S(2)}) copy-start(bf16[2048,256]{1,0:T(8,128)(2,1)} %param.9) | copy-start | bytes 3145732
  14.7 258.9 %reduce-scatter.2.cloned.1.call-start = ((), (), s32[]{:S(2)}) async-start(), calls=%async_computation.4 | async-start | bytes 3276800 | tf_op jit(solution)/shard_map/reduce_scatter | solution.py:216
  21.4 90.3 %copy-start.19 = (f32[153]{0:T(256)}, f32[153]{0:T(256)S(1)}, u32[]{:S(2)}) copy-start(f32[153]{0:T(256)S(1)} %pad.48.clone) | copy-start | bytes 1840
  21.5 7.7 %copy-start.27 = (f32[160]{0:T(256)}, f32[160]{0:T(256)S(1)}, u32[]{:S(2)}) copy-start(f32[160]{0:T(256)S(1)} %pad.47.clone) | copy-start | bytes 1924
  25.6 3.7 %copy-start.25 = (f32[128]{0:T(128)}, f32[128]{0:T(128)S(1)}, u32[]{:S(2)}) copy-start(f32[128]{0:T(128)S(1)} %get-tuple-element.33) | copy-start | bytes 1540
  25.6 86.2 %copy-start.31 = (f32[128]{0:T(128)}, f32[128]{0:T(128)S(1)}, u32[]{:S(2)}) copy-start(f32[128]{0:T(128)S(1)} %get-tuple-element.32) | copy-start | bytes 1540
  30.5 4.5 %collective-permute-start.1 = (f32[8,160,128]{2,1,0:T(8,128)}, f32[8,160,128]{2,1,0:T(8,128)}, u32[]{:S(2)}, u32[]{:S(2)}) collective-permute-start(f32[8,160,128]{2,1,0:T(8,128)} %get-tuple-element.26), channel_id=1, source_target_pairs={{0,1},{1,0},{2,3},{3,2},{4,5},{5,4},{6,7},{7,6},{8,9},{9,8},{10,11... | collective-permute-start | bytes 1966088 | tf_op jit(solution)/shard_map/ppermute | solution.py:74
  38.1 29.3 %collective-permute-start.2 = (f32[8,160,128]{2,1,0:T(8,128)S(1)}, f32[8,160,128]{2,1,0:T(8,128)}, u32[]{:S(2)}, u32[]{:S(2)}) collective-permute-start(f32[8,160,128]{2,1,0:T(8,128)S(1)} %fusion.47), channel_id=1, source_target_pairs={{0,2},{1,3},{2,4},{3,5},{4,6},{5,7},{8,10},{9,11},{10,12},{11,13},... | collective-permute-start | bytes 1966088 | tf_op jit(solution)/shard_map/ppermute | solution.py:70
  67.4 25.2 %collective-permute-start.3 = (f32[8,160,128]{2,1,0:T(8,128)}, f32[8,160,128]{2,1,0:T(8,128)}, u32[]{:S(2)}, u32[]{:S(2)}) collective-permute-start(f32[8,160,128]{2,1,0:T(8,128)} %collective-permute-done.2), channel_id=1, source_target_pairs={{0,2},{1,3},{2,4},{3,5},{4,6},{5,7},{8,10},{9,11},{10,12},{11,13},... | collective-permute-start | bytes 1966088 | tf_op jit(solution)/shard_map/ppermute | solution.py:70
  73.2 22.2 %copy-start.22 = (pred[128,128]{0,1:T(8,128)(4,1)}, pred[128,128]{0,1:T(8,128)(4,1)S(1)}, u32[]{:S(2)}) copy-start(pred[128,128]{0,1:T(8,128)(4,1)S(1)} %fusion.70) | copy-start | bytes 49156
  95.4 6.3 %collective-permute-start.4 = (f32[8,160,128]{2,1,0:T(8,128)}, f32[8,160,128]{2,1,0:T(8,128)}, u32[]{:S(2)}, u32[]{:S(2)}) collective-permute-start(f32[8,160,128]{2,1,0:T(8,128)} %get-tuple-element.25), channel_id=1, source_target_pairs={{0,1},{1,0},{2,3},{3,2},{4,5},{5,4},{6,7},{7,6},{8,9},{9,8},{10,11... | collective-permute-start | bytes 1966088 | tf_op jit(solution)/shard_map/ppermute | solution.py:82
  103.1 5.7 %copy-start.5 = (f32[16,160,128]{2,1,0:T(8,128)}, f32[16,160,128]{2,1,0:T(8,128)S(1)}, u32[]{:S(2)}) copy-start(f32[16,160,128]{2,1,0:T(8,128)S(1)} %maximum_select_fusion) | copy-start | bytes 3932164
  111.7 15.0 %copy-start.17 = (f32[128,16]{0,1:T(8,128)}, f32[128,16]{0,1:T(8,128)S(1)}, u32[]{:S(2)}) copy-start(f32[128,16]{0,1:T(8,128)S(1)} %get-tuple-element.28) | copy-start | bytes 24580
  111.8 15.0 %copy-start.33 = (f32[16,128]{1,0:T(8,128)}, f32[16,128]{1,0:T(8,128)S(1)}, u32[]{:S(2)}) copy-start(f32[16,128]{1,0:T(8,128)S(1)} %broadcast_multiply_fusion.2) | copy-start | bytes 24580
  128.1 3.7 %copy-start.28 = (f32[160]{0:T(256)S(1)}, f32[160]{0:T(256)}, u32[]{:S(2)}) copy-start(f32[160]{0:T(256)} %copy-done.27) | copy-start | bytes 1924
  128.1 3.7 %copy-start.30 = (f32[160]{0:T(256)S(1)}, f32[160]{0:T(256)}, u32[]{:S(2)}) copy-start(f32[160]{0:T(256)} %copy-done.29) | copy-start | bytes 1924
  132.0 5.0 %copy-start.14 = (f32[1,128,2048]{1,2,0:T(8,128)S(1)}, f32[1,128,2048]{1,2,0:T(8,128)}, u32[]{:S(2)}) copy-start(f32[1,128,2048]{1,2,0:T(8,128)} %copy.59) | copy-start | bytes 3145732
  132.1 4.9 %copy-start.6 = (f32[16,160,128]{2,1,0:T(8,128)S(1)}, f32[16,160,128]{2,1,0:T(8,128)}, u32[]{:S(2)}) copy-start(f32[16,160,128]{2,1,0:T(8,128)} %copy-done.5) | copy-start | bytes 3932164
  132.1 4.9 %copy-start.21 = (f32[16,153]{1,0:T(8,128)S(1)}, f32[16,153]{1,0:T(8,128)}, u32[]{:S(2)}) copy-start(f32[16,153]{1,0:T(8,128)} %get-tuple-element.30) | copy-start | bytes 29380
  132.1 4.9 %copy-start.32 = (f32[128]{0:T(128)S(1)}, f32[128]{0:T(128)}, u32[]{:S(2)}) copy-start(f32[128]{0:T(128)} %copy-done.31) | copy-start | bytes 1540
  132.2 4.9 %copy-start.34 = (f32[16,128]{1,0:T(8,128)S(1)}, f32[16,128]{1,0:T(8,128)}, u32[]{:S(2)}) copy-start(f32[16,128]{1,0:T(8,128)} %copy-done.33) | copy-start | bytes 24580
  132.2 4.9 %copy-start.36 = (f32[128,16]{0,1:T(8,128)S(1)}, f32[128,16]{0,1:T(8,128)}, u32[]{:S(2)}) copy-start(f32[128,16]{0,1:T(8,128)} %copy-done.35) | copy-start | bytes 24580
  132.2 2.3 collective-permute-start.5
  135.7 19.7 %collective-permute-start.6 = (f32[8,160,128]{2,1,0:T(8,128)S(1)}, f32[8,160,128]{2,1,0:T(8,128)S(1)}, u32[]{:S(2)}, u32[]{:S(2)}) collective-permute-start(f32[8,160,128]{2,1,0:T(8,128)S(1)} %fusion.48), channel_id=1, source_target_pairs={{2,0},{3,1},{4,2},{5,3},{6,4},{7,5},{10,8},{11,9},{12,10},{13,11},... | collective-permute-start | bytes 1966088 | tf_op jit(solution)/shard_map/ppermute | solution.py:70
  138.7 18.0 %copy-start.18 = (f32[128,16]{0,1:T(8,128)S(1)}, f32[128,16]{0,1:T(8,128)}, u32[]{:S(2)}) copy-start(f32[128,16]{0,1:T(8,128)} %copy-done.17) | copy-start | bytes 24580
  155.4 19.0 %collective-permute-start.7 = (f32[8,160,128]{2,1,0:T(8,128)S(1)}, f32[8,160,128]{2,1,0:T(8,128)S(1)}, u32[]{:S(2)}, u32[]{:S(2)}) collective-permute-start(f32[8,160,128]{2,1,0:T(8,128)S(1)} %collective-permute-done.6), channel_id=1, source_target_pairs={{2,0},{3,1},{4,2},{5,3},{6,4},{7,5},{10,8},{11,9},{12,10},{13,11},... | collective-permute-start | bytes 1966088 | tf_op jit(solution)/shard_map/ppermute | solution.py:70
  174.6 5.2 %collective-permute-start.8 = (f32[8,160,128]{2,1,0:T(8,128)S(1)}, f32[8,160,128]{2,1,0:T(8,128)S(1)}, u32[]{:S(2)}, u32[]{:S(2)}) collective-permute-start(f32[8,160,128]{2,1,0:T(8,128)S(1)} %get-tuple-element.19), channel_id=1, source_target_pairs={{0,1},{1,0},{2,3},{3,2},{4,5},{5,4},{6,7},{7,6},{8,9},{9,8},{10,11... | collective-permute-start | bytes 1966088 | tf_op jit(solution)/shard_map/ppermute | solution.py:82
  275.8 16.3 %all-to-all-start.1 = ((f32[8,64,320]{2,1,0:T(8,128)}), f32[8,64,320]{2,1,0:T(8,128)S(1)}, u32[]{:S(2)}, u32[]{:S(2)}) async-start(f32[8,64,320]{2,1,0:T(8,128)} %bitcast.171), calls=%async_computation.2 | async-start | bytes 1572864 | tf_op jit(solution)/shard_map/all_to_all | solution.py:217
  (20 other events, 40.6 us)
Sparse Core Ops, SparseCore 0:
  14.8 73.5 all-gather.1
  221.9 51.6 reduce-scatter.1
